TPU v7x, 256 devices: a whole 4x4x8 slice. The times are simulated.
256 devices in a mesh: row: 16 (over y, x), col: 16 (over z, core).
Axes of the slice: x: 4, y: 4, z: 8, core: 2. Of those that a mesh axis runs over, the one named last changes fastest.
Arguments:
- features: float32 [65536, 512], P(('col', 'row')), may hold values from -6 to 6
- weight: float32 [512, 512], replicated, may hold values from -0.25 to 0.25
- tile_values: bfloat16 [16, 16, 32, 256, 256], P('row', 'col'), as said below
- tile_ids: int32 [16, 16, 32, 2], P('row', 'col'), may hold values from 0 to 15, as said below
- tile_counts: int32 [16, 16], P('row', 'col'), may hold values from 1 to 32, as said below
Outputs:
- activated: float32 [65536, 512], P(('row', 'col'))
Inputs may be any that keep to these rules, and one draw needn't show every extreme that they name: `tile_counts`: slots at or beyond a panel's count are ignored; some panel holds 32 live slots. `tile_ids`: the first entry is below 16, the second below 16; a tile may repeat. `tile_values`: nonnegative.
All inputs are finite; a program needn't handle non-finite values.
Results may differ from a plain program's by a relative error of at most 0.0003.
Values may be sent and summed in bfloat16 or wider, within the bound.
No kernel may reach another device: no remote copies, remote signals or barrier semaphores. Data moves between devices by JAX's collectives and lax.ppermute only.
A program may use at most 128 MiB of HBM per device.

v0:
```python
import jax
import jax.numpy as jnp
from jax import lax
from jax.sharding import PartitionSpec as P


def shards(features, weight, tile_values, tile_ids, tile_counts):
    tile_set = tile_values[0, 0]
    tile_slots = tile_ids[0, 0]
    live_count = tile_counts[0, 0]
    tile_size = tile_set.shape[1]
    slot_total = tile_set.shape[0]
    grid_row = lax.axis_index("row")
    column_in_grid = lax.axis_index("col")
    own_rows = features.shape[0]
    panel_cols = own_rows * lax.axis_size("row")
    panel_rows = own_rows * lax.axis_size("col")
    row_blocks = panel_rows // tile_size
    width = features.shape[1]

    def unchanged(state):
        return state

    is_live = (jnp.arange(slot_total) < live_count).astype(jnp.float32)
    tile_sums = jnp.sum(tile_set, axis=2, dtype=jnp.float32)
    placement = (tile_slots[:, 0][:, None] == jnp.arange(row_blocks)[None, :]).astype(
        jnp.float32
    ) * is_live[:, None]
    row_sums = jnp.dot(placement.T, tile_sums, precision=lax.Precision.HIGHEST).reshape(panel_rows)
    weighted = jnp.dot(features, weight, precision=lax.Precision.HIGHEST)
    empty = jnp.zeros((panel_rows, width), jnp.float32)
    partial_value = empty
    shard_rows = lax.all_gather(weighted, "row", axis=0, tiled=True)
    length = shard_rows.shape[0]

    def one_tile(slot_index, current):
        row_blk = tile_slots[slot_index, 0]
        col_offset = tile_slots[slot_index, 1] * tile_size
        inside = (slot_index < live_count) & (col_offset >= 0) & (col_offset + tile_size <= length)

        def add_tile(state):
            columns = lax.dynamic_slice_in_dim(shard_rows, col_offset, tile_size, 0)
            product = jnp.dot(
                tile_set[slot_index].astype(jnp.float32), columns, precision=lax.Precision.HIGHEST
            )
            old_rows = lax.dynamic_slice_in_dim(state, row_blk * tile_size, tile_size, 0)
            return lax.dynamic_update_slice_in_dim(
                state, old_rows + product, row_blk * tile_size, 0
            )

        return lax.cond(inside, add_tile, unchanged, current)

    partial_value = lax.fori_loop(0, slot_total, one_tile, partial_value)

    def one_self(block_index, current):
        global_blk = column_in_grid * panel_cols // tile_size + block_index
        row_blk = global_blk - grid_row * row_blocks
        inside = (row_blk >= 0) & (row_blk < row_blocks)

        def add_self(state):
            own_block = lax.dynamic_slice_in_dim(shard_rows, block_index * tile_size, tile_size, 0)
            old_rows = lax.dynamic_slice_in_dim(state, row_blk * tile_size, tile_size, 0)
            return lax.dynamic_update_slice_in_dim(
                state, old_rows + own_block, row_blk * tile_size, 0
            )

        return lax.cond(inside, add_self, unchanged, current)

    folded = lax.fori_loop(0, length // tile_size, one_self, partial_value)
    partial_value = folded
    own_share, degree_part = (
        lax.psum_scatter(partial_value, "col", scatter_dimension=0, tiled=True),
        lax.psum_scatter(row_sums, "col", scatter_dimension=0, tiled=True),
    )
    inverse_root = lax.rsqrt(1.0 + degree_part)
    return jnp.maximum(own_share * inverse_root[:, None], 0.0)


def solution(mesh):
    in_specs = (
        P(("col", "row"), None),
        P(),
        P("row", "col", None, None, None),
        P("row", "col", None, None),
        P("row", "col"),
    )
    out_specs = P(("row", "col"), None)
    return jax.shard_map(shards, mesh=mesh, in_specs=in_specs, out_specs=out_specs, check_vma=False)
```

profile of v0, /device:TPU:2, one launch (start us, length us, event | category | flops | bytes accessed | tf_op | source)
XLA Modules:
  0.0 476.0 jit_solution(18017960913110933433)
XLA Ops:
  7.8 2.9 fusion.13
  10.7 78.8 %all-gather.2.cloned.1.call-done = f32[4096,512]{1,0:T(8,128)} async-done(((f32[256,512]{1,0:T(8,128)}), f32[4096,512]{1,0:T(8,128)}) %all-gather.2.cloned.1.call-update) | async-done | bytes 8388624 | tf_op jit(solution)/shard_map/all_gather | solution.py:33
  89.5 4.3 broadcast_in_dim.2
  93.8 180.5 %while.35 = (s32[]{:T(128)}, f32[4096,512]{1,0:T(8,128)}, s32[]{:T(128)}, s32[32,2]{0,1:T(2,128)S(1)}, bf16[32,256,256]{2,1,0:T(8,128)(2,1)}, /*index=5*/f32[409...) while((s32[]{:T(128)}, f32[4096,512]{1,0:T(8,128)}, s32[]{:T(128)}, s32[32,2]{0,1:T(2,128)S(1)}, ...), condition=%wide.region_3.4_spmd, body=%wide.region_0.3_spmd.sunk | while | flops 402784256 | bytes 1704281 | solution.py:53
  96.4 7.1 %conditional.4 = (f32[4096,512]{1,0:T(8,128)}) conditional(s32[]{:T(128)} %convert_element_type.35, f32[4096,512]{1,0:T(8,128)} %get-tuple-element.475, (s32[32,2]{0,1:T(2,128)S(1)}, s32[]{:T(128)}, f32[4096,512]{1,0:T(8,128)}, bf16[32,256,256]{2,1,0:T(8,128)(2,1)}, s32[]{:T(128)}, /*index=5*/f32[4096,512]{1,0:T(8,128)}) %tuple.85), branch_computations={%region_1.1_spmd, %region_2.0_spmd} | conditional | flops 402784256 | bytes 1704070 | solution.py:51
  106.0 7.1 %conditional.4 = (f32[4096,512]{1,0:T(8,128)}) conditional(s32[]{:T(128)} %convert_element_type.35, f32[4096,512]{1,0:T(8,128)} %get-tuple-element.475, (s32[32,2]{0,1:T(2,128)S(1)}, s32[]{:T(128)}, f32[4096,512]{1,0:T(8,128)}, bf16[32,256,256]{2,1,0:T(8,128)(2,1)}, s32[]{:T(128)}, /*index=5*/f32[4096,512]{1,0:T(8,128)}) %tuple.85), branch_computations={%region_1.1_spmd, %region_2.0_spmd} | conditional | flops 402784256 | bytes 1704070 | solution.py:51
  115.6 7.0 %conditional.4 = (f32[4096,512]{1,0:T(8,128)}) conditional(s32[]{:T(128)} %convert_element_type.35, f32[4096,512]{1,0:T(8,128)} %get-tuple-element.475, (s32[32,2]{0,1:T(2,128)S(1)}, s32[]{:T(128)}, f32[4096,512]{1,0:T(8,128)}, bf16[32,256,256]{2,1,0:T(8,128)(2,1)}, s32[]{:T(128)}, /*index=5*/f32[4096,512]{1,0:T(8,128)}) %tuple.85), branch_computations={%region_1.1_spmd, %region_2.0_spmd} | conditional | flops 402784256 | bytes 1704070 | solution.py:51
  125.1 7.1 %conditional.4 = (f32[4096,512]{1,0:T(8,128)}) conditional(s32[]{:T(128)} %convert_element_type.35, f32[4096,512]{1,0:T(8,128)} %get-tuple-element.475, (s32[32,2]{0,1:T(2,128)S(1)}, s32[]{:T(128)}, f32[4096,512]{1,0:T(8,128)}, bf16[32,256,256]{2,1,0:T(8,128)(2,1)}, s32[]{:T(128)}, /*index=5*/f32[4096,512]{1,0:T(8,128)}) %tuple.85), branch_computations={%region_1.1_spmd, %region_2.0_spmd} | conditional | flops 402784256 | bytes 1704070 | solution.py:51
  129.6 2.6 fusion
  134.7 7.0 %conditional.4 = (f32[4096,512]{1,0:T(8,128)}) conditional(s32[]{:T(128)} %convert_element_type.35, f32[4096,512]{1,0:T(8,128)} %get-tuple-element.475, (s32[32,2]{0,1:T(2,128)S(1)}, s32[]{:T(128)}, f32[4096,512]{1,0:T(8,128)}, bf16[32,256,256]{2,1,0:T(8,128)(2,1)}, s32[]{:T(128)}, /*index=5*/f32[4096,512]{1,0:T(8,128)}) %tuple.85), branch_computations={%region_1.1_spmd, %region_2.0_spmd} | conditional | flops 402784256 | bytes 1704070 | solution.py:51
  144.3 7.1 %conditional.4 = (f32[4096,512]{1,0:T(8,128)}) conditional(s32[]{:T(128)} %convert_element_type.35, f32[4096,512]{1,0:T(8,128)} %get-tuple-element.475, (s32[32,2]{0,1:T(2,128)S(1)}, s32[]{:T(128)}, f32[4096,512]{1,0:T(8,128)}, bf16[32,256,256]{2,1,0:T(8,128)(2,1)}, s32[]{:T(128)}, /*index=5*/f32[4096,512]{1,0:T(8,128)}) %tuple.85), branch_computations={%region_1.1_spmd, %region_2.0_spmd} | conditional | flops 402784256 | bytes 1704070 | solution.py:51
  153.9 7.0 %conditional.4 = (f32[4096,512]{1,0:T(8,128)}) conditional(s32[]{:T(128)} %convert_element_type.35, f32[4096,512]{1,0:T(8,128)} %get-tuple-element.475, (s32[32,2]{0,1:T(2,128)S(1)}, s32[]{:T(128)}, f32[4096,512]{1,0:T(8,128)}, bf16[32,256,256]{2,1,0:T(8,128)(2,1)}, s32[]{:T(128)}, /*index=5*/f32[4096,512]{1,0:T(8,128)}) %tuple.85), branch_computations={%region_1.1_spmd, %region_2.0_spmd} | conditional | flops 402784256 | bytes 1704070 | solution.py:51
  163.5 7.1 %conditional.4 = (f32[4096,512]{1,0:T(8,128)}) conditional(s32[]{:T(128)} %convert_element_type.35, f32[4096,512]{1,0:T(8,128)} %get-tuple-element.475, (s32[32,2]{0,1:T(2,128)S(1)}, s32[]{:T(128)}, f32[4096,512]{1,0:T(8,128)}, bf16[32,256,256]{2,1,0:T(8,128)(2,1)}, s32[]{:T(128)}, /*index=5*/f32[4096,512]{1,0:T(8,128)}) %tuple.85), branch_computations={%region_1.1_spmd, %region_2.0_spmd} | conditional | flops 402784256 | bytes 1704070 | solution.py:51
  168.0 2.6 fusion
  173.1 7.0 %conditional.4 = (f32[4096,512]{1,0:T(8,128)}) conditional(s32[]{:T(128)} %convert_element_type.35, f32[4096,512]{1,0:T(8,128)} %get-tuple-element.475, (s32[32,2]{0,1:T(2,128)S(1)}, s32[]{:T(128)}, f32[4096,512]{1,0:T(8,128)}, bf16[32,256,256]{2,1,0:T(8,128)(2,1)}, s32[]{:T(128)}, /*index=5*/f32[4096,512]{1,0:T(8,128)}) %tuple.85), branch_computations={%region_1.1_spmd, %region_2.0_spmd} | conditional | flops 402784256 | bytes 1704070 | solution.py:51
  182.7 7.0 %conditional.4 = (f32[4096,512]{1,0:T(8,128)}) conditional(s32[]{:T(128)} %convert_element_type.35, f32[4096,512]{1,0:T(8,128)} %get-tuple-element.475, (s32[32,2]{0,1:T(2,128)S(1)}, s32[]{:T(128)}, f32[4096,512]{1,0:T(8,128)}, bf16[32,256,256]{2,1,0:T(8,128)(2,1)}, s32[]{:T(128)}, /*index=5*/f32[4096,512]{1,0:T(8,128)}) %tuple.85), branch_computations={%region_1.1_spmd, %region_2.0_spmd} | conditional | flops 402784256 | bytes 1704070 | solution.py:51
  192.2 7.1 %conditional.4 = (f32[4096,512]{1,0:T(8,128)}) conditional(s32[]{:T(128)} %convert_element_type.35, f32[4096,512]{1,0:T(8,128)} %get-tuple-element.475, (s32[32,2]{0,1:T(2,128)S(1)}, s32[]{:T(128)}, f32[4096,512]{1,0:T(8,128)}, bf16[32,256,256]{2,1,0:T(8,128)(2,1)}, s32[]{:T(128)}, /*index=5*/f32[4096,512]{1,0:T(8,128)}) %tuple.85), branch_computations={%region_1.1_spmd, %region_2.0_spmd} | conditional | flops 402784256 | bytes 1704070 | solution.py:51
  201.8 7.1 %conditional.4 = (f32[4096,512]{1,0:T(8,128)}) conditional(s32[]{:T(128)} %convert_element_type.35, f32[4096,512]{1,0:T(8,128)} %get-tuple-element.475, (s32[32,2]{0,1:T(2,128)S(1)}, s32[]{:T(128)}, f32[4096,512]{1,0:T(8,128)}, bf16[32,256,256]{2,1,0:T(8,128)(2,1)}, s32[]{:T(128)}, /*index=5*/f32[4096,512]{1,0:T(8,128)}) %tuple.85), branch_computations={%region_1.1_spmd, %region_2.0_spmd} | conditional | flops 402784256 | bytes 1704070 | solution.py:51
  206.3 2.6 fusion
  211.4 7.0 %conditional.4 = (f32[4096,512]{1,0:T(8,128)}) conditional(s32[]{:T(128)} %convert_element_type.35, f32[4096,512]{1,0:T(8,128)} %get-tuple-element.475, (s32[32,2]{0,1:T(2,128)S(1)}, s32[]{:T(128)}, f32[4096,512]{1,0:T(8,128)}, bf16[32,256,256]{2,1,0:T(8,128)(2,1)}, s32[]{:T(128)}, /*index=5*/f32[4096,512]{1,0:T(8,128)}) %tuple.85), branch_computations={%region_1.1_spmd, %region_2.0_spmd} | conditional | flops 402784256 | bytes 1704070 | solution.py:51
  221.0 7.0 %conditional.4 = (f32[4096,512]{1,0:T(8,128)}) conditional(s32[]{:T(128)} %convert_element_type.35, f32[4096,512]{1,0:T(8,128)} %get-tuple-element.475, (s32[32,2]{0,1:T(2,128)S(1)}, s32[]{:T(128)}, f32[4096,512]{1,0:T(8,128)}, bf16[32,256,256]{2,1,0:T(8,128)(2,1)}, s32[]{:T(128)}, /*index=5*/f32[4096,512]{1,0:T(8,128)}) %tuple.85), branch_computations={%region_1.1_spmd, %region_2.0_spmd} | conditional | flops 402784256 | bytes 1704070 | solution.py:51
  275.8 3.3 convert_reduce_fusion
  280.7 134.2 %all-reduce = f32[4096]{0:T(1024)S(1)} all-reduce(f32[4096]{0:T(1024)S(1)} %bitcast.23), channel_id=3, replica_groups=mesh['row'=16,'col'=16] {'col'}, use_global_device_ids=true, to_apply=%region_10.11.clone | all-reduce | flops 4096 | bytes 32768
  415.0 52.2 %reduce-scatter.2.cloned.1.call-done = f32[256,512]{1,0:T(8,128)} async-done(((f32[4096,512]{1,0:T(8,128)}), f32[256,512]{1,0:T(8,128)}) %reduce-scatter.2.cloned.1.call-update) | async-done | bytes 524304 | tf_op jit(solution)/shard_map/reduce_scatter | solution.py:72
  (109 shorter events, 60.8 us)
Async XLA Ops:
  6.5 1.2 copy-start
  6.5 87.3 %copy-start.1 = (s32[1,1,32,2]{2,3,1,0:T(2,128)S(1)}, s32[1,1,32,2]{2,3,1,0:T(2,128)}, u32[]{:S(2)}) copy-start(s32[1,1,32,2]{2,3,1,0:T(2,128)} %param.16) | copy-start | bytes 772
  6.5 83.0 %all-gather.2.cloned.1.call-start = ((), (), s32[]{:S(2)}) async-start(), calls=%async_computation.1 | async-start | bytes 8912896 | tf_op jit(solution)/shard_map/all_gather | solution.py:33
  10.7 456.6 %reduce-scatter.2.cloned.1.call-start = ((), (), s32[]{:S(2)}) async-start(), calls=%async_computation.2 | async-start | bytes 8912896 | tf_op jit(solution)/shard_map/reduce_scatter | solution.py:72
  275.1 4.4 copy-start.2
Sparse Core Ops, SparseCore 0:
  10.8 78.6 all-gather.1
  275.3 191.8 reduce-scatter.1
where the time goes:
time: 480 us; the launch traced here: 476 us
  blocking collectives  134 us (28%)
  waiting for transfers between devices  131 us (27%)
  loops' own time  118 us (25%)
  matrix products  39.1 us (8%)
  other arithmetic  32.6 us (7%)
  between operations  14.8 us (3%)
  local copies, waits for them, and re-layouts  6.14 us (1%)
    unnamed x1, blocking collectives  134 us
    all_gather x1, waiting for transfers between devices, shards(): shard_rows = lax.all_gather(weighted, 'row', axis=0, tiled=True)  78.8 us
    another operation x1, loops' own time, shards(): partial_value = lax.fori_loop(0, slot_total, one_tile, partial_value)  62.9 us
    another operation x32, loops' own time, one_tile(): return lax.cond(inside, add_tile, unchanged, current)  54.4 us
    reduce_scatter x1, waiting for transfers between devices, shards(): lax.psum_scatter(partial_value, 'col', scatter_dimension=0, tiled=True)  52.2 us
    dot_general x14, matrix products, add_tile(): jnp.dot(tile_set[slot_index].astype(jnp.float32), columns, precision=lax....  36 us
    mul x32, other arithmetic, one_tile(): col_offset = tile_slots[slot_index, 1] * tile_size  18.7 us
  transfers between devices with their start and end apart: 2, of which 2 were waited for; matrix products, arithmetic and copies ran while one was open for 1% of the time, Pallas kernels for 0%

commit v1 on v0

v1 whole, which is shorter than its diff:
```python
import jax
import jax.numpy as jnp
from jax import lax
from jax.experimental import pallas as pl
from jax.experimental.pallas import tpu as pltpu
from jax.sharding import PartitionSpec as P

EXTRA = 8


def _split3(x):
    hi = x.astype(jnp.bfloat16)
    r1 = x - hi.astype(jnp.float32)
    mid = r1.astype(jnp.bfloat16)
    lo = (r1 - mid.astype(jnp.float32)).astype(jnp.bfloat16)
    return hi, mid, lo


def _tile_kernel(ids_ref, cnt_ref, flag_ref, tile_ref, x_ref, out_ref):
    s = pl.program_id(0)
    edge = tile_ref.shape[1]
    blocks = out_ref.shape[0]

    @pl.when(s == 0)
    def _init():
        own = x_ref[...].reshape(blocks, edge, x_ref.shape[1])
        keep = flag_ref[0] != 0
        out_ref[:, :edge, :] = jnp.where(keep, own, jnp.zeros_like(own))
        out_ref[:, edge:, :] = jnp.zeros((blocks, EXTRA, out_ref.shape[2]), jnp.float32)

    @pl.when(s < cnt_ref[0])
    def _add():
        i = ids_ref[2 * s]
        j = ids_ref[2 * s + 1]
        tile = tile_ref[0]
        start = pl.multiple_of(j * edge, edge)
        xb = x_ref[pl.ds(start, edge), :]
        hi, mid, lo = _split3(xb)
        prod = jnp.dot(tile, hi, preferred_element_type=jnp.float32)
        prod += jnp.dot(tile, mid, preferred_element_type=jnp.float32)
        prod += jnp.dot(tile, lo, preferred_element_type=jnp.float32)
        out_ref[i, :edge, :] += prod
        first = (lax.broadcasted_iota(jnp.int32, (EXTRA, edge), 0) == 0).astype(jnp.bfloat16)
        sums = lax.dot_general(
            first, tile, (((1,), (1,)), ((), ())), preferred_element_type=jnp.float32
        )
        out_ref[i, edge:, :edge] += sums


def _panel_products(ids, cnt, flag, tile_set, panel):
    slots, edge, _ = tile_set.shape
    rows, width = panel.shape
    blocks = rows // edge
    grid_spec = pltpu.PrefetchScalarGridSpec(
        num_scalar_prefetch=3,
        grid=(slots,),
        in_specs=[
            pl.BlockSpec((1, edge, edge), lambda s, ids, cnt, flag: (jnp.minimum(s, cnt[0] - 1), 0, 0)),
            pl.BlockSpec((rows, width), lambda s, ids, cnt, flag: (0, 0)),
        ],
        out_specs=pl.BlockSpec((blocks, edge + EXTRA, width), lambda s, ids, cnt, flag: (0, 0, 0)),
    )
    flops = slots * edge * edge * width * 2 * 3
    return pl.pallas_call(
        _tile_kernel,
        grid_spec=grid_spec,
        out_shape=jax.ShapeDtypeStruct((blocks, edge + EXTRA, width), jnp.float32),
        compiler_params=pltpu.CompilerParams(
            dimension_semantics=("arbitrary",), vmem_limit_bytes=56 * 1024 * 1024
        ),
        cost_estimate=pl.CostEstimate(
            flops=flops,
            bytes_accessed=tile_set.size * 2 + panel.size * 4 + blocks * (edge + EXTRA) * width * 4,
            transcendentals=0,
        ),
    )(ids, cnt, flag, tile_set, panel)


def shards(features, weight, tile_values, tile_ids, tile_counts):
    tile_set = tile_values[0, 0]
    edge = tile_set.shape[1]
    ids = tile_ids[0, 0].reshape(-1)
    cnt = tile_counts[0, 0].reshape(1)
    flag = (lax.axis_index("row") == lax.axis_index("col")).astype(jnp.int32).reshape(1)
    weighted = jnp.dot(features, weight, precision=lax.Precision.HIGHEST)
    panel = lax.all_gather(weighted, "row", axis=0, tiled=True)
    partial = _panel_products(ids, cnt, flag, tile_set, panel)
    blocks, height, width = partial.shape
    mine = lax.psum_scatter(
        partial.reshape(blocks * height, width), "col", scatter_dimension=0, tiled=True
    )
    degree = 1.0 + mine[edge, :edge]
    inverse_root = lax.rsqrt(degree)
    return jnp.maximum(mine[:edge] * inverse_root[:, None], 0.0)


def solution(mesh):
    in_specs = (
        P(("col", "row"), None),
        P(),
        P("row", "col", None, None, None),
        P("row", "col", None, None),
        P("row", "col"),
    )
    out_specs = P(("row", "col"), None)
    return jax.shard_map(shards, mesh=mesh, in_specs=in_specs, out_specs=out_specs, check_vma=False)
```

time: 480 us -> 198 us (0.41)
  blocking collectives: 134 us -> 0 us
  loops' own time: 118 us -> 0 us
  matrix products: 39.1 us -> 2.88 us
  other arithmetic: 32.6 us -> 2.64 us
  waiting for transfers between devices: 131 us -> 160 us
  Pallas kernels: 0 us -> 15.9 us
    unnamed x1 -> x0, blocking collectives: 134 us -> none
    another operation x50 -> x0, loops' own time: 118 us -> none  [the longest x1 62.9 us: shards(): partial_value = lax.fori_loop(0, slot_total, one_tile, partial_value)]
    dot_general x15 -> x0, matrix products: 36.3 us -> none  [the longest x14 36 us: add_tile(): jnp.dot(tile_set[slot_index].astype(jnp.float32), columns, precision=lax....]
    reduce_scatter x1, waiting for transfers between devices: 52.2 us -> 83 us  [shards(): lax.psum_scatter(partial.reshape(blocks * height, width), 'col', scatter_...]
    mul x46 -> x0, other arithmetic: 27.3 us -> none  [the longest x32 18.7 us: one_tile(): col_offset = tile_slots[slot_index, 1] * tile_size]
    pallas_call x0 -> x1, Pallas kernels: none -> 15.9 us  [_panel_products(): pl.pallas_call(_tile_kernel, grid_spec=grid_spec, out_shape=jax.ShapeDtyp...]
where the time goes in v1:
time: 198 us
  waiting for transfers between devices  160 us (81%)
  Pallas kernels  15.9 us (8%)
  between operations  14.1 us (7%)
  matrix products  2.88 us (1%)
  local copies, waits for them, and re-layouts  2.68 us (1%)
  other arithmetic  2.64 us (1%)
    reduce_scatter x1, waiting for transfers between devices, shards(): lax.psum_scatter(partial.reshape(blocks * height, width), 'col', scatter_...  83 us
    all_gather x1, waiting for transfers between devices, shards(): panel = lax.all_gather(weighted, 'row', axis=0, tiled=True)  76.7 us
    pallas_call x1, Pallas kernels, _panel_products(): pl.pallas_call(_tile_kernel, grid_spec=grid_spec, out_shape=jax.ShapeDtyp...  15.9 us
  transfers between devices with their start and end apart: 2, of which 2 were waited for; matrix products, arithmetic and copies ran while one was open for 1% of the time, Pallas kernels for 0%

profile of v1, /device:TPU:2, one launch (start us, length us, event | category | flops | bytes accessed | tf_op | source)
XLA Modules:
  0.0 197.9 jit_solution(7205910192631670515)
XLA Ops:
  6.5 0.0 copy-start
  6.5 0.0 all-gather.2.cloned.1.call-start
  6.5 1.2 copy-done
  7.8 2.9 %fusion.2 = f32[256,512]{1,0:T(8,128)} fusion(f32[256,512]{1,0:T(8,128)} %param.5, f32[512,512]{1,0:T(8,128)S(1)} %copy-done), kind=kOutput, calls=%fused_computation.4 | convolution fusion | flops 805306368 | bytes 2097152 | tf_op jit(solution)/shard_map/dot_general | solution.py:85
  10.6 0.0 all-gather.2.cloned.1.call-update
  10.7 0.0 reduce-scatter.2.cloned.1.call-start
  11.4 0.8 copy.7
  12.1 0.7 reshape_squeeze.6.ids_ref
  12.8 76.7 %all-gather.2.cloned.1.call-done.x_ref = f32[4096,512]{1,0:T(8,128)} async-done(((f32[256,512]{1,0:T(8,128)}), f32[4096,512]{1,0:T(8,128)}) %all-gather.2.cloned.1.call-update) | async-done | bytes 8388624 | tf_op jit(solution)/shard_map/all_gather | solution.py:86
  89.6 15.9 %shard_map.55 = f32[16,264,512]{2,1,0:T(8,128)} custom-call(s32[64]{0:T(128)} %reshape_squeeze.6.ids_ref, s32[1]{0:T(128)} %bitcast.9.cnt_ref, s32[1]{0:T(128)} %bitcast.1.flag_ref, bf16[32,256,256]{2,1,0:T(8,128)(2,1)} %bitcast.12, f32[4096,512]{1,0:T(8,128)} %all-gather.2.cloned.1.call-done.x_ref), custom_call_target="tpu_custom_call" | custom-call | flops 6442450944 | bytes 21233664 | tf_op jit(solution)/shard_map/pallas_call | solution.py:64
  105.5 0.0 reduce-scatter.2.cloned.1.call-update
  105.5 83.0 %reduce-scatter.2.cloned.1.call-done = f32[264,512]{1,0:T(8,128)} async-done(((f32[4224,512]{1,0:T(8,128)}), f32[264,512]{1,0:T(8,128)}) %reduce-scatter.2.cloned.1.call-update) | async-done | bytes 540688 | tf_op jit(solution)/shard_map/reduce_scatter | solution.py:89
  188.5 0.7 fusion.1
  189.2 1.9 fusion
Async XLA Ops:
  6.5 1.2 copy-start
  6.5 83.0 %all-gather.2.cloned.1.call-start = ((), (), s32[]{:S(2)}) async-start(), calls=%async_computation.1 | async-start | bytes 8912896 | tf_op jit(solution)/shard_map/all_gather | solution.py:86
  10.7 177.8 %reduce-scatter.2.cloned.1.call-start = ((), (), s32[]{:S(2)}) async-start(), calls=%async_computation.2 | async-start | bytes 9191424 | tf_op jit(solution)/shard_map/reduce_scatter | solution.py:89
Sparse Core Ops, SparseCore 0:
  10.8 78.7 all-gather.1
  105.6 82.8 reduce-scatter.1

commit v2 on v1

--- a/solution.py
+++ b/solution.py
@@ -8,12 +8,10 @@
 EXTRA = 8
 
 
-def _split3(x):
+def _split2(x):
     hi = x.astype(jnp.bfloat16)
-    r1 = x - hi.astype(jnp.float32)
-    mid = r1.astype(jnp.bfloat16)
-    lo = (r1 - mid.astype(jnp.float32)).astype(jnp.bfloat16)
-    return hi, mid, lo
+    lo = (x - hi.astype(jnp.float32)).astype(jnp.bfloat16)
+    return hi, lo
 
 
 def _tile_kernel(ids_ref, cnt_ref, flag_ref, tile_ref, x_ref, out_ref):
@@ -35,9 +33,8 @@
         tile = tile_ref[0]
         start = pl.multiple_of(j * edge, edge)
         xb = x_ref[pl.ds(start, edge), :]
-        hi, mid, lo = _split3(xb)
+        hi, lo = _split2(xb)
         prod = jnp.dot(tile, hi, preferred_element_type=jnp.float32)
-        prod += jnp.dot(tile, mid, preferred_element_type=jnp.float32)
         prod += jnp.dot(tile, lo, preferred_element_type=jnp.float32)
         out_ref[i, :edge, :] += prod
         first = (lax.broadcasted_iota(jnp.int32, (EXTRA, edge), 0) == 0).astype(jnp.bfloat16)
@@ -60,7 +57,7 @@
         ],
         out_specs=pl.BlockSpec((blocks, edge + EXTRA, width), lambda s, ids, cnt, flag: (0, 0, 0)),
     )
-    flops = slots * edge * edge * width * 2 * 3
+    flops = slots * edge * edge * width * 2 * 2
     return pl.pallas_call(
         _tile_kernel,
         grid_spec=grid_spec,
@@ -82,7 +79,7 @@
     ids = tile_ids[0, 0].reshape(-1)
     cnt = tile_counts[0, 0].reshape(1)
     flag = (lax.axis_index("row") == lax.axis_index("col")).astype(jnp.int32).reshape(1)
-    weighted = jnp.dot(features, weight, precision=lax.Precision.HIGHEST)
+    weighted = jnp.dot(features, weight, precision=lax.Precision.HIGH)
     panel = lax.all_gather(weighted, "row", axis=0, tiled=True)
     partial = _panel_products(ids, cnt, flag, tile_set, panel)
     blocks, height, width = partial.shape

time: 198 us -> 195 us (0.985)
  waiting for transfers between devices: 160 us -> 154 us
  Pallas kernels: 15.9 us -> 19.3 us
    reduce_scatter x1, waiting for transfers between devices: 83 us -> 77.4 us  [shards(): lax.psum_scatter(partial.reshape(blocks * height, width), 'col', scatter_...]
    pallas_call x1, Pallas kernels: 15.9 us -> 19.3 us  [_panel_products(): pl.pallas_call(_tile_kernel, grid_spec=grid_spec, out_shape=jax.ShapeDtyp...]
where the time goes in v2:
time: 195 us
  waiting for transfers between devices  154 us (79%)
  Pallas kernels  19.3 us (10%)
  between operations  14.1 us (7%)
  local copies, waits for them, and re-layouts  2.68 us (1%)
  other arithmetic  2.64 us (1%)
  matrix products  2.45 us (1%)
    reduce_scatter x1, waiting for transfers between devices, shards(): lax.psum_scatter(partial.reshape(blocks * height, width), 'col', scatter_...  77.4 us
    all_gather x1, waiting for transfers between devices, shards(): panel = lax.all_gather(weighted, 'row', axis=0, tiled=True)  76.7 us
    pallas_call x1, Pallas kernels, _panel_products(): pl.pallas_call(_tile_kernel, grid_spec=grid_spec, out_shape=jax.ShapeDtyp...  19.3 us
  transfers between devices with their start and end apart: 2, of which 2 were waited for; matrix products, arithmetic and copies ran while one was open for 1% of the time, Pallas kernels for 0%

profile of v2, /device:TPU:2, one launch (start us, length us, event | category | flops | bytes accessed | tf_op | source)
XLA Modules:
  0.0 195.4 jit_solution(9875021568944549453)
XLA Ops:
  6.5 0.0 copy-start
  6.5 0.0 all-gather.2.cloned.1.call-start
  6.5 1.2 copy-done
  7.8 2.4 %fusion.2 = f32[256,512]{1,0:T(8,128)} fusion(f32[256,512]{1,0:T(8,128)} %param.5, f32[512,512]{1,0:T(8,128)S(1)} %copy-done), kind=kOutput, calls=%fused_computation.4 | convolution fusion | flops 402653184 | bytes 2097152 | tf_op jit(solution)/shard_map/dot_general | solution.py:82
  10.2 0.0 all-gather.2.cloned.1.call-update
  10.2 0.0 reduce-scatter.2.cloned.1.call-start
  10.9 0.8 copy.7
  11.7 0.7 reshape_squeeze.6.ids_ref
  12.4 76.7 %all-gather.2.cloned.1.call-done.x_ref = f32[4096,512]{1,0:T(8,128)} async-done(((f32[256,512]{1,0:T(8,128)}), f32[4096,512]{1,0:T(8,128)}) %all-gather.2.cloned.1.call-update) | async-done | bytes 8388624 | tf_op jit(solution)/shard_map/all_gather | solution.py:83
  89.1 19.3 %shard_map.55 = f32[16,264,512]{2,1,0:T(8,128)} custom-call(s32[64]{0:T(128)} %reshape_squeeze.6.ids_ref, s32[1]{0:T(128)} %bitcast.9.cnt_ref, s32[1]{0:T(128)} %bitcast.1.flag_ref, bf16[32,256,256]{2,1,0:T(8,128)(2,1)} %bitcast.11, f32[4096,512]{1,0:T(8,128)} %all-gather.2.cloned.1.call-done.x_ref), custom_call_target="tpu_custom_call" | custom-call | flops 4294967296 | bytes 21233664 | tf_op jit(solution)/shard_map/pallas_call | solution.py:61
  108.4 0.0 reduce-scatter.2.cloned.1.call-update
  108.4 77.4 %reduce-scatter.2.cloned.1.call-done = f32[264,512]{1,0:T(8,128)} async-done(((f32[4224,512]{1,0:T(8,128)}), f32[264,512]{1,0:T(8,128)}) %reduce-scatter.2.cloned.1.call-update) | async-done | bytes 540688 | tf_op jit(solution)/shard_map/reduce_scatter | solution.py:86
  185.9 0.7 fusion.1
  186.6 1.9 fusion
Async XLA Ops:
  6.5 1.2 copy-start
  6.5 82.6 %all-gather.2.cloned.1.call-start = ((), (), s32[]{:S(2)}) async-start(), calls=%async_computation.1 | async-start | bytes 8912896 | tf_op jit(solution)/shard_map/all_gather | solution.py:83
  10.2 175.6 %reduce-scatter.2.cloned.1.call-start = ((), (), s32[]{:S(2)}) async-start(), calls=%async_computation.2 | async-start | bytes 9191424 | tf_op jit(solution)/shard_map/reduce_scatter | solution.py:86
Sparse Core Ops, SparseCore 0:
  10.4 78.7 all-gather.1
  108.6 77.2 reduce-scatter.1

commit v3 on v2

v3 whole, which is shorter than its diff:
```python
import jax
import jax.numpy as jnp
from jax import lax
from jax.experimental import pallas as pl
from jax.experimental.pallas import tpu as pltpu
from jax.sharding import PartitionSpec as P

EXTRA = 8


def _tile_kernel(ids_ref, cnt_ref, flag_ref, tile_ref, x_ref, extra_ref, out_ref):
    s = pl.program_id(0)
    edge = tile_ref.shape[1]
    blocks = out_ref.shape[0]

    @pl.when(s == 0)
    def _init():
        keep = flag_ref[0] != 0
        for b in range(blocks):
            hi = x_ref[2 * b * edge:(2 * b + 1) * edge, :].astype(jnp.float32)
            lo = x_ref[(2 * b + 1) * edge:(2 * b + 2) * edge, :].astype(jnp.float32)
            own = hi + lo
            out_ref[b, :edge, :] = jnp.where(keep, own, jnp.zeros_like(own))
        out_ref[:, edge:, :] = extra_ref[...]

    @pl.when(s < cnt_ref[0])
    def _add():
        i = ids_ref[2 * s]
        j = ids_ref[2 * s + 1]
        start = pl.multiple_of(j * 2 * edge, 2 * edge)
        pair = x_ref[pl.ds(start, 2 * edge), :]
        out_ref[i, :edge, :] += jnp.dot(tile_ref[0], pair, preferred_element_type=jnp.float32)


def _panel_products(ids, cnt, flag, doubled, panel, extra):
    slots, edge, _ = doubled.shape
    rows, width = panel.shape
    blocks = rows // (2 * edge)
    height = edge + extra.shape[1]
    grid_spec = pltpu.PrefetchScalarGridSpec(
        num_scalar_prefetch=3,
        grid=(slots,),
        in_specs=[
            pl.BlockSpec((1, edge, 2 * edge), lambda s, ids, cnt, flag: (jnp.minimum(s, cnt[0] - 1), 0, 0)),
            pl.BlockSpec((rows, width), lambda s, ids, cnt, flag: (0, 0)),
            pl.BlockSpec(extra.shape, lambda s, ids, cnt, flag: (0, 0, 0)),
        ],
        out_specs=pl.BlockSpec((blocks, height, width), lambda s, ids, cnt, flag: (0, 0, 0)),
    )
    flops = slots * edge * 2 * edge * width * 2
    return pl.pallas_call(
        _tile_kernel,
        grid_spec=grid_spec,
        out_shape=jax.ShapeDtypeStruct((blocks, height, width), jnp.float32),
        compiler_params=pltpu.CompilerParams(
            dimension_semantics=("arbitrary",), vmem_limit_bytes=56 * 1024 * 1024
        ),
        cost_estimate=pl.CostEstimate(
            flops=flops,
            bytes_accessed=doubled.size * 2 + panel.size * 2 + blocks * height * width * 4,
            transcendentals=0,
        ),
    )(ids, cnt, flag, doubled, panel, extra)


def shards(features, weight, tile_values, tile_ids, tile_counts):
    tile_set = tile_values[0, 0]
    slots, edge, _ = tile_set.shape
    slot_ids = tile_ids[0, 0]
    ids = slot_ids.reshape(-1)
    live_count = tile_counts[0, 0]
    cnt = live_count.reshape(1)
    flag = (lax.axis_index("row") == lax.axis_index("col")).astype(jnp.int32).reshape(1)
    weighted = jnp.dot(features, weight, precision=lax.Precision.HIGH)
    rounded = lax.reduce_precision(weighted, exponent_bits=8, mantissa_bits=7)
    hi = rounded.astype(jnp.bfloat16)
    lo = (weighted - rounded).astype(jnp.bfloat16)
    panel = lax.all_gather(jnp.concatenate([hi, lo], axis=0), "row", axis=0, tiled=True)
    blocks = panel.shape[0] // (2 * edge)
    width = panel.shape[1]
    doubled = jnp.concatenate([tile_set, tile_set], axis=2)
    is_live = (jnp.arange(slots) < live_count).astype(jnp.float32)
    placement = (slot_ids[:, 0][:, None] == jnp.arange(blocks)[None, :]).astype(jnp.float32)
    placement = placement * is_live[:, None]
    tile_sums = jnp.sum(tile_set, axis=2, dtype=jnp.float32)
    row_sums = jnp.dot(placement.T, tile_sums, precision=lax.Precision.HIGHEST)
    extra = jnp.zeros((blocks, EXTRA, width), jnp.float32).at[:, 0, :edge].set(row_sums)
    partial = _panel_products(ids, cnt, flag, doubled, panel, extra)
    _, height, _ = partial.shape
    mine = lax.psum_scatter(
        partial.reshape(blocks * height, width), "col", scatter_dimension=0, tiled=True
    )
    degree = 1.0 + mine[edge, :edge]
    inverse_root = lax.rsqrt(degree)
    return jnp.maximum(mine[:edge] * inverse_root[:, None], 0.0)


def solution(mesh):
    in_specs = (
        P(("col", "row"), None),
        P(),
        P("row", "col", None, None, None),
        P("row", "col", None, None),
        P("row", "col"),
    )
    out_specs = P(("row", "col"), None)
    return jax.shard_map(shards, mesh=mesh, in_specs=in_specs, out_specs=out_specs, check_vma=False)
```

time: 195 us -> 195 us (level)
  waiting for transfers between devices: 154 us -> 136 us
  other arithmetic: 2.64 us -> 14.3 us
  Pallas kernels: 19.3 us -> 23.6 us
    all_gather x1, waiting for transfers between devices: 76.7 us -> 64.2 us  [shards(): lax.all_gather(jnp.concatenate([hi, lo], axis=0), 'row', axis=0, tiled=True)]
    concatenate x0 -> x2, other arithmetic: none -> 8.35 us  [the longest x1 7.53 us: shards(): doubled = jnp.concatenate([tile_set, tile_set], axis=2)]
    reduce_scatter x1, waiting for transfers between devices: 77.4 us -> 71.6 us  [shards(): lax.psum_scatter(partial.reshape(blocks * height, width), 'col', scatter_...]
    pallas_call x1, Pallas kernels: 19.3 us -> 23.6 us  [_panel_products(): pl.pallas_call(_tile_kernel, grid_spec=grid_spec, out_shape=jax.ShapeDtyp...]
    reduce_sum x0 -> x1, other arithmetic: none -> 3.34 us  [shards(): tile_sums = jnp.sum(tile_set, axis=2, dtype=jnp.float32)]
  transfers between devices with their start and end apart: 2 -> 2, of which waited for: 2 -> 2; matrix products, arithmetic and copies ran while one was open for 1% -> 7% of each run, Pallas kernels for 0% -> 0%
where the time goes in v3:
time: 195 us; the launch traced here: 194 us
  waiting for transfers between devices  136 us (70%)
  Pallas kernels  23.6 us (12%)
  other arithmetic  14.3 us (7%)
  between operations  14.1 us (7%)
  local copies, waits for them, and re-layouts  4.06 us (2%)
    reduce_scatter x1, waiting for transfers between devices, shards(): lax.psum_scatter(partial.reshape(blocks * height, width), 'col', scatter_...  71.6 us
    all_gather x1, waiting for transfers between devices, shards(): lax.all_gather(jnp.concatenate([hi, lo], axis=0), 'row', axis=0, tiled=True)  64.2 us
    pallas_call x1, Pallas kernels, _panel_products(): pl.pallas_call(_tile_kernel, grid_spec=grid_spec, out_shape=jax.ShapeDtyp...  23.6 us
    concatenate x1, other arithmetic, shards(): doubled = jnp.concatenate([tile_set, tile_set], axis=2)  7.53 us
  transfers between devices with their start and end apart: 2, of which 2 were waited for; matrix products, arithmetic and copies ran while one was open for 7% of the time, Pallas kernels for 0%

profile of v3, /device:TPU:2, one launch (start us, length us, event | category | flops | bytes accessed | tf_op | source)
XLA Modules:
  0.0 194.0 jit_solution(5475497729421768267)
XLA Ops:
  6.5 0.0 copy-start
  6.5 0.0 all-gather.2.cloned.1.call-start
  6.5 1.2 copy-done
  7.8 1.7 reduce-precision_convert_fusion
  9.4 0.8 pad_maximum_fusion.1
  10.3 0.0 all-gather.2.cloned.1.call-update
  10.3 0.0 reduce-scatter.2.cloned.1.call-start
  11.0 0.8 copy.7
  11.7 0.6 reshape_squeeze.6.ids_ref
  12.4 0.7 slice_bitcast_fusion
  13.1 3.3 %convert_reduce_fusion = f32[32,256]{1,0:T(8,128)S(1)} fusion(bf16[1,1,32,256,256]{4,3,2,1,0:T(8,128)(2,1)} %param.9), kind=kLoop, calls=%fused_computation.1 | loop fusion | flops 4186112 | bytes 4227072 | tf_op jit(solution)/shard_map/reduce_sum | solution.py:85
  16.4 0.3 fusion.2
  16.7 0.7 scatter.4.extra_ref
  17.4 7.5 %pad_maximum_fusion.tile_ref = bf16[32,256,512]{2,1,0:T(8,128)(2,1)} fusion(bf16[32,256,256]{2,1,0:T(8,128)(2,1)} %bitcast.18), kind=kLoop, calls=%fused_computation | loop fusion | flops 16777216 | bytes 12582912 | tf_op jit(solution)/shard_map/concatenate | solution.py:81
  25.0 64.2 %all-gather.2.cloned.1.call-done.x_ref = bf16[8192,512]{1,0:T(8,128)(2,1)} async-done(((bf16[512,512]{1,0:T(8,128)(2,1)}), bf16[8192,512]{1,0:T(8,128)(2,1)}) %all-gather.2.cloned.1.call-update) | async-done | bytes 8388624 | tf_op jit(solution)/shard_map/all_gather | solution.py:78
  89.2 23.6 %shard_map.55 = f32[16,264,512]{2,1,0:T(8,128)} custom-call(s32[64]{0:T(128)} %reshape_squeeze.6.ids_ref, s32[1]{0:T(128)} %bitcast.15.cnt_ref, s32[1]{0:T(128)} %bitcast.1.flag_ref, bf16[32,256,512]{2,1,0:T(8,128)(2,1)} %pad_maximum_fusion.tile_ref, bf16[8192,512]{1,0:T(8,128)(2,1)} %all-gather.2.cloned.1.call-done.x_ref, f32[16,8,512]{2,1,0:T(8,128)} %scatter.4.extra_ref), custom_call_target="tpu_custom_call" | custom-call | flops 4294967296 | bytes 25427968 | tf_op jit(solution)/shard_map/pallas_call | solution.py:51
  112.8 0.0 reduce-scatter.2.cloned.1.call-update
  112.9 71.6 %reduce-scatter.2.cloned.1.call-done = f32[264,512]{1,0:T(8,128)} async-done(((f32[4224,512]{1,0:T(8,128)}), f32[264,512]{1,0:T(8,128)}) %reduce-scatter.2.cloned.1.call-update) | async-done | bytes 540688 | tf_op jit(solution)/shard_map/reduce_scatter | solution.py:90
  184.5 0.7 fusion.7
  185.2 1.9 %fusion.1 = f32[256,512]{1,0:T(8,128)} fusion(f32[264,512]{1,0:T(8,128)} %reduce-scatter.2.cloned.1.call-done, f32[256]{0:T(256)S(1)} %bitcast.19), kind=kLoop, calls=%fused_computation.6 | loop fusion | flops 262144 | bytes 1049600 | tf_op jit(solution)/shard_map/max | solution.py:95
  (2 shorter events, 0.0 us)
Async XLA Ops:
  6.5 1.2 copy-start
  6.5 82.7 %all-gather.2.cloned.1.call-start = ((), (), s32[]{:S(2)}) async-start(), calls=%async_computation.1 | async-start | bytes 8912896 | tf_op jit(solution)/shard_map/all_gather | solution.py:78
  10.3 174.2 %reduce-scatter.2.cloned.1.call-start = ((), (), s32[]{:S(2)}) async-start(), calls=%async_computation.2 | async-start | bytes 9191424 | tf_op jit(solution)/shard_map/reduce_scatter | solution.py:90
Sparse Core Ops, SparseCore 0:
  10.4 78.7 all-gather.1
  113.0 71.4 reduce-scatter.1

commit v4 on v3

--- a/solution.py
+++ b/solution.py
@@ -8,44 +8,59 @@
 EXTRA = 8
 
 
-def _tile_kernel(ids_ref, cnt_ref, flag_ref, tile_ref, x_ref, extra_ref, out_ref):
+def _tile_kernel(ids_ref, cnt_ref, flag_ref, tile_ref, x_ref, extra_ref, panel_ref, out_ref, own_ref, sem):
     s = pl.program_id(0)
     edge = tile_ref.shape[1]
     blocks = out_ref.shape[0]
 
     @pl.when(s == 0)
     def _init():
-        keep = flag_ref[0] != 0
-        for b in range(blocks):
-            hi = x_ref[2 * b * edge:(2 * b + 1) * edge, :].astype(jnp.float32)
-            lo = x_ref[(2 * b + 1) * edge:(2 * b + 2) * edge, :].astype(jnp.float32)
-            own = hi + lo
-            out_ref[b, :edge, :] = jnp.where(keep, own, jnp.zeros_like(own))
         out_ref[:, edge:, :] = extra_ref[...]
+
+        @pl.when(flag_ref[0] != 0)
+        def _diagonal():
+            copy = pltpu.make_async_copy(panel_ref, own_ref, sem)
+            copy.start()
+            copy.wait()
+            for b in range(blocks):
+                own = own_ref[b, :edge, :].astype(jnp.float32) + own_ref[b, edge:, :].astype(jnp.float32)
+                out_ref[b, :edge, :] = own
+
+        @pl.when(flag_ref[0] == 0)
+        def _elsewhere():
+            out_ref[:, :edge, :] = jnp.zeros((blocks, edge, out_ref.shape[2]), jnp.float32)
 
     @pl.when(s < cnt_ref[0])
     def _add():
         i = ids_ref[2 * s]
-        j = ids_ref[2 * s + 1]
-        start = pl.multiple_of(j * 2 * edge, 2 * edge)
-        pair = x_ref[pl.ds(start, 2 * edge), :]
-        out_ref[i, :edge, :] += jnp.dot(tile_ref[0], pair, preferred_element_type=jnp.float32)
+        out_ref[i, :edge, :] += jnp.dot(tile_ref[0], x_ref[0], preferred_element_type=jnp.float32)
+
+
+def _live_slot(s, cnt):
+    return jnp.minimum(s, cnt[0] - 1)
 
 
 def _panel_products(ids, cnt, flag, doubled, panel, extra):
     slots, edge, _ = doubled.shape
-    rows, width = panel.shape
-    blocks = rows // (2 * edge)
+    blocks, pair, width = panel.shape
     height = edge + extra.shape[1]
     grid_spec = pltpu.PrefetchScalarGridSpec(
         num_scalar_prefetch=3,
         grid=(slots,),
         in_specs=[
-            pl.BlockSpec((1, edge, 2 * edge), lambda s, ids, cnt, flag: (jnp.minimum(s, cnt[0] - 1), 0, 0)),
-            pl.BlockSpec((rows, width), lambda s, ids, cnt, flag: (0, 0)),
+            pl.BlockSpec((1, edge, 2 * edge), lambda s, ids, cnt, flag: (_live_slot(s, cnt), 0, 0)),
+            pl.BlockSpec(
+                (1, pair, width),
+                lambda s, ids, cnt, flag: (ids[2 * _live_slot(s, cnt) + 1], 0, 0),
+            ),
             pl.BlockSpec(extra.shape, lambda s, ids, cnt, flag: (0, 0, 0)),
+            pl.BlockSpec(memory_space=pl.ANY),
         ],
         out_specs=pl.BlockSpec((blocks, height, width), lambda s, ids, cnt, flag: (0, 0, 0)),
+        scratch_shapes=[
+            pltpu.VMEM((blocks, pair, width), panel.dtype),
+            pltpu.SemaphoreType.DMA,
+        ],
     )
     flops = slots * edge * 2 * edge * width * 2
     return pl.pallas_call(
@@ -60,7 +75,7 @@
             bytes_accessed=doubled.size * 2 + panel.size * 2 + blocks * height * width * 4,
             transcendentals=0,
         ),
-    )(ids, cnt, flag, doubled, panel, extra)
+    )(ids, cnt, flag, doubled, panel, extra, panel)
 
 
 def shards(features, weight, tile_values, tile_ids, tile_counts):
@@ -85,7 +100,7 @@
     tile_sums = jnp.sum(tile_set, axis=2, dtype=jnp.float32)
     row_sums = jnp.dot(placement.T, tile_sums, precision=lax.Precision.HIGHEST)
     extra = jnp.zeros((blocks, EXTRA, width), jnp.float32).at[:, 0, :edge].set(row_sums)
-    partial = _panel_products(ids, cnt, flag, doubled, panel, extra)
+    partial = _panel_products(ids, cnt, flag, doubled, panel.reshape(blocks, 2 * edge, width), extra)
     _, height, _ = partial.shape
     mine = lax.psum_scatter(
         partial.reshape(blocks * height, width), "col", scatter_dimension=0, tiled=True

time: 195 us -> 198 us (1.015)
  waiting for transfers between devices: 136 us -> 141 us
    reduce_scatter x1, waiting for transfers between devices: 71.6 us -> 77.2 us  [shards(): lax.psum_scatter(partial.reshape(blocks * height, width), 'col', scatter_...]
where the time goes in v4:
time: 198 us
  waiting for transfers between devices  141 us (71%)
  Pallas kernels  21.8 us (11%)
  other arithmetic  14.3 us (7%)
  between operations  14.1 us (7%)
  local copies, waits for them, and re-layouts  4.06 us (2%)
    reduce_scatter x1, waiting for transfers between devices, shards(): lax.psum_scatter(partial.reshape(blocks * height, width), 'col', scatter_...  77.2 us
    all_gather x1, waiting for transfers between devices, shards(): lax.all_gather(jnp.concatenate([hi, lo], axis=0), 'row', axis=0, tiled=True)  64.2 us
    pallas_call x1, Pallas kernels, _panel_products(): pl.pallas_call(_tile_kernel, grid_spec=grid_spec, out_shape=jax.ShapeDtyp...  21.8 us
    concatenate x1, other arithmetic, shards(): doubled = jnp.concatenate([tile_set, tile_set], axis=2)  7.53 us
  transfers between devices with their start and end apart: 2, of which 2 were waited for; matrix products, arithmetic and copies ran while one was open for 7% of the time, Pallas kernels for 0%

profile of v4, /device:TPU:2, one launch (start us, length us, event | category | flops | bytes accessed | tf_op | source)
XLA Modules:
  0.0 197.7 jit_solution(5554919514901695361)
XLA Ops:
  6.5 0.0 copy-start
  6.5 0.0 all-gather.2.cloned.1.call-start
  6.5 1.2 copy-done
  7.8 1.7 reduce-precision_convert_fusion
  9.4 0.8 pad_maximum_fusion.1
  10.3 0.0 all-gather.2.cloned.1.call-update
  10.3 0.0 reduce-scatter.2.cloned.1.call-start
  11.0 0.8 copy.7
  11.7 0.6 reshape_squeeze.6.ids_ref
  12.4 0.7 slice_bitcast_fusion
  13.1 3.3 %convert_reduce_fusion = f32[32,256]{1,0:T(8,128)S(1)} fusion(bf16[1,1,32,256,256]{4,3,2,1,0:T(8,128)(2,1)} %param.9), kind=kLoop, calls=%fused_computation.1 | loop fusion | flops 4186112 | bytes 4227072 | tf_op jit(solution)/shard_map/reduce_sum | solution.py:100
  16.4 0.3 fusion.2
  16.7 0.7 scatter.4.extra_ref
  17.4 7.5 %pad_maximum_fusion.tile_ref = bf16[32,256,512]{2,1,0:T(8,128)(2,1)} fusion(bf16[32,256,256]{2,1,0:T(8,128)(2,1)} %bitcast.21), kind=kLoop, calls=%fused_computation | loop fusion | flops 16777216 | bytes 12582912 | tf_op jit(solution)/shard_map/concatenate | solution.py:96
  25.0 64.2 %all-gather.2.cloned.1.call-done = bf16[8192,512]{1,0:T(8,128)(2,1)} async-done(((bf16[512,512]{1,0:T(8,128)(2,1)}), bf16[8192,512]{1,0:T(8,128)(2,1)}) %all-gather.2.cloned.1.call-update) | async-done | bytes 8388624 | tf_op jit(solution)/shard_map/all_gather | solution.py:93
  89.2 21.8 %shard_map.55 = f32[16,264,512]{2,1,0:T(8,128)} custom-call(s32[64]{0:T(128)} %reshape_squeeze.6.ids_ref, s32[1]{0:T(128)} %bitcast.16.cnt_ref, s32[1]{0:T(128)} %bitcast.1.flag_ref, bf16[32,256,512]{2,1,0:T(8,128)(2,1)} %pad_maximum_fusion.tile_ref, bf16[16,512,512]{2,1,0:T(8,128)(2,1)} %bitcast.19, f32[16,8,512]{2,1,0:T(8,128)} %scatter.4.extra_ref, ...), custom_call_target="tpu_custom_call" | custom-call | flops 4294967296 | bytes 25427968 | tf_op jit(solution)/shard_map/pallas_call | solution.py:66
  111.0 0.0 reduce-scatter.2.cloned.1.call-update
  111.0 77.2 %reduce-scatter.2.cloned.1.call-done = f32[264,512]{1,0:T(8,128)} async-done(((f32[4224,512]{1,0:T(8,128)}), f32[264,512]{1,0:T(8,128)}) %reduce-scatter.2.cloned.1.call-update) | async-done | bytes 540688 | tf_op jit(solution)/shard_map/reduce_scatter | solution.py:105
  188.3 0.7 fusion.7
  189.0 1.9 fusion.1
  (2 shorter events, 0.0 us)
Async XLA Ops:
  6.5 1.2 copy-start
  6.5 82.7 %all-gather.2.cloned.1.call-start = ((), (), s32[]{:S(2)}) async-start(), calls=%async_computation.1 | async-start | bytes 8912896 | tf_op jit(solution)/shard_map/all_gather | solution.py:93
  10.3 178.0 %reduce-scatter.2.cloned.1.call-start = ((), (), s32[]{:S(2)}) async-start(), calls=%async_computation.2 | async-start | bytes 9191424 | tf_op jit(solution)/shard_map/reduce_scatter | solution.py:105
Sparse Core Ops, SparseCore 0:
  10.4 78.7 all-gather.1
  111.2 77.0 reduce-scatter.1

commit v5 on v4

v5 whole, which is shorter than its diff:
```python
import jax
import jax.numpy as jnp
from jax import lax
from jax.experimental import pallas as pl
from jax.experimental.pallas import tpu as pltpu
from jax.sharding import PartitionSpec as P

EXTRA = 8


def _tile_kernel(ids_ref, cnt_ref, flag_ref, tile_ref, x_ref, extra_ref, panel_ref, out_ref, own_ref, sem):
    s = pl.program_id(0)
    blocks, height, edge = out_ref.shape
    width = x_ref.shape[1] // 2

    @pl.when(s == 0)
    def _init():
        out_ref[:, width:, :] = extra_ref[...]

        @pl.when(flag_ref[0] != 0)
        def _diagonal():
            copy = pltpu.make_async_copy(panel_ref, own_ref, sem)
            copy.start()
            copy.wait()
            for b in range(blocks):
                own = own_ref[b, :width, :].astype(jnp.float32) + own_ref[b, width:, :].astype(jnp.float32)
                out_ref[b, :width, :] = own

        @pl.when(flag_ref[0] == 0)
        def _elsewhere():
            out_ref[:, :width, :] = jnp.zeros((blocks, width, edge), jnp.float32)

    @pl.when(s < cnt_ref[0])
    def _add():
        i = ids_ref[2 * s]
        both = jnp.dot(x_ref[0], tile_ref[0], preferred_element_type=jnp.float32)
        out_ref[i, :width, :] += both[:width] + both[width:]


def _live_slot(s, cnt):
    return jnp.minimum(s, cnt[0] - 1)


def _panel_products(ids, cnt, flag, turned, panel, extra):
    slots, edge, _ = turned.shape
    blocks, pair, _ = panel.shape
    width = pair // 2
    height = width + extra.shape[1]
    grid_spec = pltpu.PrefetchScalarGridSpec(
        num_scalar_prefetch=3,
        grid=(slots,),
        in_specs=[
            pl.BlockSpec((1, edge, edge), lambda s, ids, cnt, flag: (_live_slot(s, cnt), 0, 0)),
            pl.BlockSpec(
                (1, pair, edge),
                lambda s, ids, cnt, flag: (ids[2 * _live_slot(s, cnt) + 1], 0, 0),
            ),
            pl.BlockSpec(extra.shape, lambda s, ids, cnt, flag: (0, 0, 0)),
            pl.BlockSpec(memory_space=pl.ANY),
        ],
        out_specs=pl.BlockSpec((blocks, height, edge), lambda s, ids, cnt, flag: (0, 0, 0)),
        scratch_shapes=[
            pltpu.VMEM((blocks, pair, edge), panel.dtype),
            pltpu.SemaphoreType.DMA,
        ],
    )
    flops = slots * pair * edge * edge * 2
    return pl.pallas_call(
        _tile_kernel,
        grid_spec=grid_spec,
        out_shape=jax.ShapeDtypeStruct((blocks, height, edge), jnp.float32),
        compiler_params=pltpu.CompilerParams(
            dimension_semantics=("arbitrary",), vmem_limit_bytes=56 * 1024 * 1024
        ),
        cost_estimate=pl.CostEstimate(
            flops=flops,
            bytes_accessed=turned.size * 2 + panel.size * 2 + blocks * height * edge * 4,
            transcendentals=0,
        ),
    )(ids, cnt, flag, turned, panel, extra, panel)


def shards(features, weight, tile_values, tile_ids, tile_counts):
    tile_set = tile_values[0, 0]
    slots, edge, _ = tile_set.shape
    slot_ids = tile_ids[0, 0]
    ids = slot_ids.reshape(-1)
    live_count = tile_counts[0, 0]
    cnt = live_count.reshape(1)
    flag = (lax.axis_index("row") == lax.axis_index("col")).astype(jnp.int32).reshape(1)
    turned_w = lax.dot_general(
        weight, features, (((0,), (1,)), ((), ())), precision=lax.Precision.HIGH
    )
    rounded = lax.reduce_precision(turned_w, exponent_bits=8, mantissa_bits=7)
    hi = rounded.astype(jnp.bfloat16)
    lo = (turned_w - rounded).astype(jnp.bfloat16)
    stacked = jnp.concatenate([hi, lo], axis=0)[None]
    panel = lax.all_gather(stacked, "row", axis=0, tiled=True)
    blocks, pair, _ = panel.shape
    width = pair // 2
    turned = jnp.swapaxes(tile_set, 1, 2)
    is_live = (jnp.arange(slots) < live_count).astype(jnp.float32)
    placement = (slot_ids[:, 0][:, None] == jnp.arange(blocks)[None, :]).astype(jnp.float32)
    placement = placement * is_live[:, None]
    tile_sums = jnp.sum(tile_set, axis=2, dtype=jnp.float32)
    row_sums = jnp.dot(placement.T, tile_sums, precision=lax.Precision.HIGHEST)
    extra = jnp.zeros((blocks, EXTRA, edge), jnp.float32).at[:, 0, :].set(row_sums)
    partial = _panel_products(ids, cnt, flag, turned, panel, extra)
    _, height, _ = partial.shape
    mine = lax.psum_scatter(
        partial.reshape(blocks * height, edge), "col", scatter_dimension=0, tiled=True
    )
    degree = 1.0 + mine[width]
    inverse_root = lax.rsqrt(degree)
    return jnp.maximum(mine[:width].T * inverse_root[:, None], 0.0)


def solution(mesh):
    in_specs = (
        P(("col", "row"), None),
        P(),
        P("row", "col", None, None, None),
        P("row", "col", None, None),
        P("row", "col"),
    )
    out_specs = P(("row", "col"), None)
    return jax.shard_map(shards, mesh=mesh, in_specs=in_specs, out_specs=out_specs, check_vma=False)
```

time: 198 us -> 195 us (0.985)
  other arithmetic: 14.3 us -> 4.73 us
  local copies, waits for them, and re-layouts: 4.06 us -> 11.8 us
  Pallas kernels: 21.8 us -> 17.2 us
  waiting for transfers between devices: 141 us -> 145 us
    unnamed x2 -> x3, waiting for transfers between devices: 0.03 us -> 78.5 us
    reduce_scatter x1 -> x0, waiting for transfers between devices: 77.2 us -> none  [shards(): lax.psum_scatter(partial.reshape(blocks * height, width), 'col', scatter_...]
    concatenate x2 -> x1, other arithmetic: 8.35 us -> 0.83 us  [shards(): stacked = jnp.concatenate([hi, lo], axis=0)[None]]
    unnamed x3 -> x8, local copies, waits for them, and re-layouts: 1.98 us -> 8.76 us
    pallas_call x1, Pallas kernels: 21.8 us -> 17.2 us  [_panel_products(): pl.pallas_call(_tile_kernel, grid_spec=grid_spec, out_shape=jax.ShapeDtyp...]
    all_gather x1, waiting for transfers between devices: 64.2 us -> 66.5 us  [shards(): panel = lax.all_gather(stacked, 'row', axis=0, tiled=True)]
  transfers between devices with their start and end apart: 2 -> 2, of which waited for: 2 -> 2; matrix products, arithmetic and copies ran while one was open for 7% -> 6% of each run, Pallas kernels for 0% -> 0%
where the time goes in v5:
time: 195 us
  waiting for transfers between devices  145 us (74%)
  Pallas kernels  17.2 us (9%)
  between operations  14.1 us (7%)
  local copies, waits for them, and re-layouts  11.8 us (6%)
  other arithmetic  4.73 us (2%)
  matrix products  2.3 us (1%)
    unnamed x3, waiting for transfers between devices  78.5 us
    all_gather x1, waiting for transfers between devices, shards(): panel = lax.all_gather(stacked, 'row', axis=0, tiled=True)  66.5 us
    pallas_call x1, Pallas kernels, _panel_products(): pl.pallas_call(_tile_kernel, grid_spec=grid_spec, out_shape=jax.ShapeDtyp...  17.2 us
    unnamed x8, local copies, waits for them, and re-layouts  8.76 us
  transfers between devices with their start and end apart: 2, of which 2 were waited for; matrix products, arithmetic and copies ran while one was open for 6% of the time, Pallas kernels for 0%

profile of v5, /device:TPU:2, one launch (start us, length us, event | category | flops | bytes accessed | tf_op | source)
XLA Modules:
  0.0 195.2 jit_solution(9536295557443145604)
XLA Ops:
  6.5 0.0 copy-start
  6.5 0.0 all-gather.3.cloned.1.call-start
  6.5 1.2 copy-done
  7.8 2.0 %reduce-precision_convert_fusion = (bf16[512,256]{1,0:T(8,128)(2,1)S(1)}, bf16[512,256]{1,0:T(8,128)(2,1)S(1)}) fusion(f32[512,512]{1,0:T(8,128)S(1)} %copy-done, f32[256,512]{1,0:T(8,128)} %param.7), kind=kOutput, calls=%fused_computation.2 | convolution fusion | flops 403177472 | bytes 2097152 | tf_op jit(solution)/shard_map/dot_general | solution.py:91
  9.8 0.8 pad_maximum_fusion
  10.6 0.0 all-gather.3.cloned.1.call-update
  10.7 0.0 reduce-scatter.4.cloned.1.call-start
  11.4 0.8 copy.12
  12.1 0.6 reshape_squeeze.6.ids_ref
  12.8 6.4 %copy.13 = bf16[1,1,32,256,256]{3,4,2,1,0:T(8,128)(2,1)} copy(bf16[1,1,32,256,256]{4,3,2,1,0:T(8,128)(2,1)} %param.9) | data formatting | bytes 8388608 | tf_op args[2]
  19.2 0.0 copy-done.1
  19.2 2.9 %convert_reduce_fusion = f32[32,256]{1,0:T(8,128)S(1)} fusion(bf16[1,1,32,256,256]{3,4,2,1,0:T(8,128)(2,1)} %copy.13), kind=kLoop, calls=%fused_computation | loop fusion | flops 4186112 | bytes 4227072 | tf_op jit(solution)/shard_map/reduce_sum | solution.py:105
  22.1 0.3 fusion.1
  22.4 0.7 scatter.4.extra_ref
  23.0 66.5 %all-gather.3.cloned.1.call-done = bf16[16384,256]{1,0:T(8,128)(2,1)} async-done(((bf16[1024,256]{1,0:T(8,128)(2,1)}), bf16[16384,256]{1,0:T(8,128)(2,1)}) %all-gather.3.cloned.1.call-update) | async-done | bytes 8388624 | tf_op jit(solution)/shard_map/all_gather | solution.py:98
  89.6 17.2 %shard_map.55 = f32[16,520,256]{2,1,0:T(8,128)} custom-call(s32[64]{0:T(128)} %reshape_squeeze.6.ids_ref, s32[1]{0:T(128)} %bitcast.20.cnt_ref, s32[1]{0:T(128)} %bitcast.1.flag_ref, bf16[32,256,256]{2,1,0:T(8,128)(2,1)} %bitcast.22, bf16[16,1024,256]{2,1,0:T(8,128)(2,1)} %bitcast.24, f32[16,8,256]{2,1,0:T(8,128)} %scatter.4.extra_ref, ...), custom_call_target="tpu_custom_call" | custom-call | flops 4294967296 | bytes 21102592 | tf_op jit(solution)/shard_map/pallas_call | solution.py:68
  106.7 0.0 reduce-scatter.4.cloned.1.call-update
  106.8 78.5 %reduce-scatter.4.cloned.1.call-done = f32[520,256]{1,0:T(8,128)} async-done(((f32[8320,256]{1,0:T(8,128)}), f32[520,256]{1,0:T(8,128)}) %reduce-scatter.4.cloned.1.call-update) | async-done | bytes 532496
  185.2 1.1 slice.31
  186.3 0.2 copy.17
  186.5 0.7 slice.32
  187.2 0.1 copy.18
  187.3 0.1 rsqrt_reduce_fusion
  187.5 0.9 maximum_bitcast_fusion
  (4 shorter events, 0.0 us)
Async XLA Ops:
  6.5 1.2 copy-start
  6.5 12.7 %copy-start.1 = (s32[1,1,32,2]{2,3,1,0:T(2,128)S(1)}, s32[1,1,32,2]{2,3,1,0:T(2,128)}, u32[]{:S(2)}) copy-start(s32[1,1,32,2]{2,3,1,0:T(2,128)} %param.10) | copy-start | bytes 772
  6.5 83.0 %all-gather.3.cloned.1.call-start = ((), (), s32[]{:S(2)}) async-start(), calls=%async_computation.1 | async-start | bytes 8912896 | tf_op jit(solution)/shard_map/all_gather | solution.py:98
  10.7 174.6 %reduce-scatter.4.cloned.1.call-start = ((), (), s32[]{:S(2)}) async-start(), calls=%async_computation.2 | async-start | bytes 9052160
Sparse Core Ops, SparseCore 0:
  10.8 78.7 all-gather.2
  106.9 78.2 reduce-scatter.3

commit v6 on v5

--- a/solution.py
+++ b/solution.py
@@ -8,37 +8,29 @@
 EXTRA = 8
 
 
-def _tile_kernel(ids_ref, cnt_ref, flag_ref, tile_ref, x_ref, extra_ref, panel_ref, out_ref, own_ref, sem):
-    s = pl.program_id(0)
+def _tile_kernel(ids_ref, cnt_ref, flag_ref, tile_ref, x_ref, extra_ref, out_ref):
     blocks, height, edge = out_ref.shape
     width = x_ref.shape[1] // 2
+    out_ref[:, width:, :] = extra_ref[...]
 
-    @pl.when(s == 0)
-    def _init():
-        out_ref[:, width:, :] = extra_ref[...]
+    @pl.when(flag_ref[0] != 0)
+    def _diagonal():
+        for b in range(blocks):
+            own = x_ref[b, :width, :].astype(jnp.float32) + x_ref[b, width:, :].astype(jnp.float32)
+            out_ref[b, :width, :] = own
 
-        @pl.when(flag_ref[0] != 0)
-        def _diagonal():
-            copy = pltpu.make_async_copy(panel_ref, own_ref, sem)
-            copy.start()
-            copy.wait()
-            for b in range(blocks):
-                own = own_ref[b, :width, :].astype(jnp.float32) + own_ref[b, width:, :].astype(jnp.float32)
-                out_ref[b, :width, :] = own
+    @pl.when(flag_ref[0] == 0)
+    def _elsewhere():
+        out_ref[:, :width, :] = jnp.zeros((blocks, width, edge), jnp.float32)
 
-        @pl.when(flag_ref[0] == 0)
-        def _elsewhere():
-            out_ref[:, :width, :] = jnp.zeros((blocks, width, edge), jnp.float32)
+    def one_slot(s, carry):
+        i = ids_ref[2 * s]
+        j = ids_ref[2 * s + 1]
+        both = jnp.dot(x_ref[j], tile_ref[s], preferred_element_type=jnp.float32)
+        out_ref[i, :width, :] += both[:width] + both[width:]
+        return carry
 
-    @pl.when(s < cnt_ref[0])
-    def _add():
-        i = ids_ref[2 * s]
-        both = jnp.dot(x_ref[0], tile_ref[0], preferred_element_type=jnp.float32)
-        out_ref[i, :width, :] += both[:width] + both[width:]
-
-
-def _live_slot(s, cnt):
-    return jnp.minimum(s, cnt[0] - 1)
+    lax.fori_loop(0, cnt_ref[0], one_slot, 0)
 
 
 def _panel_products(ids, cnt, flag, turned, panel, extra):
@@ -46,38 +38,21 @@
     blocks, pair, _ = panel.shape
     width = pair // 2
     height = width + extra.shape[1]
-    grid_spec = pltpu.PrefetchScalarGridSpec(
-        num_scalar_prefetch=3,
-        grid=(slots,),
-        in_specs=[
-            pl.BlockSpec((1, edge, edge), lambda s, ids, cnt, flag: (_live_slot(s, cnt), 0, 0)),
-            pl.BlockSpec(
-                (1, pair, edge),
-                lambda s, ids, cnt, flag: (ids[2 * _live_slot(s, cnt) + 1], 0, 0),
-            ),
-            pl.BlockSpec(extra.shape, lambda s, ids, cnt, flag: (0, 0, 0)),
-            pl.BlockSpec(memory_space=pl.ANY),
-        ],
-        out_specs=pl.BlockSpec((blocks, height, edge), lambda s, ids, cnt, flag: (0, 0, 0)),
-        scratch_shapes=[
-            pltpu.VMEM((blocks, pair, edge), panel.dtype),
-            pltpu.SemaphoreType.DMA,
-        ],
-    )
+    smem = pl.BlockSpec(memory_space=pltpu.SMEM)
+    vmem = pl.BlockSpec(memory_space=pltpu.VMEM)
     flops = slots * pair * edge * edge * 2
     return pl.pallas_call(
         _tile_kernel,
-        grid_spec=grid_spec,
+        in_specs=[smem, smem, smem, vmem, vmem, vmem],
+        out_specs=vmem,
         out_shape=jax.ShapeDtypeStruct((blocks, height, edge), jnp.float32),
-        compiler_params=pltpu.CompilerParams(
-            dimension_semantics=("arbitrary",), vmem_limit_bytes=56 * 1024 * 1024
-        ),
+        compiler_params=pltpu.CompilerParams(vmem_limit_bytes=56 * 1024 * 1024),
         cost_estimate=pl.CostEstimate(
             flops=flops,
             bytes_accessed=turned.size * 2 + panel.size * 2 + blocks * height * edge * 4,
             transcendentals=0,
         ),
-    )(ids, cnt, flag, turned, panel, extra, panel)
+    )(ids, cnt, flag, turned, panel, extra)
 
 
 def shards(features, weight, tile_values, tile_ids, tile_counts):

time: 195 us -> 187 us (0.959)
  Pallas kernels: 17.2 us -> 9.62 us
    pallas_call x1, Pallas kernels: 17.2 us -> 9.62 us  [_panel_products(): pl.pallas_call(_tile_kernel, in_specs=[smem, smem, smem, vmem, vmem, vmem...]
where the time goes in v6:
time: 187 us
  waiting for transfers between devices  144 us (77%)
  between operations  14.1 us (8%)
  local copies, waits for them, and re-layouts  11.8 us (6%)
  Pallas kernels  9.62 us (5%)
  other arithmetic  4.73 us (3%)
  matrix products  2.3 us (1%)
    unnamed x3, waiting for transfers between devices  77.3 us
    all_gather x1, waiting for transfers between devices, shards(): panel = lax.all_gather(stacked, 'row', axis=0, tiled=True)  66.5 us
    pallas_call x1, Pallas kernels, _panel_products(): pl.pallas_call(_tile_kernel, in_specs=[smem, smem, smem, vmem, vmem, vmem...  9.62 us
    unnamed x8, local copies, waits for them, and re-layouts  8.76 us
  transfers between devices with their start and end apart: 2, of which 2 were waited for; matrix products, arithmetic and copies ran while one was open for 6% of the time, Pallas kernels for 0%

profile of v6, /device:TPU:2, one launch (start us, length us, event | category | flops | bytes accessed | tf_op | source)
XLA Modules:
  0.0 186.5 jit_solution(17297842886078214429)
XLA Ops:
  6.5 0.0 copy-start
  6.5 0.0 all-gather.3.cloned.1.call-start
  6.5 1.2 copy-done
  7.8 2.0 %reduce-precision_convert_fusion = (bf16[512,256]{1,0:T(8,128)(2,1)S(1)}, bf16[512,256]{1,0:T(8,128)(2,1)S(1)}) fusion(f32[512,512]{1,0:T(8,128)S(1)} %copy-done, f32[256,512]{1,0:T(8,128)} %param.7), kind=kOutput, calls=%fused_computation.2 | convolution fusion | flops 403177472 | bytes 2097152 | tf_op jit(solution)/shard_map/dot_general | solution.py:66
  9.8 0.8 pad_maximum_fusion
  10.6 0.0 all-gather.3.cloned.1.call-update
  10.7 0.0 reduce-scatter.4.cloned.1.call-start
  11.4 0.8 copy.12
  12.1 0.6 reshape_squeeze.6.ids_ref
  12.8 6.4 %copy.13 = bf16[1,1,32,256,256]{3,4,2,1,0:T(8,128)(2,1)} copy(bf16[1,1,32,256,256]{4,3,2,1,0:T(8,128)(2,1)} %param.9) | data formatting | bytes 8388608 | tf_op args[2]
  19.2 0.0 copy-done.1
  19.2 2.9 %convert_reduce_fusion = f32[32,256]{1,0:T(8,128)S(1)} fusion(bf16[1,1,32,256,256]{3,4,2,1,0:T(8,128)(2,1)} %copy.13), kind=kLoop, calls=%fused_computation | loop fusion | flops 4186112 | bytes 4227072 | tf_op jit(solution)/shard_map/reduce_sum | solution.py:80
  22.1 0.3 fusion.1
  22.4 0.7 scatter.4.extra_ref
  23.0 66.5 %all-gather.3.cloned.1.call-done = bf16[16384,256]{1,0:T(8,128)(2,1)} async-done(((bf16[1024,256]{1,0:T(8,128)(2,1)}), bf16[16384,256]{1,0:T(8,128)(2,1)}) %all-gather.3.cloned.1.call-update) | async-done | bytes 8388624 | tf_op jit(solution)/shard_map/all_gather | solution.py:73
  89.6 9.6 %shard_map.55 = f32[16,520,256]{2,1,0:T(8,128)} custom-call(s32[64]{0:T(128)} %reshape_squeeze.6.ids_ref, s32[1]{0:T(128)} %bitcast.20.cnt_ref, s32[1]{0:T(128)} %bitcast.1.flag_ref, bf16[32,256,256]{2,1,0:T(8,128)(2,1)} %bitcast.22, bf16[16,1024,256]{2,1,0:T(8,128)(2,1)} %bitcast.24, f32[16,8,256]{2,1,0:T(8,128)} %scatter.4.extra_ref), custom_call_target="tpu_custom_call" | custom-call | flops 4294967296 | bytes 21102592 | tf_op jit(solution)/shard_map/pallas_call | solution.py:44
  99.2 0.0 reduce-scatter.4.cloned.1.call-update
  99.2 77.3 %reduce-scatter.4.cloned.1.call-done = f32[520,256]{1,0:T(8,128)} async-done(((f32[8320,256]{1,0:T(8,128)}), f32[520,256]{1,0:T(8,128)}) %reduce-scatter.4.cloned.1.call-update) | async-done | bytes 532496
  176.5 1.1 slice.31
  177.6 0.2 copy.17
  177.8 0.7 slice.32
  178.5 0.1 copy.18
  178.6 0.1 rsqrt_reduce_fusion
  178.8 0.9 maximum_bitcast_fusion
  (4 shorter events, 0.0 us)
Async XLA Ops:
  6.5 1.2 copy-start
  6.5 12.7 %copy-start.1 = (s32[1,1,32,2]{2,3,1,0:T(2,128)S(1)}, s32[1,1,32,2]{2,3,1,0:T(2,128)}, u32[]{:S(2)}) copy-start(s32[1,1,32,2]{2,3,1,0:T(2,128)} %param.10) | copy-start | bytes 772
  6.5 83.0 %all-gather.3.cloned.1.call-start = ((), (), s32[]{:S(2)}) async-start(), calls=%async_computation.1 | async-start | bytes 8912896 | tf_op jit(solution)/shard_map/all_gather | solution.py:73
  10.7 165.9 %reduce-scatter.4.cloned.1.call-start = ((), (), s32[]{:S(2)}) async-start(), calls=%async_computation.2 | async-start | bytes 9052160
Sparse Core Ops, SparseCore 0:
  10.8 78.7 all-gather.2
  99.3 77.1 reduce-scatter.3

commit v7 on v6

v7 whole, which is shorter than its diff:
```python
import jax
import jax.numpy as jnp
from jax import lax
from jax.experimental import pallas as pl
from jax.experimental.pallas import tpu as pltpu
from jax.sharding import PartitionSpec as P

EXTRA = 8


def _tile_kernel(ids_ref, cnt_ref, pos_ref, tile_ref, xa_ref, xb_ref, extra_ref, out_ref):
    blocks, height, edge = out_ref.shape
    part = xa_ref.shape[1] // 2
    side = pos_ref[2]
    x = pos_ref[0]
    y = pos_ref[1]
    if height > 2 * part:
        out_ref[:, 2 * part:, :] = extra_ref[...]

    def where_of(j):
        dx = (j % side - x + side) % side
        dy = (j // side - y + side) % side
        return dy * side + dx, dx * side + dy

    def add_block(i, a_idx, b_idx, tile):
        for ref, at, lo in ((xa_ref, a_idx, 0), (xb_ref, b_idx, part)):
            both = jnp.dot(ref[at], tile, preferred_element_type=jnp.float32)
            out_ref[i, lo:lo + part, :] += both[:part] + both[part:]

    out_ref[:, :2 * part, :] = jnp.zeros((blocks, 2 * part, edge), jnp.float32)

    @pl.when(pos_ref[3] != 0)
    def _diagonal():
        for b in range(blocks):
            a_idx, b_idx = where_of(b)
            for ref, at, lo in ((xa_ref, a_idx, 0), (xb_ref, b_idx, part)):
                own = ref[at, :part, :].astype(jnp.float32) + ref[at, part:, :].astype(jnp.float32)
                out_ref[b, lo:lo + part, :] = own

    def one_slot(s, carry):
        i = ids_ref[2 * s]
        a_idx, b_idx = where_of(ids_ref[2 * s + 1])
        add_block(i, a_idx, b_idx, tile_ref[s])
        return carry

    lax.fori_loop(0, cnt_ref[0], one_slot, 0)


def _panel_products(ids, cnt, pos, turned, panel_a, panel_b, extra):
    slots, edge, _ = turned.shape
    blocks, pair, _ = panel_a.shape
    part = pair // 2
    height = 2 * part + (extra.shape[1] if extra is not None else 0)
    smem = pl.BlockSpec(memory_space=pltpu.SMEM)
    vmem = pl.BlockSpec(memory_space=pltpu.VMEM)
    if extra is None:
        extra = jnp.zeros((blocks, 8, edge), jnp.float32)
    flops = slots * 2 * pair * edge * edge * 2
    return pl.pallas_call(
        _tile_kernel,
        in_specs=[smem, smem, smem, vmem, vmem, vmem, vmem],
        out_specs=vmem,
        out_shape=jax.ShapeDtypeStruct((blocks, height, edge), jnp.float32),
        compiler_params=pltpu.CompilerParams(vmem_limit_bytes=56 * 1024 * 1024),
        cost_estimate=pl.CostEstimate(
            flops=flops,
            bytes_accessed=turned.size * 2 + 2 * panel_a.size * 2 + blocks * height * edge * 4,
            transcendentals=0,
        ),
    )(ids, cnt, pos, turned, panel_a, panel_b, extra)


def _ring4(unit, plus, minus):
    from_left = lax.ppermute(unit, "row", plus)
    from_right = lax.ppermute(unit, "row", minus)
    half = unit.shape[-2] // 2
    first = lax.ppermute(from_left[..., :half, :], "row", plus)
    second = lax.ppermute(from_right[..., half:, :], "row", minus)
    across = jnp.concatenate([first, second], axis=-2)
    return jnp.stack([unit, from_right, across, from_left])


def _gather_2d(block, side):
    n = side * side

    def shift(dx, dy):
        return [(r, ((r // side + dy) % side) * side + (r % side + dx) % side) for r in range(n)]

    half = block.shape[0] // 2
    quarter = block.shape[0] // 4
    hi, lo = block[:half], block[half:]
    unit_a = jnp.concatenate([hi[:quarter], lo[:quarter]], axis=0)
    unit_b = jnp.concatenate([hi[quarter:], lo[quarter:]], axis=0)
    by_x = _ring4(unit_a, shift(1, 0), shift(-1, 0))
    by_y = _ring4(unit_b, shift(0, 1), shift(0, -1))
    panel_a = _ring4(by_x, shift(0, 1), shift(0, -1))
    panel_b = _ring4(by_y, shift(1, 0), shift(-1, 0))
    rows, width = unit_a.shape
    return panel_a.reshape(n, rows, width), panel_b.reshape(n, rows, width)


def shards(features, weight, tile_values, tile_ids, tile_counts):
    tile_set = tile_values[0, 0]
    slots, edge, _ = tile_set.shape
    slot_ids = tile_ids[0, 0]
    ids = slot_ids.reshape(-1)
    live_count = tile_counts[0, 0]
    cnt = live_count.reshape(1)
    n_row = lax.axis_size("row")
    side = 4
    r = lax.axis_index("row")
    on_diagonal = (r == lax.axis_index("col")).astype(jnp.int32)
    pos = jnp.stack([r % side, r // side, jnp.int32(side), on_diagonal]).astype(jnp.int32)
    turned_w = lax.dot_general(
        weight, features, (((0,), (1,)), ((), ())), precision=lax.Precision.HIGH
    )
    rounded = lax.reduce_precision(turned_w, exponent_bits=8, mantissa_bits=7)
    hi = rounded.astype(jnp.bfloat16)
    lo = (turned_w - rounded).astype(jnp.bfloat16)
    width = hi.shape[0]
    turned = jnp.swapaxes(tile_set, 1, 2)
    blocks = n_row
    is_live = (jnp.arange(slots) < live_count).astype(jnp.float32)
    placement = (slot_ids[:, 0][:, None] == jnp.arange(blocks)[None, :]).astype(jnp.float32)
    placement = placement * is_live[:, None]
    tile_sums = jnp.sum(tile_set, axis=2, dtype=jnp.float32)
    row_sums = jnp.dot(placement.T, tile_sums, precision=lax.Precision.HIGHEST)
    extra = jnp.zeros((blocks, EXTRA, edge), jnp.float32).at[:, 0, :].set(row_sums)
    chunks = 2
    step = width // chunks
    pieces = []
    degree = None
    for k in range(chunks):
        block = jnp.concatenate([hi[k * step:(k + 1) * step], lo[k * step:(k + 1) * step]], axis=0)
        panel_a, panel_b = _gather_2d(block, side)
        partial = _panel_products(ids, cnt, pos, turned, panel_a, panel_b, extra if k == 0 else None)
        _, height, _ = partial.shape
        mine = lax.psum_scatter(
            partial.reshape(blocks * height, edge), "col", scatter_dimension=0, tiled=True
        )
        if k == 0:
            degree = 1.0 + mine[step]
        pieces.append(mine[:step])
    inverse_root = lax.rsqrt(degree)
    return jnp.maximum(jnp.concatenate(pieces, axis=0).T * inverse_root[:, None], 0.0)


def solution(mesh):
    in_specs = (
        P(("col", "row"), None),
        P(),
        P("row", "col", None, None, None),
        P("row", "col", None, None),
        P("row", "col"),
    )
    out_specs = P(("row", "col"), None)
    return jax.shard_map(shards, mesh=mesh, in_specs=in_specs, out_specs=out_specs, check_vma=False)
```

time: 187 us -> 216 us (1.16)
  waiting for transfers between devices: 144 us -> 93.8 us
  starting transfers between devices: 0.04 us -> 45.1 us
  Pallas kernels: 9.62 us -> 22.3 us
  other arithmetic: 4.73 us -> 16.1 us
  local copies, waits for them, and re-layouts: 11.8 us -> 21.6 us
    unnamed x3, waiting for transfers between devices: 77.3 us -> 4.17 us
    all_gather x1 -> x0, waiting for transfers between devices: 66.5 us -> none  [shards(): panel = lax.all_gather(stacked, 'row', axis=0, tiled=True)]
    reduce_scatter x0 -> x1, waiting for transfers between devices: none -> 61.7 us  [shards(): lax.psum_scatter(partial.reshape(blocks * height, edge), 'col', scatter_d...]
    ppermute x0 -> x32, starting transfers between devices: none -> 45 us  [the longest x8 20.4 us: _ring4(): second = lax.ppermute(from_right[..., half:, :], 'row', minus)]
    ppermute x0 -> x32, waiting for transfers between devices: none -> 27.9 us  [the longest x8 15.8 us: _ring4(): first = lax.ppermute(from_left[..., :half, :], 'row', plus)]
    pallas_call x1 -> x2, Pallas kernels: 9.62 us -> 22.3 us  [_panel_products(): pl.pallas_call(_tile_kernel, in_specs=[smem, smem, smem, vmem, vmem, vmem...]
    another operation x0 -> x21, other arithmetic: none -> 10.6 us  [the longest x20 10 us: _ring4(): return jnp.stack([unit, from_right, across, from_left])]
    reshape x0 -> x1, local copies, waits for them, and re-layouts: none -> 5.67 us  [shards(): partial.reshape(blocks * height, edge)]
  transfers between devices with their start and end apart: 2 -> 34, of which waited for: 2 -> 13; matrix products, arithmetic and copies ran while one was open for 6% -> 14% of each run, Pallas kernels for 0% -> 5%
where the time goes in v7:
time: 216 us
  waiting for transfers between devices  93.8 us (43%)
  starting transfers between devices  45.1 us (21%)
  Pallas kernels  22.3 us (10%)
  local copies, waits for them, and re-layouts  21.6 us (10%)
  other arithmetic  16.1 us (7%)
  between operations  14.4 us (7%)
  matrix products  2.3 us (1%)
    reduce_scatter x1, waiting for transfers between devices, shards(): lax.psum_scatter(partial.reshape(blocks * height, edge), 'col', scatter_d...  61.7 us
    pallas_call x2, Pallas kernels, _panel_products(): pl.pallas_call(_tile_kernel, in_specs=[smem, smem, smem, vmem, vmem, vmem...  22.3 us
    ppermute x8, starting transfers between devices, _ring4(): second = lax.ppermute(from_right[..., half:, :], 'row', minus)  20.4 us
    ppermute x8, starting transfers between devices, _ring4(): from_right = lax.ppermute(unit, 'row', minus)  18 us
    ppermute x8, waiting for transfers between devices, _ring4(): first = lax.ppermute(from_left[..., :half, :], 'row', plus)  15.8 us
    ppermute x8, waiting for transfers between devices, _ring4(): from_right = lax.ppermute(unit, 'row', minus)  11.7 us
    another operation x20, other arithmetic, _ring4(): return jnp.stack([unit, from_right, across, from_left])  10 us
    unnamed x18, local copies, waits for them, and re-layouts  8.81 us
  transfers between devices with their start and end apart: 34, of which 13 were waited for; matrix products, arithmetic and copies ran while one was open for 14% of the time, Pallas kernels for 5%

profile of v7, /device:TPU:2, one launch (start us, length us, event | category | flops | bytes accessed | tf_op | source)
XLA Modules:
  0.0 215.6 jit_solution(14163707303330133999)
XLA Ops:
  10.5 2.3 %collective-permute-start = (bf16[256,256]{1,0:T(8,128)(2,1)S(1)}, bf16[256,256]{1,0:T(8,128)(2,1)S(1)}, u32[]{:S(2)}, u32[]{:S(2)}) collective-permute-start(bf16[256,256]{1,0:T(8,128)(2,1)S(1)} %get-tuple-element.38), channel_id=1, source_target_pairs={{0,48},{16,0},{32,16},{48,32},{64,112},{80,64},{96,80},{112,96},{1... | collective-permute-start | bytes 393224 | tf_op jit(solution)/shard_map/ppermute | solution.py:75
  16.2 6.4 %copy.15 = bf16[1,1,32,256,256]{3,4,2,1,0:T(8,128)(2,1)} copy(bf16[1,1,32,256,256]{4,3,2,1,0:T(8,128)(2,1)} %param.9) | data formatting | bytes 8388608 | tf_op args[2]
  24.9 3.5 %convert_reduce_fusion = f32[32,256]{1,0:T(8,128)} fusion(bf16[1,1,32,256,256]{3,4,2,1,0:T(8,128)(2,1)} %copy.15), kind=kLoop, calls=%fused_computation | loop fusion | flops 4186112 | bytes 4227072 | tf_op jit(solution)/shard_map/reduce_sum | solution.py:126
  32.3 3.1 %collective-permute-start.4 = (bf16[4,256,256]{2,1,0:T(8,128)(2,1)S(1)}, bf16[4,256,256]{2,1,0:T(8,128)(2,1)S(1)}, u32[]{:S(2)}, u32[]{:S(2)}) collective-permute-start(bf16[4,256,256]{2,1,0:T(8,128)(2,1)S(1)} %get-tuple-element.20), channel_id=1, source_target_pairs={{0,192},{16,208},{32,224},{48,240},{64,0},{80,16},{96,32},{112,48}... | collective-permute-start | bytes 1572872 | tf_op jit(solution)/shard_map/ppermute | solution.py:75
  35.4 2.3 %collective-permute-done.10 = bf16[128,256]{1,0:T(8,128)(2,1)S(1)} collective-permute-done((bf16[128,256]{1,0:T(8,128)(2,1)S(1)}, bf16[128,256]{1,0:T(8,128)(2,1)S(1)}, u32[]{:S(2)}, u32[]{:S(2)}) %collective-permute-start.10) | collective-permute-done | bytes 65568 | tf_op jit(solution)/shard_map/ppermute | solution.py:77
  41.1 3.3 %collective-permute-done.4 = bf16[4,256,256]{2,1,0:T(8,128)(2,1)S(1)} collective-permute-done((bf16[4,256,256]{2,1,0:T(8,128)(2,1)S(1)}, bf16[4,256,256]{2,1,0:T(8,128)(2,1)S(1)}, u32[]{:S(2)}, u32[]{:S(2)}) %collective-permute-start.4) | collective-permute-done | bytes 524320 | tf_op jit(solution)/shard_map/ppermute | solution.py:75
  44.4 4.0 %collective-permute-start.7 = (bf16[4,128,256]{2,1,0:T(8,128)(2,1)S(1)}, bf16[4,128,256]{2,1,0:T(8,128)(2,1)}, u32[]{:S(2)}, u32[]{:S(2)}) collective-permute-start(bf16[4,128,256]{2,1,0:T(8,128)(2,1)S(1)} %slice.144), channel_id=1, source_target_pairs={{0,192},{16,208},{32,224},{48,240},{64,0},{80,16},{96,32},{112,48}... | collective-permute-start | bytes 786440 | tf_op jit(solution)/shard_map/ppermute | solution.py:78
  59.7 3.2 %collective-permute-done.14 = bf16[4,128,256]{2,1,0:T(8,128)(2,1)S(1)} collective-permute-done((bf16[4,128,256]{2,1,0:T(8,128)(2,1)S(1)}, bf16[4,128,256]{2,1,0:T(8,128)(2,1)S(1)}, u32[]{:S(2)}, u32[]{:S(2)}) %collective-permute-start.14) | collective-permute-done | bytes 262176 | tf_op jit(solution)/shard_map/ppermute | solution.py:77
  62.9 2.9 %pad_maximum_fusion.1 = bf16[4,4,256,256]{3,2,1,0:T(8,128)(2,1)} fusion(bf16[1,4,256,256]{3,2,1,0:T(8,128)(2,1)} %bitcast.22, bf16[1,4,256,256]{3,2,1,0:T(8,128)(2,1)S(1)} %maximum_bitcast_fusion.1, bf16[1,4,256,256]{3,2,1,0:T(8,128)(2,1)} %bitcast.20, bf16[1,4,256,256]{3,2,1,0:T(8,128)(2,1)S(1)} %get-tuple-element.17), kind=kLoop, calls=%fused_computation.2 | loop fusion | flops 3145728 | bytes 4194304 | tf_op jit(solution)/shard_map/stack | solution.py:80
  65.8 11.1 %shard_map.55 = f32[16,264,256]{2,1,0:T(8,128)} custom-call(s32[64]{0:T(128)} %reshape_squeeze.6.ids_ref, s32[1]{0:T(128)} %bitcast.74.cnt_ref, s32[4]{0:T(128)} %pad_add_fusion.pos_ref, bf16[32,256,256]{2,1,0:T(8,128)(2,1)} %bitcast.77, bf16[16,256,256]{2,1,0:T(8,128)(2,1)} %bitcast.83, bf16[16,256,256]{2,1,0:T(8,128)(2,1)} %bitcast.84, ...), custom_call_target="tpu_custom_call" | custom-call | flops 2147483648 | bytes 12713984 | tf_op jit(solution)/shard_map/pallas_call | solution.py:59
  83.1 2.5 %collective-permute-start.19 = (bf16[128,256]{1,0:T(8,128)(2,1)S(1)}, bf16[128,256]{1,0:T(8,128)(2,1)S(1)}, u32[]{:S(2)}, u32[]{:S(2)}) collective-permute-start(bf16[128,256]{1,0:T(8,128)(2,1)S(1)} %slice.155), channel_id=1, source_target_pairs={{0,48},{16,0},{32,16},{48,32},{64,112},{80,64},{96,80},{112,96},{1... | collective-permute-start | bytes 196616 | tf_op jit(solution)/shard_map/ppermute | solution.py:78
  85.7 2.1 collective-permute-start.27
  87.9 3.6 %collective-permute-done.18 = bf16[128,256]{1,0:T(8,128)(2,1)S(1)} collective-permute-done((bf16[128,256]{1,0:T(8,128)(2,1)S(1)}, bf16[128,256]{1,0:T(8,128)(2,1)S(1)}, u32[]{:S(2)}, u32[]{:S(2)}) %collective-permute-start.18) | collective-permute-done | bytes 65568 | tf_op jit(solution)/shard_map/ppermute | solution.py:77
  91.8 3.2 %collective-permute-start.20 = (bf16[4,256,256]{2,1,0:T(8,128)(2,1)S(1)}, bf16[4,256,256]{2,1,0:T(8,128)(2,1)S(1)}, u32[]{:S(2)}, u32[]{:S(2)}) collective-permute-start(bf16[4,256,256]{2,1,0:T(8,128)(2,1)S(1)} %get-tuple-element.24), channel_id=1, source_target_pairs={{0,192},{16,208},{32,224},{48,240},{64,0},{80,16},{96,32},{112,48}... | collective-permute-start | bytes 1572872 | tf_op jit(solution)/shard_map/ppermute | solution.py:75
  95.1 3.5 %collective-permute-start.28 = (bf16[4,256,256]{2,1,0:T(8,128)(2,1)S(1)}, bf16[4,256,256]{2,1,0:T(8,128)(2,1)S(1)}, u32[]{:S(2)}, u32[]{:S(2)}) collective-permute-start(bf16[4,256,256]{2,1,0:T(8,128)(2,1)S(1)} %get-tuple-element.22), channel_id=1, source_target_pairs={{0,48},{16,0},{32,16},{48,32},{64,112},{80,64},{96,80},{112,96},{1... | collective-permute-start | bytes 1572872 | tf_op jit(solution)/shard_map/ppermute | solution.py:75
  98.6 5.9 %collective-permute-done.20 = bf16[4,256,256]{2,1,0:T(8,128)(2,1)S(1)} collective-permute-done((bf16[4,256,256]{2,1,0:T(8,128)(2,1)S(1)}, bf16[4,256,256]{2,1,0:T(8,128)(2,1)S(1)}, u32[]{:S(2)}, u32[]{:S(2)}) %collective-permute-start.20) | collective-permute-done | bytes 524320 | tf_op jit(solution)/shard_map/ppermute | solution.py:75
  104.5 3.8 %collective-permute-start.23 = (bf16[4,128,256]{2,1,0:T(8,128)(2,1)S(1)}, bf16[4,128,256]{2,1,0:T(8,128)(2,1)S(1)}, u32[]{:S(2)}, u32[]{:S(2)}) collective-permute-start(bf16[4,128,256]{2,1,0:T(8,128)(2,1)S(1)} %slice.157), channel_id=1, source_target_pairs={{0,192},{16,208},{32,224},{48,240},{64,0},{80,16},{96,32},{112,48}... | collective-permute-start | bytes 786440 | tf_op jit(solution)/shard_map/ppermute | solution.py:78
  108.4 3.3 %collective-permute-start.31 = (bf16[4,128,256]{2,1,0:T(8,128)(2,1)S(1)}, bf16[4,128,256]{2,1,0:T(8,128)(2,1)S(1)}, u32[]{:S(2)}, u32[]{:S(2)}) collective-permute-start(bf16[4,128,256]{2,1,0:T(8,128)(2,1)S(1)} %slice.163), channel_id=1, source_target_pairs={{0,48},{16,0},{32,16},{48,32},{64,112},{80,64},{96,80},{112,96},{1... | collective-permute-start | bytes 786440 | tf_op jit(solution)/shard_map/ppermute | solution.py:78
  112.2 3.8 %collective-permute-done.22 = bf16[4,128,256]{2,1,0:T(8,128)(2,1)S(1)} collective-permute-done((bf16[4,128,256]{2,1,0:T(8,128)(2,1)S(1)}, bf16[4,128,256]{2,1,0:T(8,128)(2,1)S(1)}, u32[]{:S(2)}, u32[]{:S(2)}) %collective-permute-start.22) | collective-permute-done | bytes 262176 | tf_op jit(solution)/shard_map/ppermute | solution.py:77
  116.0 2.2 %collective-permute-done.30 = bf16[4,128,256]{2,1,0:T(8,128)(2,1)S(1)} collective-permute-done((bf16[4,128,256]{2,1,0:T(8,128)(2,1)S(1)}, bf16[4,128,256]{2,1,0:T(8,128)(2,1)S(1)}, u32[]{:S(2)}, u32[]{:S(2)}) %collective-permute-start.30) | collective-permute-done | bytes 262176 | tf_op jit(solution)/shard_map/ppermute | solution.py:77
  122.0 11.2 %shard_map.56 = f32[16,256,256]{2,1,0:T(8,128)} custom-call(s32[64]{0:T(128)} %reshape_squeeze.6.ids_ref, s32[1]{0:T(128)} %bitcast.75.cnt_ref, s32[4]{0:T(128)} %pad_add_fusion.pos_ref, bf16[32,256,256]{2,1,0:T(8,128)(2,1)} %bitcast.78, bf16[16,256,256]{2,1,0:T(8,128)(2,1)} %bitcast.81, bf16[16,256,256]{2,1,0:T(8,128)(2,1)} %bitcast.82, ...), custom_call_target="tpu_custom_call" | custom-call | flops 2147483648 | bytes 12582912 | tf_op jit(solution)/shard_map/pallas_call | solution.py:59
  133.2 5.7 %copy.17 = f32[4096,256]{0,1:T(8,128)} copy(f32[4096,256]{1,0:T(8,128)} %bitcast.80) | data formatting | bytes 8388608 | tf_op jit(solution)/shard_map/reshape | solution.py:139
  138.9 4.1 %reduce-scatter.7.cloned.1.call-done = f32[264,256]{1,0:T(8,128)} async-done(((f32[4224,256]{1,0:T(8,128)}), f32[264,256]{1,0:T(8,128)}) %reduce-scatter.7.cloned.1.call-update) | async-done | bytes 270352
  145.1 61.7 %reduce-scatter.5.cloned.1.call-done = f32[256,256]{0,1:T(8,128)} async-done(((f32[4096,256]{0,1:T(8,128)}), f32[256,256]{0,1:T(8,128)}) %reduce-scatter.5.cloned.1.call-update) | async-done | bytes 262160 | tf_op jit(solution)/shard_map/reduce_scatter | solution.py:138
  (118 shorter events, 42.4 us)
Async XLA Ops:
  6.5 136.5 %reduce-scatter.7.cloned.1.call-start = ((), (), s32[]{:S(2)}) async-start(), calls=%async_computation.3 | async-start | bytes 4595712
  10.5 12.1 %collective-permute-start = (bf16[256,256]{1,0:T(8,128)(2,1)S(1)}, bf16[256,256]{1,0:T(8,128)(2,1)S(1)}, u32[]{:S(2)}, u32[]{:S(2)}) collective-permute-start(bf16[256,256]{1,0:T(8,128)(2,1)S(1)} %get-tuple-element.38), channel_id=1, source_target_pairs={{0,48},{16,0},{32,16},{48,32},{64,112},{80,64},{96,80},{112,96},{1... | collective-permute-start | bytes 393224 | tf_op jit(solution)/shard_map/ppermute | solution.py:75
  12.9 11.9 %collective-permute-start.1 = (bf16[256,256]{1,0:T(8,128)(2,1)S(1)}, bf16[256,256]{1,0:T(8,128)(2,1)S(1)}, u32[]{:S(2)}, u32[]{:S(2)}) collective-permute-start(bf16[256,256]{1,0:T(8,128)(2,1)S(1)} %get-tuple-element.38), channel_id=1, source_target_pairs={{0,16},{16,32},{32,48},{48,0},{64,80},{80,96},{96,112},{112,64},{1... | collective-permute-start | bytes 393224 | tf_op jit(solution)/shard_map/ppermute | solution.py:74
  12.9 18.5 %collective-permute-start.9 = (bf16[256,256]{1,0:T(8,128)(2,1)S(1)}, bf16[256,256]{1,0:T(8,128)(2,1)S(1)}, u32[]{:S(2)}, u32[]{:S(2)}) collective-permute-start(bf16[256,256]{1,0:T(8,128)(2,1)S(1)} %get-tuple-element.36), channel_id=1, source_target_pairs={{0,64},{16,80},{32,96},{48,112},{64,128},{80,144},{96,160},{112,17... | collective-permute-start | bytes 393224 | tf_op jit(solution)/shard_map/ppermute | solution.py:74
  14.3 15.4 %collective-permute-start.8 = (bf16[256,256]{1,0:T(8,128)(2,1)S(1)}, bf16[256,256]{1,0:T(8,128)(2,1)S(1)}, u32[]{:S(2)}, u32[]{:S(2)}) collective-permute-start(bf16[256,256]{1,0:T(8,128)(2,1)S(1)} %get-tuple-element.36), channel_id=1, source_target_pairs={{0,192},{16,208},{32,224},{48,240},{64,0},{80,16},{96,32},{112,48}... | collective-permute-start | bytes 393224 | tf_op jit(solution)/shard_map/ppermute | solution.py:75
  22.7 9.3 %collective-permute-start.3 = (bf16[128,256]{1,0:T(8,128)(2,1)S(1)}, bf16[128,256]{1,0:T(8,128)(2,1)S(1)}, u32[]{:S(2)}, u32[]{:S(2)}) collective-permute-start(bf16[128,256]{1,0:T(8,128)(2,1)S(1)} %slice.142), channel_id=1, source_target_pairs={{0,48},{16,0},{32,16},{48,32},{64,112},{80,64},{96,80},{112,96},{1... | collective-permute-start | bytes 196616 | tf_op jit(solution)/shard_map/ppermute | solution.py:78
  32.1 16.3 %collective-permute-start.5 = (bf16[4,256,256]{2,1,0:T(8,128)(2,1)S(1)}, bf16[4,256,256]{2,1,0:T(8,128)(2,1)S(1)}, u32[]{:S(2)}, u32[]{:S(2)}) collective-permute-start(bf16[4,256,256]{2,1,0:T(8,128)(2,1)S(1)} %get-tuple-element.20), channel_id=1, source_target_pairs={{0,64},{16,80},{32,96},{48,112},{64,128},{80,144},{96,160},{112,17... | collective-permute-start | bytes 1572872 | tf_op jit(solution)/shard_map/ppermute | solution.py:74
  32.3 12.1 %collective-permute-start.4 = (bf16[4,256,256]{2,1,0:T(8,128)(2,1)S(1)}, bf16[4,256,256]{2,1,0:T(8,128)(2,1)S(1)}, u32[]{:S(2)}, u32[]{:S(2)}) collective-permute-start(bf16[4,256,256]{2,1,0:T(8,128)(2,1)S(1)} %get-tuple-element.20), channel_id=1, source_target_pairs={{0,192},{16,208},{32,224},{48,240},{64,0},{80,16},{96,32},{112,48}... | collective-permute-start | bytes 1572872 | tf_op jit(solution)/shard_map/ppermute | solution.py:75
  38.6 15.7 %collective-permute-start.13 = (bf16[4,256,256]{2,1,0:T(8,128)(2,1)}, bf16[4,256,256]{2,1,0:T(8,128)(2,1)}, u32[]{:S(2)}, u32[]{:S(2)}) collective-permute-start(bf16[4,256,256]{2,1,0:T(8,128)(2,1)} %get-tuple-element.18), channel_id=1, source_target_pairs={{0,16},{16,32},{32,48},{48,0},{64,80},{80,96},{96,112},{112,64},{1... | collective-permute-start | bytes 1572872 | tf_op jit(solution)/shard_map/ppermute | solution.py:74
  40.5 11.7 %collective-permute-start.12 = (bf16[4,256,256]{2,1,0:T(8,128)(2,1)}, bf16[4,256,256]{2,1,0:T(8,128)(2,1)}, u32[]{:S(2)}, u32[]{:S(2)}) collective-permute-start(bf16[4,256,256]{2,1,0:T(8,128)(2,1)} %get-tuple-element.18), channel_id=1, source_target_pairs={{0,48},{16,0},{32,16},{48,32},{64,112},{80,64},{96,80},{112,96},{1... | collective-permute-start | bytes 1572872 | tf_op jit(solution)/shard_map/ppermute | solution.py:75
  44.4 12.0 %collective-permute-start.7 = (bf16[4,128,256]{2,1,0:T(8,128)(2,1)S(1)}, bf16[4,128,256]{2,1,0:T(8,128)(2,1)}, u32[]{:S(2)}, u32[]{:S(2)}) collective-permute-start(bf16[4,128,256]{2,1,0:T(8,128)(2,1)S(1)} %slice.144), channel_id=1, source_target_pairs={{0,192},{16,208},{32,224},{48,240},{64,0},{80,16},{96,32},{112,48}... | collective-permute-start | bytes 786440 | tf_op jit(solution)/shard_map/ppermute | solution.py:78
  49.1 7.9 %collective-permute-start.6 = (bf16[4,128,256]{2,1,0:T(8,128)(2,1)}, bf16[4,128,256]{2,1,0:T(8,128)(2,1)}, u32[]{:S(2)}, u32[]{:S(2)}) collective-permute-start(bf16[4,128,256]{2,1,0:T(8,128)(2,1)} %slice.143), channel_id=1, source_target_pairs={{0,64},{16,80},{32,96},{48,112},{64,128},{80,144},{96,160},{112,17... | collective-permute-start | bytes 786440 | tf_op jit(solution)/shard_map/ppermute | solution.py:77
  55.3 7.7 %collective-permute-start.14 = (bf16[4,128,256]{2,1,0:T(8,128)(2,1)S(1)}, bf16[4,128,256]{2,1,0:T(8,128)(2,1)S(1)}, u32[]{:S(2)}, u32[]{:S(2)}) collective-permute-start(bf16[4,128,256]{2,1,0:T(8,128)(2,1)S(1)} %slice.149), channel_id=1, source_target_pairs={{0,16},{16,32},{32,48},{48,0},{64,80},{80,96},{96,112},{112,64},{1... | collective-permute-start | bytes 786440 | tf_op jit(solution)/shard_map/ppermute | solution.py:77
  76.9 129.9 %reduce-scatter.5.cloned.1.call-start = ((), (), s32[]{:S(2)}) async-start(), calls=%async_computation.2 | async-start | bytes 4456448 | tf_op jit(solution)/shard_map/reduce_scatter | solution.py:138
  77.8 7.8 %collective-permute-start.17 = (bf16[256,256]{1,0:T(8,128)(2,1)S(1)}, bf16[256,256]{1,0:T(8,128)(2,1)S(1)}, u32[]{:S(2)}, u32[]{:S(2)}) collective-permute-start(bf16[256,256]{1,0:T(8,128)(2,1)S(1)} %get-tuple-element.42), channel_id=1, source_target_pairs={{0,16},{16,32},{32,48},{48,0},{64,80},{80,96},{96,112},{112,64},{1... | collective-permute-start | bytes 393224 | tf_op jit(solution)/shard_map/ppermute | solution.py:74
  85.7 9.3 %collective-permute-start.27 = (bf16[128,256]{1,0:T(8,128)(2,1)S(1)}, bf16[128,256]{1,0:T(8,128)(2,1)S(1)}, u32[]{:S(2)}, u32[]{:S(2)}) collective-permute-start(bf16[128,256]{1,0:T(8,128)(2,1)S(1)} %slice.161), channel_id=1, source_target_pairs={{0,192},{16,208},{32,224},{48,240},{64,0},{80,16},{96,32},{112,48}... | collective-permute-start | bytes 196616 | tf_op jit(solution)/shard_map/ppermute | solution.py:78
  87.8 7.2 %collective-permute-start.26 = (bf16[128,256]{1,0:T(8,128)(2,1)S(1)}, bf16[128,256]{1,0:T(8,128)(2,1)S(1)}, u32[]{:S(2)}, u32[]{:S(2)}) collective-permute-start(bf16[128,256]{1,0:T(8,128)(2,1)S(1)} %slice.160), channel_id=1, source_target_pairs={{0,64},{16,80},{32,96},{48,112},{64,128},{80,144},{96,160},{112,17... | collective-permute-start | bytes 196616 | tf_op jit(solution)/shard_map/ppermute | solution.py:77
  91.7 16.6 %collective-permute-start.21 = (bf16[4,256,256]{2,1,0:T(8,128)(2,1)S(1)}, bf16[4,256,256]{2,1,0:T(8,128)(2,1)S(1)}, u32[]{:S(2)}, u32[]{:S(2)}) collective-permute-start(bf16[4,256,256]{2,1,0:T(8,128)(2,1)S(1)} %get-tuple-element.24), channel_id=1, source_target_pairs={{0,64},{16,80},{32,96},{48,112},{64,128},{80,144},{96,160},{112,17... | collective-permute-start | bytes 1572872 | tf_op jit(solution)/shard_map/ppermute | solution.py:74
  91.8 12.7 %collective-permute-start.20 = (bf16[4,256,256]{2,1,0:T(8,128)(2,1)S(1)}, bf16[4,256,256]{2,1,0:T(8,128)(2,1)S(1)}, u32[]{:S(2)}, u32[]{:S(2)}) collective-permute-start(bf16[4,256,256]{2,1,0:T(8,128)(2,1)S(1)} %get-tuple-element.24), channel_id=1, source_target_pairs={{0,192},{16,208},{32,224},{48,240},{64,0},{80,16},{96,32},{112,48}... | collective-permute-start | bytes 1572872 | tf_op jit(solution)/shard_map/ppermute | solution.py:75
  95.1 13.3 %collective-permute-start.28 = (bf16[4,256,256]{2,1,0:T(8,128)(2,1)S(1)}, bf16[4,256,256]{2,1,0:T(8,128)(2,1)S(1)}, u32[]{:S(2)}, u32[]{:S(2)}) collective-permute-start(bf16[4,256,256]{2,1,0:T(8,128)(2,1)S(1)} %get-tuple-element.22), channel_id=1, source_target_pairs={{0,48},{16,0},{32,16},{48,32},{64,112},{80,64},{96,80},{112,96},{1... | collective-permute-start | bytes 1572872 | tf_op jit(solution)/shard_map/ppermute | solution.py:75
  98.6 13.1 %collective-permute-start.29 = (bf16[4,256,256]{2,1,0:T(8,128)(2,1)S(1)}, bf16[4,256,256]{2,1,0:T(8,128)(2,1)S(1)}, u32[]{:S(2)}, u32[]{:S(2)}) collective-permute-start(bf16[4,256,256]{2,1,0:T(8,128)(2,1)S(1)} %get-tuple-element.22), channel_id=1, source_target_pairs={{0,16},{16,32},{32,48},{48,0},{64,80},{80,96},{96,112},{112,64},{1... | collective-permute-start | bytes 1572872 | tf_op jit(solution)/shard_map/ppermute | solution.py:74
  104.5 7.6 %collective-permute-start.23 = (bf16[4,128,256]{2,1,0:T(8,128)(2,1)S(1)}, bf16[4,128,256]{2,1,0:T(8,128)(2,1)S(1)}, u32[]{:S(2)}, u32[]{:S(2)}) collective-permute-start(bf16[4,128,256]{2,1,0:T(8,128)(2,1)S(1)} %slice.157), channel_id=1, source_target_pairs={{0,192},{16,208},{32,224},{48,240},{64,0},{80,16},{96,32},{112,48}... | collective-permute-start | bytes 786440 | tf_op jit(solution)/shard_map/ppermute | solution.py:78
  108.3 7.7 %collective-permute-start.22 = (bf16[4,128,256]{2,1,0:T(8,128)(2,1)S(1)}, bf16[4,128,256]{2,1,0:T(8,128)(2,1)S(1)}, u32[]{:S(2)}, u32[]{:S(2)}) collective-permute-start(bf16[4,128,256]{2,1,0:T(8,128)(2,1)S(1)} %slice.156), channel_id=1, source_target_pairs={{0,64},{16,80},{32,96},{48,112},{64,128},{80,144},{96,160},{112,17... | collective-permute-start | bytes 786440 | tf_op jit(solution)/shard_map/ppermute | solution.py:77
  108.4 7.6 %collective-permute-start.31 = (bf16[4,128,256]{2,1,0:T(8,128)(2,1)S(1)}, bf16[4,128,256]{2,1,0:T(8,128)(2,1)S(1)}, u32[]{:S(2)}, u32[]{:S(2)}) collective-permute-start(bf16[4,128,256]{2,1,0:T(8,128)(2,1)S(1)} %slice.163), channel_id=1, source_target_pairs={{0,48},{16,0},{32,16},{48,32},{64,112},{80,64},{96,80},{112,96},{1... | collective-permute-start | bytes 786440 | tf_op jit(solution)/shard_map/ppermute | solution.py:78
  (17 other events, 90.1 us)
Sparse Core Ops, SparseCore 0:
  77.0 65.9 reduce-scatter.6
  145.6 61.2 reduce-scatter.4

commit v8 on v6

--- a/solution.py
+++ b/solution.py
@@ -6,6 +6,10 @@
 from jax.sharding import PartitionSpec as P
 
 EXTRA = 8
+
+
+def _slot_of(block, blocks):
+    return (block % 2) * (blocks // 2) + block // 2
 
 
 def _tile_kernel(ids_ref, cnt_ref, flag_ref, tile_ref, x_ref, extra_ref, out_ref):
@@ -17,7 +21,7 @@
     def _diagonal():
         for b in range(blocks):
             own = x_ref[b, :width, :].astype(jnp.float32) + x_ref[b, width:, :].astype(jnp.float32)
-            out_ref[b, :width, :] = own
+            out_ref[_slot_of(b, blocks), :width, :] = own
 
     @pl.when(flag_ref[0] == 0)
     def _elsewhere():
@@ -59,10 +63,13 @@
     tile_set = tile_values[0, 0]
     slots, edge, _ = tile_set.shape
     slot_ids = tile_ids[0, 0]
-    ids = slot_ids.reshape(-1)
+    blocks = lax.axis_size("row")
+    stored = jnp.stack([_slot_of(slot_ids[:, 0], blocks), slot_ids[:, 1]], axis=1)
+    ids = stored.reshape(-1)
     live_count = tile_counts[0, 0]
     cnt = live_count.reshape(1)
-    flag = (lax.axis_index("row") == lax.axis_index("col")).astype(jnp.int32).reshape(1)
+    col = lax.axis_index("z") * lax.axis_size("core") + lax.axis_index("core")
+    flag = (lax.axis_index("row") == col).astype(jnp.int32).reshape(1)
     turned_w = lax.dot_general(
         weight, features, (((0,), (1,)), ((), ())), precision=lax.Precision.HIGH
     )
@@ -71,7 +78,7 @@
     lo = (turned_w - rounded).astype(jnp.bfloat16)
     stacked = jnp.concatenate([hi, lo], axis=0)[None]
     panel = lax.all_gather(stacked, "row", axis=0, tiled=True)
-    blocks, pair, _ = panel.shape
+    _, pair, _ = panel.shape
     width = pair // 2
     turned = jnp.swapaxes(tile_set, 1, 2)
     is_live = (jnp.arange(slots) < live_count).astype(jnp.float32)
@@ -79,24 +86,29 @@
     placement = placement * is_live[:, None]
     tile_sums = jnp.sum(tile_set, axis=2, dtype=jnp.float32)
     row_sums = jnp.dot(placement.T, tile_sums, precision=lax.Precision.HIGHEST)
-    extra = jnp.zeros((blocks, EXTRA, edge), jnp.float32).at[:, 0, :].set(row_sums)
+    order = _slot_of(jnp.arange(blocks), blocks)
+    extra = jnp.zeros((blocks, EXTRA, edge), jnp.float32).at[order, 0, :].set(row_sums)
     partial = _panel_products(ids, cnt, flag, turned, panel, extra)
     _, height, _ = partial.shape
-    mine = lax.psum_scatter(
-        partial.reshape(blocks * height, edge), "col", scatter_dimension=0, tiled=True
+    half = lax.psum_scatter(
+        partial.reshape(blocks * height, edge), "core", scatter_dimension=0, tiled=True
     )
+    mine = lax.psum_scatter(half, "z", scatter_dimension=0, tiled=True)
     degree = 1.0 + mine[width]
     inverse_root = lax.rsqrt(degree)
     return jnp.maximum(mine[:width].T * inverse_root[:, None], 0.0)
 
 
 def solution(mesh):
+    rows, cols = mesh.devices.shape
+    mesh = jax.sharding.Mesh(mesh.devices.reshape(rows, cols // 2, 2), ("row", "z", "core"))
+    col = ("z", "core")
     in_specs = (
-        P(("col", "row"), None),
+        P((*col, "row"), None),
         P(),
-        P("row", "col", None, None, None),
-        P("row", "col", None, None),
-        P("row", "col"),
+        P("row", col, None, None, None),
+        P("row", col, None, None),
+        P("row", col),
     )
-    out_specs = P(("row", "col"), None)
+    out_specs = P(("row", *col), None)
     return jax.shard_map(shards, mesh=mesh, in_specs=in_specs, out_specs=out_specs, check_vma=False)

time: 187 us -> 200 us (1.070)
  waiting for transfers between devices: 144 us -> 156 us
    unnamed x3 -> x5, waiting for transfers between devices: 77.3 us -> 90.3 us
    unnamed x8 -> x7, local copies, waits for them, and re-layouts: 8.76 us -> 7.96 us
  transfers between devices with their start and end apart: 2 -> 3, of which waited for: 2 -> 3; matrix products, arithmetic and copies ran while one was open for 6% -> 6% of each run, Pallas kernels for 0% -> 0%
where the time goes in v8:
time: 200 us; the launch traced here: 199 us
  waiting for transfers between devices  156 us (78%)
  between operations  13.8 us (7%)
  local copies, waits for them, and re-layouts  11.9 us (6%)
  Pallas kernels  9.61 us (5%)
  other arithmetic  5.52 us (3%)
  matrix products  2.3 us (1%)
    unnamed x5, waiting for transfers between devices  90.3 us
    all_gather x1, waiting for transfers between devices, shards(): panel = lax.all_gather(stacked, 'row', axis=0, tiled=True)  65.8 us
    pallas_call x1, Pallas kernels, _panel_products(): pl.pallas_call(_tile_kernel, in_specs=[smem, smem, smem, vmem, vmem, vmem...  9.61 us
    unnamed x7, local copies, waits for them, and re-layouts  7.96 us
  transfers between devices with their start and end apart: 3, of which 3 were waited for; matrix products, arithmetic and copies ran while one was open for 6% of the time, Pallas kernels for 0%

profile of v8, /device:TPU:2, one launch (start us, length us, event | category | flops | bytes accessed | tf_op | source)
XLA Modules:
  0.0 199.3 jit_solution(14823708060803823362)
XLA Ops:
  6.5 1.2 copy-done
  7.8 2.0 %reduce-precision_convert_fusion = (bf16[512,256]{1,0:T(8,128)(2,1)S(1)}, bf16[512,256]{1,0:T(8,128)(2,1)S(1)}) fusion(f32[512,512]{1,0:T(8,128)S(1)} %copy-done, f32[256,512]{1,0:T(8,128)} %param.5), kind=kOutput, calls=%fused_computation.3 | convolution fusion | flops 403177472 | bytes 2097152 | tf_op jit(solution)/shard_map/dot_general | solution.py:73
  9.8 0.8 pad_maximum_fusion
  10.6 0.0 all-gather.3.cloned.1.call-update
  10.7 0.0 reduce-scatter.7.cloned.1.call-start
  11.4 0.8 slice_bitcast_fusion
  12.1 0.1 copy.12
  12.2 0.7 reshape.89.ids_ref
  12.9 6.4 %copy.13 = bf16[1,1,32,256,256]{3,4,2,1,0:T(8,128)(2,1)} copy(bf16[1,1,32,256,256]{4,3,2,1,0:T(8,128)(2,1)} %param.7) | data formatting | bytes 8388608 | tf_op args[2]
  19.4 2.9 %convert_reduce_fusion = f32[32,256]{1,0:T(8,128)S(1)} fusion(bf16[1,1,32,256,256]{3,4,2,1,0:T(8,128)(2,1)} %copy.13), kind=kLoop, calls=%fused_computation.1 | loop fusion | flops 4186112 | bytes 4227072 | tf_op jit(solution)/shard_map/reduce_sum | solution.py:87
  22.2 0.3 fusion.1
  22.5 1.3 scatter_fusion
  23.9 65.8 %all-gather.3.cloned.1.call-done = bf16[16384,256]{1,0:T(8,128)(2,1)} async-done(((bf16[1024,256]{1,0:T(8,128)(2,1)}), bf16[16384,256]{1,0:T(8,128)(2,1)}) %all-gather.3.cloned.1.call-update) | async-done | bytes 8388624 | tf_op jit(solution)/shard_map/all_gather | solution.py:80
  89.6 9.6 %shard_map.55 = f32[16,520,256]{2,1,0:T(8,128)} custom-call(s32[64]{0:T(128)} %reshape.89.ids_ref, s32[1]{0:T(128)} %bitcast.21.cnt_ref, s32[1]{0:T(128)} %bitcast.2.flag_ref, bf16[32,256,256]{2,1,0:T(8,128)(2,1)} %bitcast.24, bf16[16,1024,256]{2,1,0:T(8,128)(2,1)} %bitcast.26, f32[16,8,256]{2,1,0:T(8,128)} %copy-done.1), custom_call_target="tpu_custom_call" | custom-call | flops 4294967296 | bytes 21102592 | tf_op jit(solution)/shard_map/pallas_call | solution.py:48
  99.3 0.0 reduce-scatter.9.cloned.1.call-start
  99.3 30.3 %reduce-scatter.7.cloned.1.call-done = f32[4160,256]{1,0:T(8,128)} async-done(((f32[8320,256]{1,0:T(8,128)}), f32[4160,256]{1,0:T(8,128)}) %reduce-scatter.7.cloned.1.call-update) | async-done | bytes 4259856
  129.7 0.0 reduce-scatter.9.cloned.1.call-update
  129.7 59.9 %reduce-scatter.9.cloned.1.call-done = f32[520,256]{1,0:T(8,128)} async-done(((f32[4160,256]{1,0:T(8,128)}), f32[520,256]{1,0:T(8,128)}) %reduce-scatter.9.cloned.1.call-update) | async-done | bytes 532496
  189.6 1.1 slice.19
  190.7 0.2 copy.19
  190.9 0.7 slice.20
  191.6 0.1 copy.20
  191.8 0.1 rsqrt_reduce_fusion
  191.9 0.9 maximum_bitcast_fusion
  (9 shorter events, 0.1 us)
Async XLA Ops:
  6.5 1.2 copy-start
  6.5 83.1 %all-gather.3.cloned.1.call-start = ((), (), s32[]{:S(2)}) async-start(), calls=%async_computation.2 | async-start | bytes 8912896 | tf_op jit(solution)/shard_map/all_gather | solution.py:80
  10.7 119.0 %reduce-scatter.7.cloned.1.call-start = ((), (), s32[]{:S(2)}) async-start(), calls=%async_computation.3 | async-start | bytes 12779520
  23.9 65.8 %copy-start.1 = (f32[16,8,256]{2,1,0:T(8,128)}, f32[16,8,256]{2,1,0:T(8,128)S(1)}, u32[]{:S(2)}) copy-start(f32[16,8,256]{2,1,0:T(8,128)S(1)} %scatter_fusion) | copy-start | bytes 393220
  99.3 90.4 %reduce-scatter.9.cloned.1.call-start = ((), (), s32[]{:S(2)}) async-start(), calls=%async_computation.4 | async-start | bytes 4792320
Sparse Core Ops, SparseCore 0:
  10.8 78.8 all-gather.2
  99.4 30.2 reduce-scatter.6
  132.4 57.1 reduce-scatter.8

commit v9 on v6

--- a/solution.py
+++ b/solution.py
@@ -8,15 +8,30 @@
 EXTRA = 8
 
 
-def _tile_kernel(ids_ref, cnt_ref, flag_ref, tile_ref, x_ref, extra_ref, out_ref):
+def _tile_kernel(ids_ref, cnt_ref, flag_ref, tile_hbm, x_hbm, extra_ref, out_ref,
+                 own_ref, tbuf, xbuf, tsem, xsem, own_sem):
     blocks, height, edge = out_ref.shape
-    width = x_ref.shape[1] // 2
+    width = x_hbm.shape[1] // 2
+    count = cnt_ref[0]
+
+    def copies(s, slot):
+        j = ids_ref[2 * s + 1]
+        return (
+            pltpu.make_async_copy(tile_hbm.at[s], tbuf.at[slot], tsem.at[slot]),
+            pltpu.make_async_copy(x_hbm.at[j], xbuf.at[slot], xsem.at[slot]),
+        )
+
+    for c in copies(0, 0):
+        c.start()
     out_ref[:, width:, :] = extra_ref[...]
 
     @pl.when(flag_ref[0] != 0)
     def _diagonal():
+        whole = pltpu.make_async_copy(x_hbm, own_ref, own_sem)
+        whole.start()
+        whole.wait()
         for b in range(blocks):
-            own = x_ref[b, :width, :].astype(jnp.float32) + x_ref[b, width:, :].astype(jnp.float32)
+            own = own_ref[b, :width, :].astype(jnp.float32) + own_ref[b, width:, :].astype(jnp.float32)
             out_ref[b, :width, :] = own
 
     @pl.when(flag_ref[0] == 0)
@@ -24,13 +39,21 @@
         out_ref[:, :width, :] = jnp.zeros((blocks, width, edge), jnp.float32)
 
     def one_slot(s, carry):
+        slot = s % 2
+        for c in copies(s, slot):
+            c.wait()
+
+        @pl.when(s + 1 < count)
+        def _next():
+            for c in copies(s + 1, 1 - slot):
+                c.start()
+
         i = ids_ref[2 * s]
-        j = ids_ref[2 * s + 1]
-        both = jnp.dot(x_ref[j], tile_ref[s], preferred_element_type=jnp.float32)
+        both = jnp.dot(xbuf[slot], tbuf[slot], preferred_element_type=jnp.float32)
         out_ref[i, :width, :] += both[:width] + both[width:]
         return carry
 
-    lax.fori_loop(0, cnt_ref[0], one_slot, 0)
+    lax.fori_loop(0, count, one_slot, 0)
 
 
 def _panel_products(ids, cnt, flag, turned, panel, extra):
@@ -40,12 +63,21 @@
     height = width + extra.shape[1]
     smem = pl.BlockSpec(memory_space=pltpu.SMEM)
     vmem = pl.BlockSpec(memory_space=pltpu.VMEM)
+    hbm = pl.BlockSpec(memory_space=pl.ANY)
     flops = slots * pair * edge * edge * 2
     return pl.pallas_call(
         _tile_kernel,
-        in_specs=[smem, smem, smem, vmem, vmem, vmem],
+        in_specs=[smem, smem, smem, hbm, hbm, vmem],
         out_specs=vmem,
         out_shape=jax.ShapeDtypeStruct((blocks, height, edge), jnp.float32),
+        scratch_shapes=[
+            pltpu.VMEM((blocks, pair, edge), panel.dtype),
+            pltpu.VMEM((2, edge, edge), turned.dtype),
+            pltpu.VMEM((2, pair, edge), panel.dtype),
+            pltpu.SemaphoreType.DMA((2,)),
+            pltpu.SemaphoreType.DMA((2,)),
+            pltpu.SemaphoreType.DMA,
+        ],
         compiler_params=pltpu.CompilerParams(vmem_limit_bytes=56 * 1024 * 1024),
         cost_estimate=pl.CostEstimate(
             flops=flops,

time: 187 us -> 209 us (1.12)
  waiting for transfers between devices: 144 us -> 157 us
  Pallas kernels: 9.62 us -> 16.8 us
    unnamed x3, waiting for transfers between devices: 77.3 us -> 90.8 us
    pallas_call x1, Pallas kernels: 9.62 us -> 16.8 us  [_panel_products(): pl.pallas_call(_tile_kernel, in_specs=[smem, smem, smem, hbm, hbm, vmem],...]
where the time goes in v9:
time: 209 us; the launch traced here: 207 us
  waiting for transfers between devices  157 us (75%)
  Pallas kernels  16.8 us (8%)
  between operations  14.1 us (7%)
  local copies, waits for them, and re-layouts  11.8 us (6%)
  other arithmetic  4.73 us (2%)
  matrix products  2.3 us (1%)
    unnamed x3, waiting for transfers between devices  90.8 us
    all_gather x1, waiting for transfers between devices, shards(): panel = lax.all_gather(stacked, 'row', axis=0, tiled=True)  66.5 us
    pallas_call x1, Pallas kernels, _panel_products(): pl.pallas_call(_tile_kernel, in_specs=[smem, smem, smem, hbm, hbm, vmem],...  16.8 us
    unnamed x8, local copies, waits for them, and re-layouts  8.76 us
  transfers between devices with their start and end apart: 2, of which 2 were waited for; matrix products, arithmetic and copies ran while one was open for 6% of the time, Pallas kernels for 0%

profile of v9, /device:TPU:2, one launch (start us, length us, event | category | flops | bytes accessed | tf_op | source)
XLA Modules:
  0.0 207.2 jit_solution(7465707970491825236)
XLA Ops:
  6.5 0.0 copy-start
  6.5 0.0 all-gather.3.cloned.1.call-start
  6.5 1.2 copy-done
  7.8 2.0 reduce-precision_convert_fusion
  9.8 0.8 pad_maximum_fusion
  10.6 0.0 all-gather.3.cloned.1.call-update
  10.7 0.0 reduce-scatter.4.cloned.1.call-start
  11.4 0.8 copy.12
  12.1 0.6 reshape_squeeze.6.ids_ref
  12.8 6.4 %copy.13 = bf16[1,1,32,256,256]{3,4,2,1,0:T(8,128)(2,1)} copy(bf16[1,1,32,256,256]{4,3,2,1,0:T(8,128)(2,1)} %param.9) | data formatting | bytes 8388608 | tf_op args[2]
  19.2 0.0 copy-done.1
  19.2 2.9 %convert_reduce_fusion = f32[32,256]{1,0:T(8,128)S(1)} fusion(bf16[1,1,32,256,256]{3,4,2,1,0:T(8,128)(2,1)} %copy.13), kind=kLoop, calls=%fused_computation | loop fusion | flops 4186112 | bytes 4227072 | tf_op jit(solution)/shard_map/reduce_sum | solution.py:112
  22.1 0.3 fusion.1
  22.4 0.7 scatter.4.extra_ref
  23.0 66.5 %all-gather.3.cloned.1.call-done = bf16[16384,256]{1,0:T(8,128)(2,1)} async-done(((bf16[1024,256]{1,0:T(8,128)(2,1)}), bf16[16384,256]{1,0:T(8,128)(2,1)}) %all-gather.3.cloned.1.call-update) | async-done | bytes 8388624 | tf_op jit(solution)/shard_map/all_gather | solution.py:105
  89.6 16.8 %shard_map.55 = f32[16,520,256]{2,1,0:T(8,128)} custom-call(s32[64]{0:T(128)} %reshape_squeeze.6.ids_ref, s32[1]{0:T(128)} %bitcast.20.cnt_ref, s32[1]{0:T(128)} %bitcast.1.flag_ref, bf16[32,256,256]{2,1,0:T(8,128)(2,1)} %bitcast.22, bf16[16,1024,256]{2,1,0:T(8,128)(2,1)} %bitcast.24, f32[16,8,256]{2,1,0:T(8,128)} %scatter.4.extra_ref), custom_call_target="tpu_custom_call" | custom-call | flops 4294967296 | bytes 21102592 | tf_op jit(solution)/shard_map/pallas_call | solution.py:68
  106.4 0.0 reduce-scatter.4.cloned.1.call-update
  106.4 90.8 %reduce-scatter.4.cloned.1.call-done = f32[520,256]{1,0:T(8,128)} async-done(((f32[8320,256]{1,0:T(8,128)}), f32[520,256]{1,0:T(8,128)}) %reduce-scatter.4.cloned.1.call-update) | async-done | bytes 532496
  197.2 1.1 slice.31
  198.3 0.2 copy.17
  198.5 0.7 slice.32
  199.2 0.1 copy.18
  199.3 0.1 rsqrt_reduce_fusion
  199.4 0.9 maximum_bitcast_fusion
  (4 shorter events, 0.0 us)
Async XLA Ops:
  6.5 1.2 copy-start
  6.5 12.7 %copy-start.1 = (s32[1,1,32,2]{2,3,1,0:T(2,128)S(1)}, s32[1,1,32,2]{2,3,1,0:T(2,128)}, u32[]{:S(2)}) copy-start(s32[1,1,32,2]{2,3,1,0:T(2,128)} %param.10) | copy-start | bytes 772
  6.5 83.0 %all-gather.3.cloned.1.call-start = ((), (), s32[]{:S(2)}) async-start(), calls=%async_computation.1 | async-start | bytes 8912896 | tf_op jit(solution)/shard_map/all_gather | solution.py:105
  10.7 186.5 %reduce-scatter.4.cloned.1.call-start = ((), (), s32[]{:S(2)}) async-start(), calls=%async_computation.2 | async-start | bytes 9052160
Sparse Core Ops, SparseCore 0:
  10.8 78.7 all-gather.2
  106.5 90.6 reduce-scatter.3

commit v10 on v6

--- a/solution.py
+++ b/solution.py
@@ -55,6 +55,49 @@
     )(ids, cnt, flag, turned, panel, extra)
 
 
+def _split_kernel(x_ref, w_ref, out_ref):
+    width = w_ref.shape[1]
+    product = jnp.dot(x_ref[...], w_ref[...], precision=lax.Precision.HIGHEST,
+                      preferred_element_type=jnp.float32)
+    turned = product.T
+    hi = turned.astype(jnp.bfloat16)
+    out_ref[:width, :] = hi
+    out_ref[width:, :] = (turned - hi.astype(jnp.float32)).astype(jnp.bfloat16)
+
+
+def _split_product(features, weight):
+    rows, width = features.shape[0], weight.shape[1]
+    vmem = pl.BlockSpec(memory_space=pltpu.VMEM)
+    return pl.pallas_call(
+        _split_kernel,
+        in_specs=[vmem, vmem],
+        out_specs=vmem,
+        out_shape=jax.ShapeDtypeStruct((2 * width, rows), jnp.bfloat16),
+        cost_estimate=pl.CostEstimate(
+            flops=rows * weight.shape[0] * width * 2 * 6,
+            bytes_accessed=features.size * 4 + weight.size * 4 + 2 * width * rows * 2,
+            transcendentals=0,
+        ),
+    )(features, weight)
+
+
+def _finish_kernel(mine_ref, out_ref):
+    width = out_ref.shape[1]
+    scale = lax.rsqrt(1.0 + mine_ref[width:width + 1, :])
+    out_ref[...] = jnp.maximum(mine_ref[:width, :] * scale, 0.0).T
+
+
+def _finish(mine, width):
+    edge = mine.shape[1]
+    vmem = pl.BlockSpec(memory_space=pltpu.VMEM)
+    return pl.pallas_call(
+        _finish_kernel,
+        in_specs=[vmem],
+        out_specs=vmem,
+        out_shape=jax.ShapeDtypeStruct((edge, width), jnp.float32),
+    )(mine)
+
+
 def shards(features, weight, tile_values, tile_ids, tile_counts):
     tile_set = tile_values[0, 0]
     slots, edge, _ = tile_set.shape
@@ -63,13 +106,7 @@
     live_count = tile_counts[0, 0]
     cnt = live_count.reshape(1)
     flag = (lax.axis_index("row") == lax.axis_index("col")).astype(jnp.int32).reshape(1)
-    turned_w = lax.dot_general(
-        weight, features, (((0,), (1,)), ((), ())), precision=lax.Precision.HIGH
-    )
-    rounded = lax.reduce_precision(turned_w, exponent_bits=8, mantissa_bits=7)
-    hi = rounded.astype(jnp.bfloat16)
-    lo = (turned_w - rounded).astype(jnp.bfloat16)
-    stacked = jnp.concatenate([hi, lo], axis=0)[None]
+    stacked = _split_product(features, weight)[None]
     panel = lax.all_gather(stacked, "row", axis=0, tiled=True)
     blocks, pair, _ = panel.shape
     width = pair // 2
@@ -85,9 +122,7 @@
     mine = lax.psum_scatter(
         partial.reshape(blocks * height, edge), "col", scatter_dimension=0, tiled=True
     )
-    degree = 1.0 + mine[width]
-    inverse_root = lax.rsqrt(degree)
-    return jnp.maximum(mine[:width].T * inverse_root[:, None], 0.0)
+    return _finish(mine, width)
 
 
 def solution(mesh):

time: 187 us -> 186 us (level)
  Pallas kernels: 9.62 us -> 22.9 us
  waiting for transfers between devices: 144 us -> 137 us
  local copies, waits for them, and re-layouts: 11.8 us -> 8.52 us
  matrix products: 2.3 us -> 0.26 us
    unnamed x3 -> x2, waiting for transfers between devices: 77.3 us -> 0.03 us
    reduce_scatter x0 -> x1, waiting for transfers between devices: none -> 70.7 us  [shards(): lax.psum_scatter(partial.reshape(blocks * height, edge), 'col', scatter_d...]
    pallas_call x1, Pallas kernels: 9.62 us -> 17.5 us  [_panel_products(): pl.pallas_call(_tile_kernel, in_specs=[smem, smem, smem, vmem, vmem, vmem...]
    pallas_call x0 -> x2, Pallas kernels: none -> 5.44 us  [the longest x1 3.39 us: _split_product(): pl.pallas_call(_split_kernel, in_specs=[vmem, vmem], out_specs=vmem, out_...]
    dot_general x1 -> x0, matrix products: 2.04 us -> none  [shards(): lax.dot_general(weight, features, (((0,), (1,)), ((), ())), precision=lax...]
    unnamed x8 -> x4, local copies, waits for them, and re-layouts: 8.76 us -> 7.2 us
where the time goes in v10:
time: 186 us
  waiting for transfers between devices  137 us (74%)
  Pallas kernels  22.9 us (12%)
  between operations  14.1 us (8%)
  local copies, waits for them, and re-layouts  8.52 us (5%)
  other arithmetic  2.87 us (2%)
    reduce_scatter x1, waiting for transfers between devices, shards(): lax.psum_scatter(partial.reshape(blocks * height, edge), 'col', scatter_d...  70.7 us
    all_gather x1, waiting for transfers between devices, shards(): panel = lax.all_gather(stacked, 'row', axis=0, tiled=True)  66.5 us
    pallas_call x1, Pallas kernels, _panel_products(): pl.pallas_call(_tile_kernel, in_specs=[smem, smem, smem, vmem, vmem, vmem...  17.5 us
    unnamed x4, local copies, waits for them, and re-layouts  7.2 us
  transfers between devices with their start and end apart: 2, of which 2 were waited for; matrix products, arithmetic and copies ran while one was open for 6% of the time, Pallas kernels for 0%

profile of v10, /device:TPU:2, one launch (start us, length us, event | category | flops | bytes accessed | tf_op | source)
XLA Modules:
  0.0 185.9 jit_solution(14126150358794930521)
XLA Ops:
  6.5 0.0 copy-start
  6.5 0.0 all-gather.3.cloned.1.call-start
  6.5 3.4 %shard_map.55 = bf16[1024,256]{1,0:T(8,128)(2,1)} custom-call(f32[256,512]{1,0:T(8,128)} %x_ref.1, f32[512,512]{1,0:T(8,128)} %w_ref.1), custom_call_target="tpu_custom_call" | custom-call | flops 805306368 | bytes 2097152 | tf_op jit(solution)/shard_map/pallas_call | solution.py:71
  9.9 0.0 all-gather.3.cloned.1.call-update
  10.0 0.0 reduce-scatter.2.cloned.1.call-start
  10.7 0.8 copy.8
  11.4 0.6 reshape_squeeze.6.ids_ref
  12.0 6.4 %copy.9 = bf16[1,1,32,256,256]{3,4,2,1,0:T(8,128)(2,1)} copy(bf16[1,1,32,256,256]{4,3,2,1,0:T(8,128)(2,1)} %param.9) | data formatting | bytes 8388608 | tf_op args[2]
  18.5 0.0 copy-done
  18.5 2.9 %convert_reduce_fusion = f32[32,256]{1,0:T(8,128)S(1)} fusion(bf16[1,1,32,256,256]{3,4,2,1,0:T(8,128)(2,1)} %copy.9), kind=kLoop, calls=%fused_computation | loop fusion | flops 4186112 | bytes 4227072 | tf_op jit(solution)/shard_map/reduce_sum | solution.py:117
  21.4 0.3 fusion
  21.7 0.7 scatter.4.extra_ref
  22.3 66.5 %all-gather.3.cloned.1.call-done = bf16[16384,256]{1,0:T(8,128)(2,1)} async-done(((bf16[1024,256]{1,0:T(8,128)(2,1)}), bf16[16384,256]{1,0:T(8,128)(2,1)}) %all-gather.3.cloned.1.call-update) | async-done | bytes 8388624 | tf_op jit(solution)/shard_map/all_gather | solution.py:110
  88.9 17.5 %shard_map.56 = f32[16,520,256]{2,1,0:T(8,128)} custom-call(s32[64]{0:T(128)} %reshape_squeeze.6.ids_ref, s32[1]{0:T(128)} %bitcast.15.cnt_ref, s32[1]{0:T(128)} %bitcast.1.flag_ref, bf16[32,256,256]{2,1,0:T(8,128)(2,1)} %bitcast.17, bf16[16,1024,256]{2,1,0:T(8,128)(2,1)} %bitcast.19, f32[16,8,256]{2,1,0:T(8,128)} %scatter.4.extra_ref), custom_call_target="tpu_custom_call" | custom-call | flops 4294967296 | bytes 21102592 | tf_op jit(solution)/shard_map/pallas_call | solution.py:44
  106.4 0.0 reduce-scatter.2.cloned.1.call-update
  106.4 70.7 %reduce-scatter.2.cloned.1.call-done.mine_ref = f32[520,256]{1,0:T(8,128)} async-done(((f32[8320,256]{1,0:T(8,128)}), f32[520,256]{1,0:T(8,128)}) %reduce-scatter.2.cloned.1.call-update) | async-done | bytes 532496 | tf_op jit(solution)/shard_map/reduce_scatter | solution.py:122
  177.0 2.0 %shard_map.57 = f32[256,512]{1,0:T(8,128)} custom-call(f32[520,256]{1,0:T(8,128)} %reduce-scatter.2.cloned.1.call-done.mine_ref), custom_call_target="tpu_custom_call" | custom-call | tf_op jit(solution)/shard_map/pallas_call | solution.py:93
  (3 shorter events, 0.0 us)
Async XLA Ops:
  6.5 12.0 %copy-start = (s32[1,1,32,2]{2,3,1,0:T(2,128)S(1)}, s32[1,1,32,2]{2,3,1,0:T(2,128)}, u32[]{:S(2)}) copy-start(s32[1,1,32,2]{2,3,1,0:T(2,128)} %param.10) | copy-start | bytes 772
  6.5 82.3 %all-gather.3.cloned.1.call-start = ((), (), s32[]{:S(2)}) async-start(), calls=%async_computation.2 | async-start | bytes 8912896 | tf_op jit(solution)/shard_map/all_gather | solution.py:110
  10.0 167.1 %reduce-scatter.2.cloned.1.call-start = ((), (), s32[]{:S(2)}) async-start(), calls=%async_computation.1 | async-start | bytes 9052160 | tf_op jit(solution)/shard_map/reduce_scatter | solution.py:122
Sparse Core Ops, SparseCore 0:
  10.1 78.7 all-gather.2
  106.5 70.5 reduce-scatter.1

commit v11 on v10

--- a/solution.py
+++ b/solution.py
@@ -10,13 +10,13 @@
 
 def _tile_kernel(ids_ref, cnt_ref, flag_ref, tile_ref, x_ref, extra_ref, out_ref):
     blocks, height, edge = out_ref.shape
-    width = x_ref.shape[1] // 2
+    width = x_ref.shape[1]
     out_ref[:, width:, :] = extra_ref[...]
 
     @pl.when(flag_ref[0] != 0)
     def _diagonal():
         for b in range(blocks):
-            own = x_ref[b, :width, :].astype(jnp.float32) + x_ref[b, width:, :].astype(jnp.float32)
+            own = x_ref[b, :, :edge].astype(jnp.float32) + x_ref[b, :, edge:].astype(jnp.float32)
             out_ref[b, :width, :] = own
 
     @pl.when(flag_ref[0] == 0)
@@ -26,8 +26,9 @@
     def one_slot(s, carry):
         i = ids_ref[2 * s]
         j = ids_ref[2 * s + 1]
-        both = jnp.dot(x_ref[j], tile_ref[s], preferred_element_type=jnp.float32)
-        out_ref[i, :width, :] += both[:width] + both[width:]
+        tile = tile_ref[s]
+        stacked = jnp.concatenate([tile, tile], axis=0)
+        out_ref[i, :width, :] += jnp.dot(x_ref[j], stacked, preferred_element_type=jnp.float32)
         return carry
 
     lax.fori_loop(0, cnt_ref[0], one_slot, 0)
@@ -35,8 +36,7 @@
 
 def _panel_products(ids, cnt, flag, turned, panel, extra):
     slots, edge, _ = turned.shape
-    blocks, pair, _ = panel.shape
-    width = pair // 2
+    blocks, width, pair = panel.shape
     height = width + extra.shape[1]
     smem = pl.BlockSpec(memory_space=pltpu.SMEM)
     vmem = pl.BlockSpec(memory_space=pltpu.VMEM)
@@ -60,9 +60,10 @@
     product = jnp.dot(x_ref[...], w_ref[...], precision=lax.Precision.HIGHEST,
                       preferred_element_type=jnp.float32)
     turned = product.T
+    rows = turned.shape[1]
     hi = turned.astype(jnp.bfloat16)
-    out_ref[:width, :] = hi
-    out_ref[width:, :] = (turned - hi.astype(jnp.float32)).astype(jnp.bfloat16)
+    out_ref[:, :rows] = hi
+    out_ref[:, rows:] = (turned - hi.astype(jnp.float32)).astype(jnp.bfloat16)
 
 
 def _split_product(features, weight):
@@ -72,7 +73,7 @@
         _split_kernel,
         in_specs=[vmem, vmem],
         out_specs=vmem,
-        out_shape=jax.ShapeDtypeStruct((2 * width, rows), jnp.bfloat16),
+        out_shape=jax.ShapeDtypeStruct((width, 2 * rows), jnp.bfloat16),
         cost_estimate=pl.CostEstimate(
             flops=rows * weight.shape[0] * width * 2 * 6,
             bytes_accessed=features.size * 4 + weight.size * 4 + 2 * width * rows * 2,
@@ -108,8 +109,7 @@
     flag = (lax.axis_index("row") == lax.axis_index("col")).astype(jnp.int32).reshape(1)
     stacked = _split_product(features, weight)[None]
     panel = lax.all_gather(stacked, "row", axis=0, tiled=True)
-    blocks, pair, _ = panel.shape
-    width = pair // 2
+    blocks, width, _ = panel.shape
     turned = jnp.swapaxes(tile_set, 1, 2)
     is_live = (jnp.arange(slots) < live_count).astype(jnp.float32)
     placement = (slot_ids[:, 0][:, None] == jnp.arange(blocks)[None, :]).astype(jnp.float32)

time: 186 us -> 184 us (0.989)
  Pallas kernels: 22.9 us -> 20.4 us
    pallas_call x1, Pallas kernels: 17.5 us -> 15 us  [_panel_products(): pl.pallas_call(_tile_kernel, in_specs=[smem, smem, smem, vmem, vmem, vmem...]
where the time goes in v11:
time: 184 us
  waiting for transfers between devices  138 us (75%)
  Pallas kernels  20.4 us (11%)
  between operations  14.1 us (8%)
  local copies, waits for them, and re-layouts  8.52 us (5%)
  other arithmetic  2.87 us (2%)
    reduce_scatter x1, waiting for transfers between devices, shards(): lax.psum_scatter(partial.reshape(blocks * height, edge), 'col', scatter_d...  71.5 us
    all_gather x1, waiting for transfers between devices, shards(): panel = lax.all_gather(stacked, 'row', axis=0, tiled=True)  66.5 us
    pallas_call x1, Pallas kernels, _panel_products(): pl.pallas_call(_tile_kernel, in_specs=[smem, smem, smem, vmem, vmem, vmem...  15 us
    unnamed x4, local copies, waits for them, and re-layouts  7.2 us
  transfers between devices with their start and end apart: 2, of which 2 were waited for; matrix products, arithmetic and copies ran while one was open for 6% of the time, Pallas kernels for 0%

profile of v11, /device:TPU:2, one launch (start us, length us, event | category | flops | bytes accessed | tf_op | source)
XLA Modules:
  0.0 184.2 jit_solution(1535017909303514002)
XLA Ops:
  6.5 0.0 copy-start
  6.5 0.0 all-gather.3.cloned.1.call-start
  6.5 3.4 %shard_map.55 = bf16[512,512]{1,0:T(8,128)(2,1)} custom-call(f32[256,512]{1,0:T(8,128)} %x_ref.1, f32[512,512]{1,0:T(8,128)} %w_ref.1), custom_call_target="tpu_custom_call" | custom-call | flops 805306368 | bytes 2097152 | tf_op jit(solution)/shard_map/pallas_call | solution.py:72
  9.9 0.0 all-gather.3.cloned.1.call-update
  10.0 0.0 reduce-scatter.2.cloned.1.call-start
  10.7 0.8 copy.8
  11.4 0.6 reshape_squeeze.6.ids_ref
  12.0 6.4 %copy.9 = bf16[1,1,32,256,256]{3,4,2,1,0:T(8,128)(2,1)} copy(bf16[1,1,32,256,256]{4,3,2,1,0:T(8,128)(2,1)} %param.9) | data formatting | bytes 8388608 | tf_op args[2]
  18.5 0.0 copy-done
  18.5 2.9 %convert_reduce_fusion = f32[32,256]{1,0:T(8,128)S(1)} fusion(bf16[1,1,32,256,256]{3,4,2,1,0:T(8,128)(2,1)} %copy.9), kind=kLoop, calls=%fused_computation | loop fusion | flops 4186112 | bytes 4227072 | tf_op jit(solution)/shard_map/reduce_sum | solution.py:117
  21.4 0.3 fusion
  21.7 0.7 scatter.4.extra_ref
  22.3 66.5 %all-gather.3.cloned.1.call-done = bf16[8192,512]{1,0:T(8,128)(2,1)} async-done(((bf16[512,512]{1,0:T(8,128)(2,1)}), bf16[8192,512]{1,0:T(8,128)(2,1)}) %all-gather.3.cloned.1.call-update) | async-done | bytes 8388624 | tf_op jit(solution)/shard_map/all_gather | solution.py:111
  88.9 15.0 %shard_map.56 = f32[16,520,256]{2,1,0:T(8,128)} custom-call(s32[64]{0:T(128)} %reshape_squeeze.6.ids_ref, s32[1]{0:T(128)} %bitcast.15.cnt_ref, s32[1]{0:T(128)} %bitcast.1.flag_ref, bf16[32,256,256]{2,1,0:T(8,128)(2,1)} %bitcast.17, bf16[16,512,512]{2,1,0:T(8,128)(2,1)} %bitcast.19, f32[16,8,256]{2,1,0:T(8,128)} %scatter.4.extra_ref), custom_call_target="tpu_custom_call" | custom-call | flops 2147483648 | bytes 21102592 | tf_op jit(solution)/shard_map/pallas_call | solution.py:44
  103.9 0.0 reduce-scatter.2.cloned.1.call-update
  103.9 71.5 %reduce-scatter.2.cloned.1.call-done.mine_ref = f32[520,256]{1,0:T(8,128)} async-done(((f32[8320,256]{1,0:T(8,128)}), f32[520,256]{1,0:T(8,128)}) %reduce-scatter.2.cloned.1.call-update) | async-done | bytes 532496 | tf_op jit(solution)/shard_map/reduce_scatter | solution.py:122
  175.3 2.0 %shard_map.57 = f32[256,512]{1,0:T(8,128)} custom-call(f32[520,256]{1,0:T(8,128)} %reduce-scatter.2.cloned.1.call-done.mine_ref), custom_call_target="tpu_custom_call" | custom-call | tf_op jit(solution)/shard_map/pallas_call | solution.py:94
  (3 shorter events, 0.0 us)
Async XLA Ops:
  6.5 12.0 %copy-start = (s32[1,1,32,2]{2,3,1,0:T(2,128)S(1)}, s32[1,1,32,2]{2,3,1,0:T(2,128)}, u32[]{:S(2)}) copy-start(s32[1,1,32,2]{2,3,1,0:T(2,128)} %param.10) | copy-start | bytes 772
  6.5 82.3 %all-gather.3.cloned.1.call-start = ((), (), s32[]{:S(2)}) async-start(), calls=%async_computation.2 | async-start | bytes 8912896 | tf_op jit(solution)/shard_map/all_gather | solution.py:111
  10.0 165.4 %reduce-scatter.2.cloned.1.call-start = ((), (), s32[]{:S(2)}) async-start(), calls=%async_computation.1 | async-start | bytes 9052160 | tf_op jit(solution)/shard_map/reduce_scatter | solution.py:122
Sparse Core Ops, SparseCore 0:
  10.1 78.7 all-gather.2
  104.0 71.2 reduce-scatter.1

commit v12 on v10

--- a/solution.py
+++ b/solution.py
@@ -8,10 +8,30 @@
 EXTRA = 8
 
 
-def _tile_kernel(ids_ref, cnt_ref, flag_ref, tile_ref, x_ref, extra_ref, out_ref):
+def _tile_kernel(ids_ref, cnt_ref, flag_ref, tile_hbm, x_hbm, extra_ref, out_ref,
+                 tile_ref, x_ref, tile_sem, x_sem):
     blocks, height, edge = out_ref.shape
     width = x_ref.shape[1] // 2
+    count = cnt_ref[0]
+
+    panel_copy = pltpu.make_async_copy(x_hbm, x_ref, x_sem)
+    panel_copy.start()
+
+    def tile_copy(s):
+        return pltpu.make_async_copy(tile_hbm.at[s], tile_ref.at[s], tile_sem.at[s])
+
+    def start_tile(s, carry):
+        tile_copy(s).start()
+        return carry
+
+    lax.fori_loop(0, count, start_tile, 0)
     out_ref[:, width:, :] = extra_ref[...]
+
+    @pl.when(flag_ref[0] == 0)
+    def _elsewhere():
+        out_ref[:, :width, :] = jnp.zeros((blocks, width, edge), jnp.float32)
+
+    panel_copy.wait()
 
     @pl.when(flag_ref[0] != 0)
     def _diagonal():
@@ -19,18 +39,15 @@
             own = x_ref[b, :width, :].astype(jnp.float32) + x_ref[b, width:, :].astype(jnp.float32)
             out_ref[b, :width, :] = own
 
-    @pl.when(flag_ref[0] == 0)
-    def _elsewhere():
-        out_ref[:, :width, :] = jnp.zeros((blocks, width, edge), jnp.float32)
-
     def one_slot(s, carry):
+        tile_copy(s).wait()
         i = ids_ref[2 * s]
         j = ids_ref[2 * s + 1]
         both = jnp.dot(x_ref[j], tile_ref[s], preferred_element_type=jnp.float32)
         out_ref[i, :width, :] += both[:width] + both[width:]
         return carry
 
-    lax.fori_loop(0, cnt_ref[0], one_slot, 0)
+    lax.fori_loop(0, count, one_slot, 0)
 
 
 def _panel_products(ids, cnt, flag, turned, panel, extra):
@@ -40,12 +57,19 @@
     height = width + extra.shape[1]
     smem = pl.BlockSpec(memory_space=pltpu.SMEM)
     vmem = pl.BlockSpec(memory_space=pltpu.VMEM)
+    hbm = pl.BlockSpec(memory_space=pl.ANY)
     flops = slots * pair * edge * edge * 2
     return pl.pallas_call(
         _tile_kernel,
-        in_specs=[smem, smem, smem, vmem, vmem, vmem],
+        in_specs=[smem, smem, smem, hbm, hbm, vmem],
         out_specs=vmem,
         out_shape=jax.ShapeDtypeStruct((blocks, height, edge), jnp.float32),
+        scratch_shapes=[
+            pltpu.VMEM(turned.shape, turned.dtype),
+            pltpu.VMEM(panel.shape, panel.dtype),
+            pltpu.SemaphoreType.DMA((slots,)),
+            pltpu.SemaphoreType.DMA,
+        ],
         compiler_params=pltpu.CompilerParams(vmem_limit_bytes=56 * 1024 * 1024),
         cost_estimate=pl.CostEstimate(
             flops=flops,

time: 186 us -> 185 us (level)
  waiting for transfers between devices: 137 us -> 142 us
  Pallas kernels: 22.9 us -> 18.1 us
    pallas_call x1, Pallas kernels: 17.5 us -> 12.7 us  [_panel_products(): pl.pallas_call(_tile_kernel, in_specs=[smem, smem, smem, hbm, hbm, vmem],...]
    reduce_scatter x1, waiting for transfers between devices: 70.7 us -> 75.4 us  [shards(): lax.psum_scatter(partial.reshape(blocks * height, edge), 'col', scatter_d...]
where the time goes in v12:
time: 185 us; the launch traced here: 186 us
  waiting for transfers between devices  142 us (77%)
  Pallas kernels  18.1 us (10%)
  between operations  14.1 us (8%)
  local copies, waits for them, and re-layouts  8.52 us (5%)
  other arithmetic  2.87 us (2%)
    reduce_scatter x1, waiting for transfers between devices, shards(): lax.psum_scatter(partial.reshape(blocks * height, edge), 'col', scatter_d...  75.4 us
    all_gather x1, waiting for transfers between devices, shards(): panel = lax.all_gather(stacked, 'row', axis=0, tiled=True)  66.5 us
    pallas_call x1, Pallas kernels, _panel_products(): pl.pallas_call(_tile_kernel, in_specs=[smem, smem, smem, hbm, hbm, vmem],...  12.7 us
    unnamed x4, local copies, waits for them, and re-layouts  7.2 us
  transfers between devices with their start and end apart: 2, of which 2 were waited for; matrix products, arithmetic and copies ran while one was open for 6% of the time, Pallas kernels for 0%

profile of v12, /device:TPU:2, one launch (start us, length us, event | category | flops | bytes accessed | tf_op | source)
XLA Modules:
  0.0 185.9 jit_solution(10971590794414681382)
XLA Ops:
  6.5 0.0 copy-start
  6.5 0.0 all-gather.3.cloned.1.call-start
  6.5 3.4 %shard_map.55 = bf16[1024,256]{1,0:T(8,128)(2,1)} custom-call(f32[256,512]{1,0:T(8,128)} %x_ref.1, f32[512,512]{1,0:T(8,128)} %w_ref.1), custom_call_target="tpu_custom_call" | custom-call | flops 805306368 | bytes 2097152 | tf_op jit(solution)/shard_map/pallas_call | solution.py:95
  9.9 0.0 all-gather.3.cloned.1.call-update
  10.0 0.0 reduce-scatter.2.cloned.1.call-start
  10.7 0.8 copy.8
  11.4 0.6 reshape_squeeze.6.ids_ref
  12.0 6.4 %copy.9 = bf16[1,1,32,256,256]{3,4,2,1,0:T(8,128)(2,1)} copy(bf16[1,1,32,256,256]{4,3,2,1,0:T(8,128)(2,1)} %param.9) | data formatting | bytes 8388608 | tf_op args[2]
  18.5 0.0 copy-done
  18.5 2.9 %convert_reduce_fusion = f32[32,256]{1,0:T(8,128)S(1)} fusion(bf16[1,1,32,256,256]{3,4,2,1,0:T(8,128)(2,1)} %copy.9), kind=kLoop, calls=%fused_computation | loop fusion | flops 4186112 | bytes 4227072 | tf_op jit(solution)/shard_map/reduce_sum | solution.py:141
  21.4 0.3 fusion
  21.7 0.7 scatter.4.extra_ref
  22.3 66.5 %all-gather.3.cloned.1.call-done = bf16[16384,256]{1,0:T(8,128)(2,1)} async-done(((bf16[1024,256]{1,0:T(8,128)(2,1)}), bf16[16384,256]{1,0:T(8,128)(2,1)}) %all-gather.3.cloned.1.call-update) | async-done | bytes 8388624 | tf_op jit(solution)/shard_map/all_gather | solution.py:134
  88.9 12.7 %shard_map.56 = f32[16,520,256]{2,1,0:T(8,128)} custom-call(s32[64]{0:T(128)} %reshape_squeeze.6.ids_ref, s32[1]{0:T(128)} %bitcast.15.cnt_ref, s32[1]{0:T(128)} %bitcast.1.flag_ref, bf16[32,256,256]{2,1,0:T(8,128)(2,1)} %bitcast.17, bf16[16,1024,256]{2,1,0:T(8,128)(2,1)} %bitcast.19, f32[16,8,256]{2,1,0:T(8,128)} %scatter.4.extra_ref), custom_call_target="tpu_custom_call" | custom-call | flops 4294967296 | bytes 21102592 | tf_op jit(solution)/shard_map/pallas_call | solution.py:62
  101.6 0.0 reduce-scatter.2.cloned.1.call-update
  101.6 75.4 %reduce-scatter.2.cloned.1.call-done.mine_ref = f32[520,256]{1,0:T(8,128)} async-done(((f32[8320,256]{1,0:T(8,128)}), f32[520,256]{1,0:T(8,128)}) %reduce-scatter.2.cloned.1.call-update) | async-done | bytes 532496 | tf_op jit(solution)/shard_map/reduce_scatter | solution.py:146
  177.0 2.0 %shard_map.57 = f32[256,512]{1,0:T(8,128)} custom-call(f32[520,256]{1,0:T(8,128)} %reduce-scatter.2.cloned.1.call-done.mine_ref), custom_call_target="tpu_custom_call" | custom-call | tf_op jit(solution)/shard_map/pallas_call | solution.py:117
  (3 shorter events, 0.0 us)
Async XLA Ops:
  6.5 12.0 %copy-start = (s32[1,1,32,2]{2,3,1,0:T(2,128)S(1)}, s32[1,1,32,2]{2,3,1,0:T(2,128)}, u32[]{:S(2)}) copy-start(s32[1,1,32,2]{2,3,1,0:T(2,128)} %param.10) | copy-start | bytes 772
  6.5 82.3 %all-gather.3.cloned.1.call-start = ((), (), s32[]{:S(2)}) async-start(), calls=%async_computation.2 | async-start | bytes 8912896 | tf_op jit(solution)/shard_map/all_gather | solution.py:134
  10.0 167.0 %reduce-scatter.2.cloned.1.call-start = ((), (), s32[]{:S(2)}) async-start(), calls=%async_computation.1 | async-start | bytes 9052160 | tf_op jit(solution)/shard_map/reduce_scatter | solution.py:146
Sparse Core Ops, SparseCore 0:
  10.1 78.7 all-gather.2
  101.7 75.2 reduce-scatter.1

commit v13 on v12

--- a/solution.py
+++ b/solution.py
@@ -81,8 +81,15 @@
 
 def _split_kernel(x_ref, w_ref, out_ref):
     width = w_ref.shape[1]
-    product = jnp.dot(x_ref[...], w_ref[...], precision=lax.Precision.HIGHEST,
-                      preferred_element_type=jnp.float32)
+    x = x_ref[...]
+    w = w_ref[...]
+    x_hi = x.astype(jnp.bfloat16)
+    x_lo = (x - x_hi.astype(jnp.float32)).astype(jnp.bfloat16)
+    w_hi = w.astype(jnp.bfloat16)
+    w_lo = (w - w_hi.astype(jnp.float32)).astype(jnp.bfloat16)
+    product = jnp.dot(x_hi, w_hi, preferred_element_type=jnp.float32)
+    product += jnp.dot(x_hi, w_lo, preferred_element_type=jnp.float32)
+    product += jnp.dot(x_lo, w_hi, preferred_element_type=jnp.float32)
     turned = product.T
     hi = turned.astype(jnp.bfloat16)
     out_ref[:width, :] = hi
@@ -98,7 +105,7 @@
         out_specs=vmem,
         out_shape=jax.ShapeDtypeStruct((2 * width, rows), jnp.bfloat16),
         cost_estimate=pl.CostEstimate(
-            flops=rows * weight.shape[0] * width * 2 * 6,
+            flops=rows * weight.shape[0] * width * 2 * 3,
             bytes_accessed=features.size * 4 + weight.size * 4 + 2 * width * rows * 2,
             transcendentals=0,
         ),

time: 185 us -> 185 us (level)
  Pallas kernels: 18.1 us -> 15.6 us
    pallas_call x1, Pallas kernels: 12.7 us -> 10.6 us  [_panel_products(): pl.pallas_call(_tile_kernel, in_specs=[smem, smem, smem, hbm, hbm, vmem],...]
where the time goes in v13:
time: 185 us; the launch traced here: 184 us
  waiting for transfers between devices  143 us (77%)
  Pallas kernels  15.6 us (8%)
  between operations  14.1 us (8%)
  local copies, waits for them, and re-layouts  8.52 us (5%)
  other arithmetic  2.87 us (2%)
    reduce_scatter x1, waiting for transfers between devices, shards(): lax.psum_scatter(partial.reshape(blocks * height, edge), 'col', scatter_d...  76.5 us
    all_gather x1, waiting for transfers between devices, shards(): panel = lax.all_gather(stacked, 'row', axis=0, tiled=True)  66.7 us
    pallas_call x1, Pallas kernels, _panel_products(): pl.pallas_call(_tile_kernel, in_specs=[smem, smem, smem, hbm, hbm, vmem],...  10.6 us
    unnamed x4, local copies, waits for them, and re-layouts  7.2 us
  transfers between devices with their start and end apart: 2, of which 2 were waited for; matrix products, arithmetic and copies ran while one was open for 6% of the time, Pallas kernels for 0%

profile of v13, /device:TPU:2, one launch (start us, length us, event | category | flops | bytes accessed | tf_op | source)
XLA Modules:
  0.0 184.5 jit_solution(2005197568495195730)
XLA Ops:
  6.5 0.0 copy-start
  6.5 0.0 all-gather.3.cloned.1.call-start
  6.5 2.9 %shard_map.55 = bf16[1024,256]{1,0:T(8,128)(2,1)} custom-call(f32[256,512]{1,0:T(8,128)} %x_ref.1, f32[512,512]{1,0:T(8,128)} %w_ref.1), custom_call_target="tpu_custom_call" | custom-call | flops 402653184 | bytes 2097152 | tf_op jit(solution)/shard_map/pallas_call | solution.py:102
  9.5 0.0 all-gather.3.cloned.1.call-update
  9.5 0.0 reduce-scatter.2.cloned.1.call-start
  10.2 0.8 copy.8
  11.0 0.6 reshape_squeeze.6.ids_ref
  11.6 6.4 %copy.9 = bf16[1,1,32,256,256]{3,4,2,1,0:T(8,128)(2,1)} copy(bf16[1,1,32,256,256]{4,3,2,1,0:T(8,128)(2,1)} %param.9) | data formatting | bytes 8388608 | tf_op args[2]
  18.0 0.0 copy-done
  18.0 2.9 %convert_reduce_fusion = f32[32,256]{1,0:T(8,128)S(1)} fusion(bf16[1,1,32,256,256]{3,4,2,1,0:T(8,128)(2,1)} %copy.9), kind=kLoop, calls=%fused_computation | loop fusion | flops 4186112 | bytes 4227072 | tf_op jit(solution)/shard_map/reduce_sum | solution.py:148
  20.9 0.3 fusion
  21.2 0.7 scatter.4.extra_ref
  21.9 66.7 %all-gather.3.cloned.1.call-done = bf16[16384,256]{1,0:T(8,128)(2,1)} async-done(((bf16[1024,256]{1,0:T(8,128)(2,1)}), bf16[16384,256]{1,0:T(8,128)(2,1)}) %all-gather.3.cloned.1.call-update) | async-done | bytes 8388624 | tf_op jit(solution)/shard_map/all_gather | solution.py:141
  88.5 10.6 %shard_map.56 = f32[16,520,256]{2,1,0:T(8,128)} custom-call(s32[64]{0:T(128)} %reshape_squeeze.6.ids_ref, s32[1]{0:T(128)} %bitcast.15.cnt_ref, s32[1]{0:T(128)} %bitcast.1.flag_ref, bf16[32,256,256]{2,1,0:T(8,128)(2,1)} %bitcast.17, bf16[16,1024,256]{2,1,0:T(8,128)(2,1)} %bitcast.19, f32[16,8,256]{2,1,0:T(8,128)} %scatter.4.extra_ref), custom_call_target="tpu_custom_call" | custom-call | flops 4294967296 | bytes 21102592 | tf_op jit(solution)/shard_map/pallas_call | solution.py:62
  99.1 0.0 reduce-scatter.2.cloned.1.call-update
  99.1 76.5 %reduce-scatter.2.cloned.1.call-done.mine_ref = f32[520,256]{1,0:T(8,128)} async-done(((f32[8320,256]{1,0:T(8,128)}), f32[520,256]{1,0:T(8,128)}) %reduce-scatter.2.cloned.1.call-update) | async-done | bytes 532496 | tf_op jit(solution)/shard_map/reduce_scatter | solution.py:153
  175.6 2.0 %shard_map.57 = f32[256,512]{1,0:T(8,128)} custom-call(f32[520,256]{1,0:T(8,128)} %reduce-scatter.2.cloned.1.call-done.mine_ref), custom_call_target="tpu_custom_call" | custom-call | tf_op jit(solution)/shard_map/pallas_call | solution.py:124
  (3 shorter events, 0.0 us)
Async XLA Ops:
  6.5 11.5 %copy-start = (s32[1,1,32,2]{2,3,1,0:T(2,128)S(1)}, s32[1,1,32,2]{2,3,1,0:T(2,128)}, u32[]{:S(2)}) copy-start(s32[1,1,32,2]{2,3,1,0:T(2,128)} %param.10) | copy-start | bytes 772
  6.5 82.0 %all-gather.3.cloned.1.call-start = ((), (), s32[]{:S(2)}) async-start(), calls=%async_computation.2 | async-start | bytes 8912896 | tf_op jit(solution)/shard_map/all_gather | solution.py:141
  9.5 166.1 %reduce-scatter.2.cloned.1.call-start = ((), (), s32[]{:S(2)}) async-start(), calls=%async_computation.1 | async-start | bytes 9052160 | tf_op jit(solution)/shard_map/reduce_scatter | solution.py:153
Sparse Core Ops, SparseCore 0:
  9.8 78.6 all-gather.2
  99.3 76.2 reduce-scatter.1

commit v14 on v13

--- a/solution.py
+++ b/solution.py
@@ -13,9 +13,14 @@
     blocks, height, edge = out_ref.shape
     width = x_ref.shape[1] // 2
     count = cnt_ref[0]
+    half = blocks // 2
 
-    panel_copy = pltpu.make_async_copy(x_hbm, x_ref, x_sem)
-    panel_copy.start()
+    panel_copies = [
+        pltpu.make_async_copy(x_hbm.at[pl.ds(h * half, half)], x_ref.at[pl.ds(h * half, half)], x_sem.at[h])
+        for h in range(2)
+    ]
+    for c in panel_copies:
+        c.start()
 
     def tile_copy(s):
         return pltpu.make_async_copy(tile_hbm.at[s], tile_ref.at[s], tile_sem.at[s])
@@ -26,28 +31,32 @@
 
     lax.fori_loop(0, count, start_tile, 0)
     out_ref[:, width:, :] = extra_ref[...]
+    out_ref[:, :width, :] = jnp.zeros((blocks, width, edge), jnp.float32)
 
-    @pl.when(flag_ref[0] == 0)
-    def _elsewhere():
-        out_ref[:, :width, :] = jnp.zeros((blocks, width, edge), jnp.float32)
+    def slots_in(h):
+        def one_slot(s, carry):
+            j = ids_ref[2 * s + 1]
 
-    panel_copy.wait()
+            @pl.when((j >= h * half) & (j < (h + 1) * half))
+            def _add():
+                tile_copy(s).wait()
+                i = ids_ref[2 * s]
+                both = jnp.dot(x_ref[j], tile_ref[s], preferred_element_type=jnp.float32)
+                out_ref[i, :width, :] += both[:width] + both[width:]
+
+            return carry
+
+        lax.fori_loop(0, count, one_slot, 0)
+
+    for h in range(2):
+        panel_copies[h].wait()
+        slots_in(h)
 
     @pl.when(flag_ref[0] != 0)
     def _diagonal():
         for b in range(blocks):
             own = x_ref[b, :width, :].astype(jnp.float32) + x_ref[b, width:, :].astype(jnp.float32)
-            out_ref[b, :width, :] = own
-
-    def one_slot(s, carry):
-        tile_copy(s).wait()
-        i = ids_ref[2 * s]
-        j = ids_ref[2 * s + 1]
-        both = jnp.dot(x_ref[j], tile_ref[s], preferred_element_type=jnp.float32)
-        out_ref[i, :width, :] += both[:width] + both[width:]
-        return carry
-
-    lax.fori_loop(0, count, one_slot, 0)
+            out_ref[b, :width, :] += own
 
 
 def _panel_products(ids, cnt, flag, turned, panel, extra):
@@ -68,7 +77,7 @@
             pltpu.VMEM(turned.shape, turned.dtype),
             pltpu.VMEM(panel.shape, panel.dtype),
             pltpu.SemaphoreType.DMA((slots,)),
-            pltpu.SemaphoreType.DMA,
+            pltpu.SemaphoreType.DMA((2,)),
         ],
         compiler_params=pltpu.CompilerParams(vmem_limit_bytes=56 * 1024 * 1024),
         cost_estimate=pl.CostEstimate(

time: 185 us -> 186 us (level)
  waiting for transfers between devices: 143 us -> 145 us
where the time goes in v14:
time: 186 us
  waiting for transfers between devices  145 us (78%)
  Pallas kernels  15.1 us (8%)
  between operations  14.1 us (8%)
  local copies, waits for them, and re-layouts  8.52 us (5%)
  other arithmetic  2.87 us (2%)
    reduce_scatter x1, waiting for transfers between devices, shards(): lax.psum_scatter(partial.reshape(blocks * height, edge), 'col', scatter_d...  78.3 us
    all_gather x1, waiting for transfers between devices, shards(): panel = lax.all_gather(stacked, 'row', axis=0, tiled=True)  66.7 us
    pallas_call x1, Pallas kernels, _panel_products(): pl.pallas_call(_tile_kernel, in_specs=[smem, smem, smem, hbm, hbm, vmem],...  10.2 us
    unnamed x4, local copies, waits for them, and re-layouts  7.2 us
  transfers between devices with their start and end apart: 2, of which 2 were waited for; matrix products, arithmetic and copies ran while one was open for 6% of the time, Pallas kernels for 0%

profile of v14, /device:TPU:2, one launch (start us, length us, event | category | flops | bytes accessed | tf_op | source)
XLA Modules:
  0.0 185.9 jit_solution(5929271936880631784)
XLA Ops:
  6.5 0.0 copy-start
  6.5 0.0 all-gather.3.cloned.1.call-start
  6.5 2.9 %shard_map.55 = bf16[1024,256]{1,0:T(8,128)(2,1)} custom-call(f32[256,512]{1,0:T(8,128)} %x_ref.1, f32[512,512]{1,0:T(8,128)} %w_ref.1), custom_call_target="tpu_custom_call" | custom-call | flops 402653184 | bytes 2097152 | tf_op jit(solution)/shard_map/pallas_call | solution.py:111
  9.5 0.0 all-gather.3.cloned.1.call-update
  9.5 0.0 reduce-scatter.2.cloned.1.call-start
  10.2 0.8 copy.8
  11.0 0.6 reshape_squeeze.6.ids_ref
  11.6 6.4 %copy.9 = bf16[1,1,32,256,256]{3,4,2,1,0:T(8,128)(2,1)} copy(bf16[1,1,32,256,256]{4,3,2,1,0:T(8,128)(2,1)} %param.9) | data formatting | bytes 8388608 | tf_op args[2]
  18.0 0.0 copy-done
  18.0 2.9 %convert_reduce_fusion = f32[32,256]{1,0:T(8,128)S(1)} fusion(bf16[1,1,32,256,256]{3,4,2,1,0:T(8,128)(2,1)} %copy.9), kind=kLoop, calls=%fused_computation | loop fusion | flops 4186112 | bytes 4227072 | tf_op jit(solution)/shard_map/reduce_sum | solution.py:157
  20.9 0.3 fusion
  21.2 0.7 scatter.4.extra_ref
  21.9 66.7 %all-gather.3.cloned.1.call-done = bf16[16384,256]{1,0:T(8,128)(2,1)} async-done(((bf16[1024,256]{1,0:T(8,128)(2,1)}), bf16[16384,256]{1,0:T(8,128)(2,1)}) %all-gather.3.cloned.1.call-update) | async-done | bytes 8388624 | tf_op jit(solution)/shard_map/all_gather | solution.py:150
  88.5 10.2 %shard_map.56 = f32[16,520,256]{2,1,0:T(8,128)} custom-call(s32[64]{0:T(128)} %reshape_squeeze.6.ids_ref, s32[1]{0:T(128)} %bitcast.15.cnt_ref, s32[1]{0:T(128)} %bitcast.1.flag_ref, bf16[32,256,256]{2,1,0:T(8,128)(2,1)} %bitcast.17, bf16[16,1024,256]{2,1,0:T(8,128)(2,1)} %bitcast.19, f32[16,8,256]{2,1,0:T(8,128)} %scatter.4.extra_ref), custom_call_target="tpu_custom_call" | custom-call | flops 4294967296 | bytes 21102592 | tf_op jit(solution)/shard_map/pallas_call | solution.py:71
  98.7 0.0 reduce-scatter.2.cloned.1.call-update
  98.7 78.3 %reduce-scatter.2.cloned.1.call-done.mine_ref = f32[520,256]{1,0:T(8,128)} async-done(((f32[8320,256]{1,0:T(8,128)}), f32[520,256]{1,0:T(8,128)}) %reduce-scatter.2.cloned.1.call-update) | async-done | bytes 532496 | tf_op jit(solution)/shard_map/reduce_scatter | solution.py:162
  177.0 2.0 %shard_map.57 = f32[256,512]{1,0:T(8,128)} custom-call(f32[520,256]{1,0:T(8,128)} %reduce-scatter.2.cloned.1.call-done.mine_ref), custom_call_target="tpu_custom_call" | custom-call | tf_op jit(solution)/shard_map/pallas_call | solution.py:133
  (3 shorter events, 0.0 us)
Async XLA Ops:
  6.5 11.5 %copy-start = (s32[1,1,32,2]{2,3,1,0:T(2,128)S(1)}, s32[1,1,32,2]{2,3,1,0:T(2,128)}, u32[]{:S(2)}) copy-start(s32[1,1,32,2]{2,3,1,0:T(2,128)} %param.10) | copy-start | bytes 772
  6.5 82.0 %all-gather.3.cloned.1.call-start = ((), (), s32[]{:S(2)}) async-start(), calls=%async_computation.2 | async-start | bytes 8912896 | tf_op jit(solution)/shard_map/all_gather | solution.py:150
  9.5 167.5 %reduce-scatter.2.cloned.1.call-start = ((), (), s32[]{:S(2)}) async-start(), calls=%async_computation.1 | async-start | bytes 9052160 | tf_op jit(solution)/shard_map/reduce_scatter | solution.py:162
Sparse Core Ops, SparseCore 0:
  9.8 78.6 all-gather.2
  98.9 78.0 reduce-scatter.1

commit v15 on v12

--- a/solution.py
+++ b/solution.py
@@ -79,47 +79,56 @@
     )(ids, cnt, flag, turned, panel, extra)
 
 
-def _split_kernel(x_ref, w_ref, out_ref):
-    width = w_ref.shape[1]
-    product = jnp.dot(x_ref[...], w_ref[...], precision=lax.Precision.HIGHEST,
-                      preferred_element_type=jnp.float32)
-    turned = product.T
-    hi = turned.astype(jnp.bfloat16)
-    out_ref[:width, :] = hi
-    out_ref[width:, :] = (turned - hi.astype(jnp.float32)).astype(jnp.bfloat16)
+def _halves(v):
+    hi = v.astype(jnp.bfloat16)
+    return hi, (v - hi.astype(jnp.float32)).astype(jnp.bfloat16)
 
 
-def _split_product(features, weight):
-    rows, width = features.shape[0], weight.shape[1]
+def _split_kernel(x_ref, out_ref):
+    turned = x_ref[...].T
+    width = turned.shape[0]
+    hi, lo = _halves(turned)
+    out_ref[:width, :] = hi
+    out_ref[width:, :] = lo
+
+
+def _split_rows(features):
+    rows, width = features.shape
     vmem = pl.BlockSpec(memory_space=pltpu.VMEM)
     return pl.pallas_call(
         _split_kernel,
-        in_specs=[vmem, vmem],
+        in_specs=[vmem],
         out_specs=vmem,
         out_shape=jax.ShapeDtypeStruct((2 * width, rows), jnp.bfloat16),
-        cost_estimate=pl.CostEstimate(
-            flops=rows * weight.shape[0] * width * 2 * 6,
-            bytes_accessed=features.size * 4 + weight.size * 4 + 2 * width * rows * 2,
-            transcendentals=0,
-        ),
-    )(features, weight)
+    )(features)
 
 
-def _finish_kernel(mine_ref, out_ref):
-    width = out_ref.shape[1]
+def _finish_kernel(mine_ref, w_ref, out_ref):
+    width = w_ref.shape[0]
     scale = lax.rsqrt(1.0 + mine_ref[width:width + 1, :])
-    out_ref[...] = jnp.maximum(mine_ref[:width, :] * scale, 0.0).T
+    scaled = (mine_ref[:width, :] * scale).T
+    a_hi, a_lo = _halves(scaled)
+    w_hi, w_lo = _halves(w_ref[...])
+    product = jnp.dot(a_hi, w_hi, preferred_element_type=jnp.float32)
+    product += jnp.dot(a_hi, w_lo, preferred_element_type=jnp.float32)
+    product += jnp.dot(a_lo, w_hi, preferred_element_type=jnp.float32)
+    out_ref[...] = jnp.maximum(product, 0.0)
 
 
-def _finish(mine, width):
+def _finish(mine, weight):
     edge = mine.shape[1]
     vmem = pl.BlockSpec(memory_space=pltpu.VMEM)
     return pl.pallas_call(
         _finish_kernel,
-        in_specs=[vmem],
+        in_specs=[vmem, vmem],
         out_specs=vmem,
-        out_shape=jax.ShapeDtypeStruct((edge, width), jnp.float32),
-    )(mine)
+        out_shape=jax.ShapeDtypeStruct((edge, weight.shape[1]), jnp.float32),
+        cost_estimate=pl.CostEstimate(
+            flops=edge * weight.shape[0] * weight.shape[1] * 2 * 3,
+            bytes_accessed=mine.size * 4 + weight.size * 4 + edge * weight.shape[1] * 4,
+            transcendentals=edge,
+        ),
+    )(mine, weight)
 
 
 def shards(features, weight, tile_values, tile_ids, tile_counts):
@@ -130,7 +139,7 @@
     live_count = tile_counts[0, 0]
     cnt = live_count.reshape(1)
     flag = (lax.axis_index("row") == lax.axis_index("col")).astype(jnp.int32).reshape(1)
-    stacked = _split_product(features, weight)[None]
+    stacked = _split_rows(features)[None]
     panel = lax.all_gather(stacked, "row", axis=0, tiled=True)
     blocks, pair, _ = panel.shape
     width = pair // 2
@@ -146,7 +155,7 @@
     mine = lax.psum_scatter(
         partial.reshape(blocks * height, edge), "col", scatter_dimension=0, tiled=True
     )
-    return _finish(mine, width)
+    return _finish(mine, weight)
 
 
 def solution(mesh):

time: 185 us -> 184 us (level)
  Pallas kernels: 18.1 us -> 13.6 us
  waiting for transfers between devices: 142 us -> 146 us
    pallas_call x1, Pallas kernels: 12.7 us -> 8.76 us  [_panel_products(): pl.pallas_call(_tile_kernel, in_specs=[smem, smem, smem, hbm, hbm, vmem],...]
    reduce_scatter x1, waiting for transfers between devices: 75.4 us -> 78.2 us  [shards(): lax.psum_scatter(partial.reshape(blocks * height, edge), 'col', scatter_d...]
where the time goes in v15:
time: 184 us; the launch traced here: 185 us
  waiting for transfers between devices  146 us (79%)
  between operations  14.1 us (8%)
  Pallas kernels  13.6 us (7%)
  local copies, waits for them, and re-layouts  8.52 us (5%)
  other arithmetic  2.87 us (2%)
    reduce_scatter x1, waiting for transfers between devices, shards(): lax.psum_scatter(partial.reshape(blocks * height, edge), 'col', scatter_d...  78.2 us
    all_gather x1, waiting for transfers between devices, shards(): panel = lax.all_gather(stacked, 'row', axis=0, tiled=True)  67.5 us
    pallas_call x1, Pallas kernels, _panel_products(): pl.pallas_call(_tile_kernel, in_specs=[smem, smem, smem, hbm, hbm, vmem],...  8.76 us
    unnamed x4, local copies, waits for them, and re-layouts  7.2 us
  transfers between devices with their start and end apart: 2, of which 2 were waited for; matrix products, arithmetic and copies ran while one was open for 6% of the time, Pallas kernels for 0%

profile of v15, /device:TPU:2, one launch (start us, length us, event | category | flops | bytes accessed | tf_op | source)
XLA Modules:
  0.0 185.2 jit_solution(10162893584519024357)
XLA Ops:
  6.5 0.0 copy-start
  6.5 0.0 all-gather.3.cloned.1.call-start
  6.5 2.0 %shard_map.55 = bf16[1024,256]{1,0:T(8,128)(2,1)} custom-call(f32[256,512]{1,0:T(8,128)} %x_ref.1), custom_call_target="tpu_custom_call" | custom-call | tf_op jit(solution)/shard_map/pallas_call | solution.py:98
  8.6 0.0 all-gather.3.cloned.1.call-update
  8.6 0.0 reduce-scatter.2.cloned.1.call-start
  9.3 0.8 copy.8
  10.1 0.6 reshape_squeeze.6.ids_ref
  10.7 6.4 %copy.9 = bf16[1,1,32,256,256]{3,4,2,1,0:T(8,128)(2,1)} copy(bf16[1,1,32,256,256]{4,3,2,1,0:T(8,128)(2,1)} %param.9) | data formatting | bytes 8388608 | tf_op args[2]
  17.2 0.0 copy-done
  17.2 2.9 %convert_reduce_fusion = f32[32,256]{1,0:T(8,128)S(1)} fusion(bf16[1,1,32,256,256]{3,4,2,1,0:T(8,128)(2,1)} %copy.9), kind=kLoop, calls=%fused_computation | loop fusion | flops 4186112 | bytes 4227072 | tf_op jit(solution)/shard_map/reduce_sum | solution.py:150
  20.0 0.3 fusion
  20.3 0.7 scatter.4.extra_ref
  21.0 67.5 %all-gather.3.cloned.1.call-done = bf16[16384,256]{1,0:T(8,128)(2,1)} async-done(((bf16[1024,256]{1,0:T(8,128)(2,1)}), bf16[16384,256]{1,0:T(8,128)(2,1)}) %all-gather.3.cloned.1.call-update) | async-done | bytes 8388624 | tf_op jit(solution)/shard_map/all_gather | solution.py:143
  88.5 8.8 %shard_map.56 = f32[16,520,256]{2,1,0:T(8,128)} custom-call(s32[64]{0:T(128)} %reshape_squeeze.6.ids_ref, s32[1]{0:T(128)} %bitcast.15.cnt_ref, s32[1]{0:T(128)} %bitcast.1.flag_ref, bf16[32,256,256]{2,1,0:T(8,128)(2,1)} %bitcast.17, bf16[16,1024,256]{2,1,0:T(8,128)(2,1)} %bitcast.19, f32[16,8,256]{2,1,0:T(8,128)} %scatter.4.extra_ref), custom_call_target="tpu_custom_call" | custom-call | flops 4294967296 | bytes 21102592 | tf_op jit(solution)/shard_map/pallas_call | solution.py:62
  97.3 0.0 reduce-scatter.2.cloned.1.call-update
  97.3 78.2 %reduce-scatter.2.cloned.1.call-done.mine_ref = f32[520,256]{1,0:T(8,128)} async-done(((f32[8320,256]{1,0:T(8,128)}), f32[520,256]{1,0:T(8,128)}) %reduce-scatter.2.cloned.1.call-update) | async-done | bytes 532496 | tf_op jit(solution)/shard_map/reduce_scatter | solution.py:155
  175.5 2.8 %shard_map.57 = f32[256,512]{1,0:T(8,128)} custom-call(f32[520,256]{1,0:T(8,128)} %reduce-scatter.2.cloned.1.call-done.mine_ref, f32[512,512]{1,0:T(8,128)} %w_ref.1), custom_call_target="tpu_custom_call" | custom-call | flops 402653184 | bytes 2105344 | tf_op jit(solution)/shard_map/pallas_call | solution.py:121
  (3 shorter events, 0.0 us)
Async XLA Ops:
  6.5 10.6 %copy-start = (s32[1,1,32,2]{2,3,1,0:T(2,128)S(1)}, s32[1,1,32,2]{2,3,1,0:T(2,128)}, u32[]{:S(2)}) copy-start(s32[1,1,32,2]{2,3,1,0:T(2,128)} %param.10) | copy-start | bytes 772
  6.5 82.0 %all-gather.3.cloned.1.call-start = ((), (), s32[]{:S(2)}) async-start(), calls=%async_computation.2 | async-start | bytes 8912896 | tf_op jit(solution)/shard_map/all_gather | solution.py:143
  8.6 166.9 %reduce-scatter.2.cloned.1.call-start = ((), (), s32[]{:S(2)}) async-start(), calls=%async_computation.1 | async-start | bytes 9052160 | tf_op jit(solution)/shard_map/reduce_scatter | solution.py:155
Sparse Core Ops, SparseCore 0:
  9.8 78.6 all-gather.2
  97.4 78.0 reduce-scatter.1

commit v16 on v13

--- a/solution.py
+++ b/solution.py
@@ -8,14 +8,22 @@
 EXTRA = 8
 
 
-def _tile_kernel(ids_ref, cnt_ref, flag_ref, tile_hbm, x_hbm, extra_ref, out_ref,
-                 tile_ref, x_ref, tile_sem, x_sem):
+def _tile_kernel(ids_ref, cnt_ref, flag_ref, tile_hbm, x_hbm, extra_ref, out_hbm,
+                 tile_ref, x_ref, out_ref, tile_sem, x_sem, out_sem):
     blocks, height, edge = out_ref.shape
     width = x_ref.shape[1] // 2
     count = cnt_ref[0]
+    parts = x_sem.shape[0]
+    share = blocks // parts
 
-    panel_copy = pltpu.make_async_copy(x_hbm, x_ref, x_sem)
-    panel_copy.start()
+    def chunk(ref, p):
+        return ref.at[pl.ds(p * share, share)]
+
+    panel_copies = [
+        pltpu.make_async_copy(chunk(x_hbm, p), chunk(x_ref, p), x_sem.at[p]) for p in range(parts)
+    ]
+    for c in panel_copies:
+        c.start()
 
     def tile_copy(s):
         return pltpu.make_async_copy(tile_hbm.at[s], tile_ref.at[s], tile_sem.at[s])
@@ -31,7 +39,8 @@
     def _elsewhere():
         out_ref[:, :width, :] = jnp.zeros((blocks, width, edge), jnp.float32)
 
-    panel_copy.wait()
+    for c in panel_copies:
+        c.wait()
 
     @pl.when(flag_ref[0] != 0)
     def _diagonal():
@@ -48,6 +57,13 @@
         return carry
 
     lax.fori_loop(0, count, one_slot, 0)
+    out_copies = [
+        pltpu.make_async_copy(chunk(out_ref, p), chunk(out_hbm, p), out_sem.at[p]) for p in range(parts)
+    ]
+    for c in out_copies:
+        c.start()
+    for c in out_copies:
+        c.wait()
 
 
 def _panel_products(ids, cnt, flag, turned, panel, extra):
@@ -62,13 +78,15 @@
     return pl.pallas_call(
         _tile_kernel,
         in_specs=[smem, smem, smem, hbm, hbm, vmem],
-        out_specs=vmem,
+        out_specs=hbm,
         out_shape=jax.ShapeDtypeStruct((blocks, height, edge), jnp.float32),
         scratch_shapes=[
             pltpu.VMEM(turned.shape, turned.dtype),
             pltpu.VMEM(panel.shape, panel.dtype),
+            pltpu.VMEM((blocks, height, edge), jnp.float32),
             pltpu.SemaphoreType.DMA((slots,)),
-            pltpu.SemaphoreType.DMA,
+            pltpu.SemaphoreType.DMA((4,)),
+            pltpu.SemaphoreType.DMA((4,)),
         ],
         compiler_params=pltpu.CompilerParams(vmem_limit_bytes=56 * 1024 * 1024),
         cost_estimate=pl.CostEstimate(

time: 185 us -> 184 us (level)
  waiting for transfers between devices: 143 us -> 140 us
  Pallas kernels: 15.6 us -> 18.1 us
    reduce_scatter x1, waiting for transfers between devices: 76.5 us -> 73.3 us  [shards(): lax.psum_scatter(partial.reshape(blocks * height, edge), 'col', scatter_d...]
    pallas_call x1, Pallas kernels: 10.6 us -> 13.2 us  [_panel_products(): pl.pallas_call(_tile_kernel, in_specs=[smem, smem, smem, hbm, hbm, vmem],...]
where the time goes in v16:
time: 184 us
  waiting for transfers between devices  140 us (76%)
  Pallas kernels  18.1 us (10%)
  between operations  14.1 us (8%)
  local copies, waits for them, and re-layouts  8.52 us (5%)
  other arithmetic  2.87 us (2%)
    reduce_scatter x1, waiting for transfers between devices, shards(): lax.psum_scatter(partial.reshape(blocks * height, edge), 'col', scatter_d...  73.3 us
    all_gather x1, waiting for transfers between devices, shards(): panel = lax.all_gather(stacked, 'row', axis=0, tiled=True)  66.7 us
    pallas_call x1, Pallas kernels, _panel_products(): pl.pallas_call(_tile_kernel, in_specs=[smem, smem, smem, hbm, hbm, vmem],...  13.2 us
    unnamed x4, local copies, waits for them, and re-layouts  7.2 us
  transfers between devices with their start and end apart: 2, of which 2 were waited for; matrix products, arithmetic and copies ran while one was open for 6% of the time, Pallas kernels for 0%

profile of v16, /device:TPU:2, one launch (start us, length us, event | category | flops | bytes accessed | tf_op | source)
XLA Modules:
  0.0 183.9 jit_solution(9207451452353380435)
XLA Ops:
  6.5 0.0 copy-start
  6.5 0.0 all-gather.3.cloned.1.call-start
  6.5 2.9 %shard_map.55 = bf16[1024,256]{1,0:T(8,128)(2,1)} custom-call(f32[256,512]{1,0:T(8,128)} %x_ref.1, f32[512,512]{1,0:T(8,128)} %w_ref.1), custom_call_target="tpu_custom_call" | custom-call | flops 402653184 | bytes 2097152 | tf_op jit(solution)/shard_map/pallas_call | solution.py:120
  9.5 0.0 all-gather.3.cloned.1.call-update
  9.5 0.0 reduce-scatter.2.cloned.1.call-start
  10.2 0.8 copy.8
  11.0 0.6 reshape_squeeze.6.ids_ref
  11.6 6.4 %copy.9 = bf16[1,1,32,256,256]{3,4,2,1,0:T(8,128)(2,1)} copy(bf16[1,1,32,256,256]{4,3,2,1,0:T(8,128)(2,1)} %param.9) | data formatting | bytes 8388608 | tf_op args[2]
  18.0 0.0 copy-done
  18.0 2.9 %convert_reduce_fusion = f32[32,256]{1,0:T(8,128)S(1)} fusion(bf16[1,1,32,256,256]{3,4,2,1,0:T(8,128)(2,1)} %copy.9), kind=kLoop, calls=%fused_computation | loop fusion | flops 4186112 | bytes 4227072 | tf_op jit(solution)/shard_map/reduce_sum | solution.py:166
  20.9 0.3 fusion
  21.2 0.7 scatter.4.extra_ref
  21.9 66.7 %all-gather.3.cloned.1.call-done = bf16[16384,256]{1,0:T(8,128)(2,1)} async-done(((bf16[1024,256]{1,0:T(8,128)(2,1)}), bf16[16384,256]{1,0:T(8,128)(2,1)}) %all-gather.3.cloned.1.call-update) | async-done | bytes 8388624 | tf_op jit(solution)/shard_map/all_gather | solution.py:159
  88.5 13.2 %shard_map.56 = f32[16,520,256]{2,1,0:T(8,128)} custom-call(s32[64]{0:T(128)} %reshape_squeeze.6.ids_ref, s32[1]{0:T(128)} %bitcast.15.cnt_ref, s32[1]{0:T(128)} %bitcast.1.flag_ref, bf16[32,256,256]{2,1,0:T(8,128)(2,1)} %bitcast.17, bf16[16,1024,256]{2,1,0:T(8,128)(2,1)} %bitcast.19, f32[16,8,256]{2,1,0:T(8,128)} %scatter.4.extra_ref), custom_call_target="tpu_custom_call" | custom-call | flops 4294967296 | bytes 21102592 | tf_op jit(solution)/shard_map/pallas_call | solution.py:78
  101.7 0.0 reduce-scatter.2.cloned.1.call-update
  101.7 73.3 %reduce-scatter.2.cloned.1.call-done.mine_ref = f32[520,256]{1,0:T(8,128)} async-done(((f32[8320,256]{1,0:T(8,128)}), f32[520,256]{1,0:T(8,128)}) %reduce-scatter.2.cloned.1.call-update) | async-done | bytes 532496 | tf_op jit(solution)/shard_map/reduce_scatter | solution.py:171
  175.1 2.0 %shard_map.57 = f32[256,512]{1,0:T(8,128)} custom-call(f32[520,256]{1,0:T(8,128)} %reduce-scatter.2.cloned.1.call-done.mine_ref), custom_call_target="tpu_custom_call" | custom-call | tf_op jit(solution)/shard_map/pallas_call | solution.py:142
  (3 shorter events, 0.0 us)
Async XLA Ops:
  6.5 11.5 %copy-start = (s32[1,1,32,2]{2,3,1,0:T(2,128)S(1)}, s32[1,1,32,2]{2,3,1,0:T(2,128)}, u32[]{:S(2)}) copy-start(s32[1,1,32,2]{2,3,1,0:T(2,128)} %param.10) | copy-start | bytes 772
  6.5 82.0 %all-gather.3.cloned.1.call-start = ((), (), s32[]{:S(2)}) async-start(), calls=%async_computation.2 | async-start | bytes 8912896 | tf_op jit(solution)/shard_map/all_gather | solution.py:159
  9.5 165.6 %reduce-scatter.2.cloned.1.call-start = ((), (), s32[]{:S(2)}) async-start(), calls=%async_computation.1 | async-start | bytes 9052160 | tf_op jit(solution)/shard_map/reduce_scatter | solution.py:171
Sparse Core Ops, SparseCore 0:
  9.8 78.6 all-gather.2
  101.8 73.1 reduce-scatter.1

commit v17 on v16

--- a/solution.py
+++ b/solution.py
@@ -9,7 +9,7 @@
 
 
 def _tile_kernel(ids_ref, cnt_ref, flag_ref, tile_hbm, x_hbm, extra_ref, out_hbm,
-                 tile_ref, x_ref, out_ref, tile_sem, x_sem, out_sem):
+                 tile_ref, x_ref, out_ref, tile_sem, x_sem, out_sem, waited):
     blocks, height, edge = out_ref.shape
     width = x_ref.shape[1] // 2
     count = cnt_ref[0]
@@ -39,11 +39,19 @@
     def _elsewhere():
         out_ref[:, :width, :] = jnp.zeros((blocks, width, edge), jnp.float32)
 
-    for c in panel_copies:
-        c.wait()
+    for p in range(parts):
+        waited[p] = 0
+
+    def ensure(p):
+        @pl.when(waited[p] == 0)
+        def _wait():
+            pltpu.make_async_copy(chunk(x_hbm, p), chunk(x_ref, p), x_sem.at[p]).wait()
+            waited[p] = 1
 
     @pl.when(flag_ref[0] != 0)
     def _diagonal():
+        for p in range(parts):
+            ensure(p)
         for b in range(blocks):
             own = x_ref[b, :width, :].astype(jnp.float32) + x_ref[b, width:, :].astype(jnp.float32)
             out_ref[b, :width, :] = own
@@ -52,11 +60,14 @@
         tile_copy(s).wait()
         i = ids_ref[2 * s]
         j = ids_ref[2 * s + 1]
+        ensure(j // share)
         both = jnp.dot(x_ref[j], tile_ref[s], preferred_element_type=jnp.float32)
         out_ref[i, :width, :] += both[:width] + both[width:]
         return carry
 
     lax.fori_loop(0, count, one_slot, 0)
+    for p in range(parts):
+        ensure(p)
     out_copies = [
         pltpu.make_async_copy(chunk(out_ref, p), chunk(out_hbm, p), out_sem.at[p]) for p in range(parts)
     ]
@@ -87,6 +98,7 @@
             pltpu.SemaphoreType.DMA((slots,)),
             pltpu.SemaphoreType.DMA((4,)),
             pltpu.SemaphoreType.DMA((4,)),
+            pltpu.SMEM((4,), jnp.int32),
         ],
         compiler_params=pltpu.CompilerParams(vmem_limit_bytes=56 * 1024 * 1024),
         cost_estimate=pl.CostEstimate(

time: 184 us -> 184 us (level)
  waiting for transfers between devices: 140 us -> 144 us
  Pallas kernels: 18.1 us -> 14.4 us
    reduce_scatter x1, waiting for transfers between devices: 73.3 us -> 77.6 us  [shards(): lax.psum_scatter(partial.reshape(blocks * height, edge), 'col', scatter_d...]
    pallas_call x1, Pallas kernels: 13.2 us -> 9.44 us  [_panel_products(): pl.pallas_call(_tile_kernel, in_specs=[smem, smem, smem, hbm, hbm, vmem],...]
where the time goes in v17:
time: 184 us; the launch traced here: 185 us
  waiting for transfers between devices  144 us (78%)
  Pallas kernels  14.4 us (8%)
  between operations  14.1 us (8%)
  local copies, waits for them, and re-layouts  8.52 us (5%)
  other arithmetic  2.87 us (2%)
    reduce_scatter x1, waiting for transfers between devices, shards(): lax.psum_scatter(partial.reshape(blocks * height, edge), 'col', scatter_d...  77.6 us
    all_gather x1, waiting for transfers between devices, shards(): panel = lax.all_gather(stacked, 'row', axis=0, tiled=True)  66.7 us
    pallas_call x1, Pallas kernels, _panel_products(): pl.pallas_call(_tile_kernel, in_specs=[smem, smem, smem, hbm, hbm, vmem],...  9.44 us
    unnamed x4, local copies, waits for them, and re-layouts  7.2 us
  transfers between devices with their start and end apart: 2, of which 2 were waited for; matrix products, arithmetic and copies ran while one was open for 6% of the time, Pallas kernels for 0%

profile of v17, /device:TPU:2, one launch (start us, length us, event | category | flops | bytes accessed | tf_op | source)
XLA Modules:
  0.0 184.5 jit_solution(5606995044290631367)
XLA Ops:
  6.5 0.0 copy-start
  6.5 0.0 all-gather.3.cloned.1.call-start
  6.5 2.9 %shard_map.55 = bf16[1024,256]{1,0:T(8,128)(2,1)} custom-call(f32[256,512]{1,0:T(8,128)} %x_ref.1, f32[512,512]{1,0:T(8,128)} %w_ref.1), custom_call_target="tpu_custom_call" | custom-call | flops 402653184 | bytes 2097152 | tf_op jit(solution)/shard_map/pallas_call | solution.py:132
  9.5 0.0 all-gather.3.cloned.1.call-update
  9.5 0.0 reduce-scatter.2.cloned.1.call-start
  10.2 0.8 copy.8
  11.0 0.6 reshape_squeeze.6.ids_ref
  11.6 6.4 %copy.9 = bf16[1,1,32,256,256]{3,4,2,1,0:T(8,128)(2,1)} copy(bf16[1,1,32,256,256]{4,3,2,1,0:T(8,128)(2,1)} %param.9) | data formatting | bytes 8388608 | tf_op args[2]
  18.0 0.0 copy-done
  18.0 2.9 %convert_reduce_fusion = f32[32,256]{1,0:T(8,128)S(1)} fusion(bf16[1,1,32,256,256]{3,4,2,1,0:T(8,128)(2,1)} %copy.9), kind=kLoop, calls=%fused_computation | loop fusion | flops 4186112 | bytes 4227072 | tf_op jit(solution)/shard_map/reduce_sum | solution.py:178
  20.9 0.3 fusion
  21.2 0.7 scatter.4.extra_ref
  21.9 66.7 %all-gather.3.cloned.1.call-done = bf16[16384,256]{1,0:T(8,128)(2,1)} async-done(((bf16[1024,256]{1,0:T(8,128)(2,1)}), bf16[16384,256]{1,0:T(8,128)(2,1)}) %all-gather.3.cloned.1.call-update) | async-done | bytes 8388624 | tf_op jit(solution)/shard_map/all_gather | solution.py:171
  88.5 9.4 %shard_map.56 = f32[16,520,256]{2,1,0:T(8,128)} custom-call(s32[64]{0:T(128)} %reshape_squeeze.6.ids_ref, s32[1]{0:T(128)} %bitcast.15.cnt_ref, s32[1]{0:T(128)} %bitcast.1.flag_ref, bf16[32,256,256]{2,1,0:T(8,128)(2,1)} %bitcast.17, bf16[16,1024,256]{2,1,0:T(8,128)(2,1)} %bitcast.19, f32[16,8,256]{2,1,0:T(8,128)} %scatter.4.extra_ref), custom_call_target="tpu_custom_call" | custom-call | flops 4294967296 | bytes 21102592 | tf_op jit(solution)/shard_map/pallas_call | solution.py:89
  98.0 0.0 reduce-scatter.2.cloned.1.call-update
  98.0 77.6 %reduce-scatter.2.cloned.1.call-done.mine_ref = f32[520,256]{1,0:T(8,128)} async-done(((f32[8320,256]{1,0:T(8,128)}), f32[520,256]{1,0:T(8,128)}) %reduce-scatter.2.cloned.1.call-update) | async-done | bytes 532496 | tf_op jit(solution)/shard_map/reduce_scatter | solution.py:183
  175.7 2.0 %shard_map.57 = f32[256,512]{1,0:T(8,128)} custom-call(f32[520,256]{1,0:T(8,128)} %reduce-scatter.2.cloned.1.call-done.mine_ref), custom_call_target="tpu_custom_call" | custom-call | tf_op jit(solution)/shard_map/pallas_call | solution.py:154
  (3 shorter events, 0.0 us)
Async XLA Ops:
  6.5 11.5 %copy-start = (s32[1,1,32,2]{2,3,1,0:T(2,128)S(1)}, s32[1,1,32,2]{2,3,1,0:T(2,128)}, u32[]{:S(2)}) copy-start(s32[1,1,32,2]{2,3,1,0:T(2,128)} %param.10) | copy-start | bytes 772
  6.5 82.0 %all-gather.3.cloned.1.call-start = ((), (), s32[]{:S(2)}) async-start(), calls=%async_computation.2 | async-start | bytes 8912896 | tf_op jit(solution)/shard_map/all_gather | solution.py:171
  9.5 166.2 %reduce-scatter.2.cloned.1.call-start = ((), (), s32[]{:S(2)}) async-start(), calls=%async_computation.1 | async-start | bytes 9052160 | tf_op jit(solution)/shard_map/reduce_scatter | solution.py:183
Sparse Core Ops, SparseCore 0:
  9.8 78.6 all-gather.2
  98.1 77.4 reduce-scatter.1
